TPU v7x, 256 devices: a whole 4x4x8 slice. The times are simulated.
256 devices in a mesh: seq: 8 (over x_hi, y), exp: 32 (over x_lo, z, core).
Axes of the slice: x: 4 (x_hi: 2, x_lo: 2; x = x_hi * 2 + x_lo), y: 4, z: 8, core: 2. Of those that a mesh axis runs over, the one named last changes fastest.
Arguments:
- tokens: bfloat16 [8192, 2560], P('exp'), may hold values from -6 to 6
- norm_gain: float32 [2560], replicated, may hold values from 0.1 to 1.9
- routes: int32 [8192, 6], P('exp'), may hold values from 0 to 63, all different within a row; in each aligned block of 256 rows (0 to 255, 256 to 511, ...) at most 25 rows name the same one
- route_weights: bfloat16 [8192, 6], P('exp'), may hold values from 0.049804688 to 0.3984375
- w_gate: bfloat16 [64, 2560, 1536], P('exp', None, 'seq'), may hold values from -0.125 to 0.125
- w_up: bfloat16 [64, 2560, 1536], P('exp', None, 'seq'), may hold values from -0.125 to 0.125
- w_down: bfloat16 [64, 1536, 2560], P('exp', 'seq'), may hold values from -0.15625 to 0.15625
- kv_prefill: bfloat16 [4, 2048, 32, 1024], P(None, ('seq', 'exp')), may hold values from -6 to 6
- block_map: int32 [2048], P(('seq', 'exp')), may hold values from 0 to 2047, as said below
- block_empty: int32 [2048], P(('seq', 'exp')), may hold values 0 or 1
Outputs:
- moe_out: bfloat16 [8192, 2560], P('exp', 'seq')
- kv_decode: bfloat16 [4, 2048, 32, 1024], P(None, ('seq', 'exp'))
Inputs may be any that keep to these rules, and one draw needn't show every extreme that they name: `routes`: in each aligned block of 256 rows no expert is named by more than 25 rows, a bound that some block reaches. block_map is a permutation of the 2048 blocks; a block keeps its index of exp, and each device sends exactly 1 block to each device of its seq group, itself included.
All inputs are finite; a program needn't handle non-finite values. No bound on the sum of `block_empty` on one device may be relied on, other than what follows from the above.
Results may differ from a plain program's by a relative error of at most 0.013.
Values may be sent and summed in bfloat16 or wider, within the bound.
No kernel may reach another device: no remote copies, remote signals or barrier semaphores. Data moves between devices by JAX's collectives and lax.ppermute only.
A program may use at most 128 MiB of HBM per device.

v0:
```python
import jax
import jax.numpy as jnp
from jax import lax
from jax.sharding import PartitionSpec as P


def passed_along(block, axis, distance):
    devices = range(lax.axis_size(axis))
    route = [((i - distance) % len(devices), i) for i in devices]
    return lax.ppermute(block, axis, route)


def rms_normed(tokens, norm_gain):
    values = tokens.astype(jnp.float32)
    scale = lax.rsqrt(jnp.mean(values * values, axis=-1, keepdims=True) + 1e-06)
    return (values * scale * norm_gain).astype(jnp.bfloat16)


def slot_layout(routes, experts, local_experts, owners, capacity):
    flat_routes = routes.reshape(-1)
    onehot = (flat_routes[:, None] == jnp.arange(experts, dtype=jnp.int32)[None, :]).astype(
        jnp.int32
    )
    before = jnp.cumsum(onehot, axis=0) - onehot
    position = jnp.sum(before * onehot, axis=1)
    owner = flat_routes // local_experts
    local_index = flat_routes % local_experts
    return (local_index * owners + owner) * capacity + position


def fill_slots(normed, slot_index, total_slots, topk):
    row_count = normed.shape[0]
    token_of = jnp.arange(slot_index.shape[0], dtype=jnp.int32) // topk
    source = jnp.full((total_slots,), row_count, jnp.int32).at[slot_index].set(token_of)
    padded = jnp.concatenate([normed, jnp.zeros((1, normed.shape[1]), normed.dtype)], axis=0)
    return padded[source]


def expert_block(rows, w_gate, w_up, w_down):
    gate = jnp.einsum("erd,edf->erf", rows, w_gate, preferred_element_type=jnp.float32)
    upward = jnp.einsum("erd,edf->erf", rows, w_up, preferred_element_type=jnp.float32)
    hidden = (jax.nn.silu(gate) * upward).astype(jnp.bfloat16)
    return jnp.einsum("erf,efd->erd", hidden, w_down, preferred_element_type=jnp.float32).astype(
        jnp.bfloat16
    )


def relayout(kv_prefill, block_map, block_empty):
    layers, blocks, block_rows, kv_width = kv_prefill.shape
    seq_count = lax.axis_size("seq")
    exp_count = lax.axis_size("exp")
    per_peer = blocks // seq_count
    keep = (1 - block_empty).astype(jnp.bfloat16)
    kept = kv_prefill * keep[None, :, None, None]
    peer = block_map // blocks // exp_count
    target = block_map % blocks
    order = jnp.argsort(peer * blocks + jnp.arange(blocks, dtype=jnp.int32))
    outgoing = kept[:, order].reshape(layers, seq_count, per_peer, block_rows, kv_width)
    labels = target[order].astype(jnp.bfloat16).reshape(1, seq_count, per_peer)
    my_seq = lax.axis_index("seq")
    arrived = outgoing
    tags = labels
    for step in range(1, seq_count):
        ahead = (my_seq + step) % seq_count
        piece = lax.dynamic_slice_in_dim(outgoing, ahead, 1, 1)
        label = lax.dynamic_slice_in_dim(labels, ahead, 1, 1)
        piece, label = passed_along((piece, label), "seq", step)
        behind = (my_seq - step + seq_count) % seq_count
        arrived = lax.dynamic_update_slice_in_dim(arrived, piece, behind, 1)
        tags = lax.dynamic_update_slice_in_dim(tags, label, behind, 1)
    arrived = arrived.reshape(layers, blocks, block_rows, kv_width)
    slots = tags.reshape(blocks).astype(jnp.int32)
    return arrived[:, jnp.argsort(slots)]


def per_device(
    tokens,
    norm_gain,
    routes,
    route_weights,
    w_gate,
    w_up,
    w_down,
    kv_prefill,
    block_map,
    block_empty,
):
    local_experts = w_gate.shape[0]
    exp_count = lax.axis_size("exp")
    experts = local_experts * exp_count
    tok_count, topk = routes.shape
    capacity = tok_count * topk // experts + 1
    normed = rms_normed(tokens, norm_gain)
    width = normed.shape[1]
    slot_index = slot_layout(routes, experts, local_experts, exp_count, capacity)
    total_slots = local_experts * exp_count * capacity
    outgoing = fill_slots(normed, slot_index, total_slots, topk).reshape(
        local_experts, exp_count * capacity, width
    )
    arrived = lax.all_to_all(outgoing, "exp", split_axis=1, concat_axis=1, tiled=True)
    partial_value = expert_block(arrived, w_gate, w_up, w_down)
    weights = route_weights.astype(jnp.float32)[:, :, None]
    returned = lax.all_to_all(
        partial_value, "exp", split_axis=1, concat_axis=1, tiled=True
    ).reshape(total_slots, width)
    picked = returned[slot_index].astype(jnp.float32).reshape(tok_count, topk, width)
    terms = jnp.sum(picked * weights, axis=1)
    mixed = lax.psum_scatter(terms.astype(jnp.bfloat16), "seq", scatter_dimension=1, tiled=True)
    kv_decode = relayout(kv_prefill, block_map, block_empty)
    return (mixed, kv_decode)


def solution(mesh):
    in_specs = (
        P("exp", None),
        P(),
        P("exp", None),
        P("exp", None),
        P("exp", None, "seq"),
        P("exp", None, "seq"),
        P("exp", "seq", None),
        P(None, ("seq", "exp"), None, None),
        P(("seq", "exp")),
        P(("seq", "exp")),
    )
    out_specs = (P("exp", "seq"), P(None, ("seq", "exp"), None, None))
    return jax.shard_map(
        per_device, mesh=mesh, in_specs=in_specs, out_specs=out_specs, check_vma=False
    )
```

profile of v0, /device:TPU:120, one launch (start us, length us, event | category | flops | bytes accessed | tf_op | source)
XLA Modules:
  0.0 717.7 jit_solution(14914148657757064392)
XLA Ops:
  7.2 1.0 copy.42
  8.6 1.7 fusion.4
  10.3 0.8 fusion.16
  11.1 34.6 %reduce-window.6 = s32[64,12,128]{2,1,0:T(8,128)} reduce-window(s32[64,12,128]{2,1,0:T(8,128)} %fusion.16, s32[]{:T(128)} %constant.187.clone.1), window={size=1x1x128 pad=0_0x0_0x127_0}, to_apply=%region_1.0 | reduce-window | flops 12484608 | bytes 786436 | tf_op jit(solution)/shard_map/reduce-window
  45.7 2.0 slice.18
  47.8 1.3 copy.45
  49.2 1.2 broadcast_add_fusion
  50.7 6.2 scatter_custom_fusion
  57.4 8.3 %gather_fusion = bf16[1600,2560]{1,0:T(8,128)(2,1)} fusion(bf16[257,2560]{1,0:T(8,128)(2,1)S(1)} %concatenate.3, s32[2048]{0:T(1024)S(1)} %pad_clamp_fusion.1), kind=kCustom, calls=%fused_computation | custom fusion | bytes 16390400 | tf_op jit(solution)/shard_map/gather | solution.py:36
  65.7 37.7 %copy.47 = bf16[2,800,2560]{2,0,1:T(2,128)(2,1)S(1)} copy(bf16[2,800,2560]{2,1,0:T(8,128)(2,1)} %bitcast.71) | data formatting | bytes 16384000 | tf_op jit(solution)/shard_map/reshape | solution.py:97
  103.3 188.8 %all_to_all.10 = bf16[2,800,2560]{2,0,1:T(2,128)(2,1)S(1)} all-to-all(bf16[2,800,2560]{2,0,1:T(2,128)(2,1)S(1)} %copy.47), channel_id=1, replica_groups=mesh['seq'=8,'exp'=32] {'exp'}, dimensions={1} | all-to-all | bytes 16384000 | tf_op jit(solution)/shard_map/all_to_all | solution.py:100
  292.1 3.2 copy-done.2
  295.3 4.2 fusion.2
  299.5 14.7 %convolution_convert_fusion = bf16[2,800,2560]{2,1,0:T(8,128)(2,1)} fusion(bf16[2,192,2560]{2,1,0:T(8,128)(2,1)S(1)} %copy-done, bf16[2,2560,192]{1,2,0:T(8,128)(2,1)} %param.15, bf16[2,800,2560]{2,0,1:T(2,128)(2,1)} %copy-done.2, f32[2,800,192]{1,2,0:T(8,128)} %fusion.2), kind=kOutput, calls=%fused_computation.11 | convolution fusion | flops 3151667200 | bytes 21544960 | tf_op jit(solution)/shard_map/erf,efd->erd/dot_general | solution.py:43
  314.2 38.5 %copy.50 = bf16[2,800,2560]{2,0,1:T(2,128)(2,1)} copy(bf16[2,800,2560]{2,1,0:T(8,128)(2,1)} %convolution_convert_fusion) | data formatting | bytes 16384000 | tf_op jit(solution)/shard_map/convert_element_type | solution.py:43
  352.7 7.3 %all-to-all-start.1 = ((bf16[2,800,2560]{2,0,1:T(2,128)(2,1)}), bf16[2,800,2560]{2,0,1:T(2,128)(2,1)}, u32[]{:S(2)}, u32[]{:S(2)}) async-start(bf16[2,800,2560]{2,0,1:T(2,128)(2,1)} %copy.50), calls=%async_computation.1 | async-start | bytes 16384000 | tf_op jit(solution)/shard_map/all_to_all | solution.py:103
  360.4 1.0 sort.31
  361.4 182.3 %all-to-all-done.1 = bf16[2,800,2560]{2,0,1:T(2,128)(2,1)} async-done(((bf16[2,800,2560]{2,0,1:T(2,128)(2,1)}), bf16[2,800,2560]{2,0,1:T(2,128)(2,1)}, u32[]{:S(2)}, u32[]{:S(2)}) %all-to-all-start.1) | async-done | bytes 8192032 | tf_op jit(solution)/shard_map/all_to_all | solution.py:103
  543.7 7.8 %copy.51 = bf16[2,800,2560]{2,1,0:T(8,128)(2,1)} copy(bf16[2,800,2560]{2,0,1:T(2,128)(2,1)} %all-to-all-done.1) | data formatting | bytes 16384000 | tf_op jit(solution)/shard_map/all_to_all | solution.py:103
  551.5 19.5 %gather_fusion.1 = bf16[1536,2560]{1,0:T(8,128)(2,1)} fusion(bf16[1600,2560]{1,0:T(8,128)(2,1)} %bitcast.70, s32[2048]{0:T(1024)S(1)} %pad_clamp_fusion), kind=kCustom, calls=%fused_computation.1 | custom fusion | bytes 15734784 | tf_op jit(solution)/shard_map/gather | solution.py:106
  571.0 14.2 %reshape.261 = f32[256,6,2560]{2,1,0:T(8,128)} reshape(bf16[1536,2560]{1,0:T(8,128)(2,1)} %gather_fusion.1) | data formatting | bytes 23592960 | tf_op jit(solution)/shard_map/convert_element_type | solution.py:106
  585.2 11.4 %multiply_reduce_fusion = bf16[256,2560]{1,0:T(8,128)(2,1)S(1)} fusion(f32[256,6,2560]{2,1,0:T(8,128)} %reshape.261, f32[256,6]{1,0:T(8,128)S(1)} %copy.52), kind=kLoop, calls=%fused_computation.6 | loop fusion | flops 7208960 | bytes 17045504 | tf_op jit(solution)/shard_map/reduce_sum | solution.py:107
  596.6 1.5 copy.56
  598.2 3.1 broadcast_multiply_fusion
  601.3 3.6 gather_fusion.2
  605.0 1.6 dynamic-slice_bitcast_fusion
  606.6 2.5 collective-permute-start
  609.0 2.6 collective-permute-start.1
  611.7 2.7 collective-permute-start.3
  615.1 0.7 fusion.29
  615.8 3.4 collective-permute-start.7
  619.2 22.8 %collective-permute-done.7 = bf16[1,1,1]{2,1,0:T(2,128)(2,1)} collective-permute-done((bf16[1,1,1]{2,1,0:T(2,128)(2,1)}, bf16[1,1,1]{2,1,0:T(2,128)(2,1)}, u32[]{:S(2)}, u32[]{:S(2)}) %collective-permute-start.7) | collective-permute-done | bytes 34 | tf_op jit(solution)/shard_map/ppermute | solution.py:10
  642.2 0.8 dynamic_update_slice.63
  643.0 4.5 collective-permute-done.8
  647.4 3.4 collective-permute-start.9
  650.8 0.8 dynamic_update_slice.64
  651.6 0.7 collective-permute-done.9
  652.4 5.8 collective-permute-start.10
  658.2 0.7 dynamic_update_slice.65
  658.8 0.9 collective-permute-done.10
  659.7 4.4 collective-permute-start.11
  664.2 0.7 dynamic_update_slice.66
  664.9 0.8 collective-permute-done.11
  665.7 4.4 collective-permute-start.12
  670.1 0.8 dynamic_update_slice.67
  670.9 2.4 collective-permute-done.12
  673.4 2.1 collective-permute-start.13
  675.5 0.8 dynamic_update_slice.68
  676.3 4.5 collective-permute-done.13
  681.7 1.0 sort.32
  682.7 1.3 collective-permute-start.5
  683.9 0.7 bitcast_dynamic-update-slice_fusion.6
  684.7 3.6 collective-permute-start.6
  688.3 0.7 bitcast_dynamic-update-slice_fusion.5
  689.0 0.7 bitcast_dynamic-update-slice_fusion.4
  689.7 0.7 bitcast_dynamic-update-slice_fusion.3
  690.4 0.7 bitcast_dynamic-update-slice_fusion.2
  691.1 4.0 collective-permute-done.5
  695.2 0.7 bitcast_dynamic-update-slice_fusion.1
  695.9 3.9 collective-permute-done.6
  699.7 0.7 bitcast_dynamic-update-slice_fusion
  700.5 3.2 copy.53
  703.7 3.6 gather_fusion.4
  707.3 3.3 copy.55
  (55 shorter events, 3.6 us)
Async XLA Ops:
  7.2 292.3 %copy-start = (bf16[2,192,2560]{2,1,0:T(8,128)(2,1)S(1)}, bf16[2,192,2560]{2,1,0:T(8,128)(2,1)}, u32[]{:S(2)}) copy-start(bf16[2,192,2560]{2,1,0:T(8,128)(2,1)} %param.16) | copy-start | bytes 5898244
  11.1 45.8 %copy-start.3 = (bf16[256,2560]{1,0:T(8,128)(2,1)S(1)}, bf16[256,2560]{1,0:T(8,128)(2,1)}, u32[]{:S(2)}) copy-start(bf16[256,2560]{1,0:T(8,128)(2,1)} %param.10) | copy-start | bytes 3932164
  11.1 45.8 %copy-start.4 = (f32[2560]{0:T(1024)S(1)}, f32[2560]{0:T(1024)}, u32[]{:S(2)}) copy-start(f32[2560]{0:T(1024)} %param.11) | copy-start | bytes 30724
  103.3 192.0 %copy-start.6 = (bf16[2,2560,192]{1,2,0:T(8,128)(2,1)S(1)}, bf16[2,2560,192]{1,2,0:T(8,128)(2,1)}, u32[]{:S(2)}) copy-start(bf16[2,2560,192]{1,2,0:T(8,128)(2,1)} %param.14) | copy-start | bytes 5898244
  292.1 3.2 copy-start.2
  352.7 7.6 %copy-start.5 = (bf16[256,6]{0,1:T(8,128)(2,1)S(1)}, bf16[256,6]{0,1:T(8,128)(2,1)}, u32[]{:S(2)}) copy-start(bf16[256,6]{0,1:T(8,128)(2,1)} %param.13) | copy-start | bytes 9220
  352.7 7.7 %copy-start.7 = (s32[8]{0:T(128)S(1)}, s32[8]{0:T(128)}, u32[]{:S(2)}) copy-start(s32[8]{0:T(128)} %param.18) | copy-start | bytes 100
  352.7 8.7 %copy-start.8 = (s32[8]{0:T(128)S(1)}, s32[8]{0:T(128)}, u32[]{:S(2)}) copy-start(s32[8]{0:T(128)} %param.19) | copy-start | bytes 100
  352.7 191.0 %all-to-all-start.1 = ((bf16[2,800,2560]{2,0,1:T(2,128)(2,1)}), bf16[2,800,2560]{2,0,1:T(2,128)(2,1)}, u32[]{:S(2)}, u32[]{:S(2)}) async-start(bf16[2,800,2560]{2,0,1:T(2,128)(2,1)} %copy.50), calls=%async_computation.1 | async-start | bytes 16384000 | tf_op jit(solution)/shard_map/all_to_all | solution.py:103
  360.0 350.6 %reduce-scatter.4.cloned.1.call-start = ((), (), s32[]{:S(2)}) async-start(), calls=%async_computation.3 | async-start | bytes 1474560
  606.6 76.1 %collective-permute-start = (bf16[4,1,1,32,1024]{4,3,0,2,1:T(8,128)(2,1)S(1)}, bf16[4,1,1,32,1024]{4,3,0,2,1:T(8,128)(2,1)S(1)}, u32[]{:S(2)}, u32[]{:S(2)}) collective-permute-start(bf16[4,1,1,32,1024]{4,3,0,2,1:T(8,128)(2,1)S(1)} %get-tuple-element.20), channel_id=1, source_target_pairs={{224,0},{0,32},{32,64},{64,96},{96,128},{128,160},{160,192},{192,2... | collective-permute-start | bytes 786440 | tf_op jit(solution)/shard_map/ppermute | solution.py:10
  609.0 75.6 %collective-permute-start.1 = (bf16[4,1,1,32,1024]{4,3,0,2,1:T(8,128)(2,1)S(1)}, bf16[4,1,1,32,1024]{4,3,0,2,1:T(8,128)(2,1)S(1)}, u32[]{:S(2)}, u32[]{:S(2)}) collective-permute-start(bf16[4,1,1,32,1024]{4,3,0,2,1:T(8,128)(2,1)S(1)} %get-tuple-element.19), channel_id=1, source_target_pairs={{192,0},{224,32},{0,64},{32,96},{64,128},{96,160},{128,192},{160,2... | collective-permute-start | bytes 786440 | tf_op jit(solution)/shard_map/ppermute | solution.py:10
  611.6 77.3 %collective-permute-start.2 = (bf16[4,1,1,32,1024]{4,3,0,2,1:T(8,128)(2,1)S(1)}, bf16[4,1,1,32,1024]{4,3,0,2,1:T(8,128)(2,1)S(1)}, u32[]{:S(2)}, u32[]{:S(2)}) collective-permute-start(bf16[4,1,1,32,1024]{4,3,0,2,1:T(8,128)(2,1)S(1)} %get-tuple-element.18), channel_id=1, source_target_pairs={{160,0},{192,32},{224,64},{0,96},{32,128},{64,160},{96,192},{128,2... | collective-permute-start | bytes 786440 | tf_op jit(solution)/shard_map/ppermute | solution.py:10
  611.7 78.0 %collective-permute-start.3 = (bf16[4,1,1,32,1024]{4,3,0,2,1:T(8,128)(2,1)S(1)}, bf16[4,1,1,32,1024]{4,3,0,2,1:T(8,128)(2,1)S(1)}, u32[]{:S(2)}, u32[]{:S(2)}) collective-permute-start(bf16[4,1,1,32,1024]{4,3,0,2,1:T(8,128)(2,1)S(1)} %get-tuple-element.17), channel_id=1, source_target_pairs={{128,0},{160,32},{192,64},{224,96},{0,128},{32,160},{64,192},{96,2... | collective-permute-start | bytes 786440 | tf_op jit(solution)/shard_map/ppermute | solution.py:10
  615.8 26.2 %collective-permute-start.7 = (bf16[1,1,1]{2,1,0:T(2,128)(2,1)}, bf16[1,1,1]{2,1,0:T(2,128)(2,1)}, u32[]{:S(2)}, u32[]{:S(2)}) collective-permute-start(bf16[1,1,1]{2,1,0:T(2,128)(2,1)} %bitcast.19), channel_id=1, source_target_pairs={{224,0},{0,32},{32,64},{64,96},{96,128},{128,160},{160,192},{192,2... | collective-permute-start | bytes 14 | tf_op jit(solution)/shard_map/ppermute | solution.py:10
  642.0 5.4 collective-permute-start.8
  647.4 4.9 collective-permute-start.9
  652.4 7.4 %collective-permute-start.10 = (bf16[1,1,1]{2,1,0:T(2,128)(2,1)}, bf16[1,1,1]{2,1,0:T(2,128)(2,1)}, u32[]{:S(2)}, u32[]{:S(2)}) collective-permute-start(bf16[1,1,1]{2,1,0:T(2,128)(2,1)} %bitcast.25), channel_id=1, source_target_pairs={{128,0},{160,32},{192,64},{224,96},{0,128},{32,160},{64,192},{96,2... | collective-permute-start | bytes 14 | tf_op jit(solution)/shard_map/ppermute | solution.py:10
  659.7 6.0 collective-permute-start.11
  665.7 7.6 %collective-permute-start.12 = (bf16[1,1,1]{2,1,0:T(2,128)(2,1)}, bf16[1,1,1]{2,1,0:T(2,128)(2,1)}, u32[]{:S(2)}, u32[]{:S(2)}) collective-permute-start(bf16[1,1,1]{2,1,0:T(2,128)(2,1)} %bitcast.29), channel_id=1, source_target_pairs={{64,0},{96,32},{128,64},{160,96},{192,128},{224,160},{0,192},{32,2... | collective-permute-start | bytes 14 | tf_op jit(solution)/shard_map/ppermute | solution.py:10
  673.4 7.4 %collective-permute-start.13 = (bf16[1,1,1]{2,1,0:T(2,128)(2,1)}, bf16[1,1,1]{2,1,0:T(2,128)(2,1)}, u32[]{:S(2)}, u32[]{:S(2)}) collective-permute-start(bf16[1,1,1]{2,1,0:T(2,128)(2,1)} %bitcast.31), channel_id=1, source_target_pairs={{32,0},{64,32},{96,64},{128,96},{160,128},{192,160},{224,192},{0,2... | collective-permute-start | bytes 14 | tf_op jit(solution)/shard_map/ppermute | solution.py:10
  680.8 9.6 %collective-permute-start.4 = (bf16[4,1,1,32,1024]{4,3,0,2,1:T(8,128)(2,1)S(1)}, bf16[4,1,1,32,1024]{4,3,0,2,1:T(8,128)(2,1)S(1)}, u32[]{:S(2)}, u32[]{:S(2)}) collective-permute-start(bf16[4,1,1,32,1024]{4,3,0,2,1:T(8,128)(2,1)S(1)} %get-tuple-element.16), channel_id=1, source_target_pairs={{96,0},{128,32},{160,64},{192,96},{224,128},{0,160},{32,192},{64,2... | collective-permute-start | bytes 786440 | tf_op jit(solution)/shard_map/ppermute | solution.py:10
  682.7 12.5 %collective-permute-start.5 = (bf16[4,1,1,32,1024]{4,3,0,2,1:T(8,128)(2,1)S(1)}, bf16[4,1,1,32,1024]{4,3,0,2,1:T(8,128)(2,1)S(1)}, u32[]{:S(2)}, u32[]{:S(2)}) collective-permute-start(bf16[4,1,1,32,1024]{4,3,0,2,1:T(8,128)(2,1)S(1)} %get-tuple-element.15), channel_id=1, source_target_pairs={{64,0},{96,32},{128,64},{160,96},{192,128},{224,160},{0,192},{32,2... | collective-permute-start | bytes 786440 | tf_op jit(solution)/shard_map/ppermute | solution.py:10
  684.7 15.1 %collective-permute-start.6 = (bf16[4,1,1,32,1024]{4,3,0,2,1:T(8,128)(2,1)S(1)}, bf16[4,1,1,32,1024]{4,3,0,2,1:T(8,128)(2,1)S(1)}, u32[]{:S(2)}, u32[]{:S(2)}) collective-permute-start(bf16[4,1,1,32,1024]{4,3,0,2,1:T(8,128)(2,1)S(1)} %get-tuple-element.14), channel_id=1, source_target_pairs={{32,0},{64,32},{96,64},{128,96},{160,128},{192,160},{224,192},{0,2... | collective-permute-start | bytes 786440 | tf_op jit(solution)/shard_map/ppermute | solution.py:10
  707.3 3.3 copy-start.1
Sparse Core Ops, SparseCore 0:
  598.2 89.1 reduce-scatter.3
where the time goes:
time: 727 us; the launch traced here: 718 us
  waiting for transfers between devices  227 us (31%)
  blocking collectives  189 us (26%)
  local copies, waits for them, and re-layouts  169 us (23%)
  other arithmetic  55.6 us (8%)
  starting transfers between devices  44.2 us (6%)
  matrix products  18.9 us (3%)
  between operations  14.6 us (2%)
    all_to_all x1, blocking collectives, per_device(): lax.all_to_all(outgoing, 'exp', split_axis=1, concat_axis=1, tiled=True)  189 us
    all_to_all x1, waiting for transfers between devices, per_device(): lax.all_to_all(partial_value, 'exp', split_axis=1, concat_axis=1, tiled=T...  182 us
    ppermute x14, waiting for transfers between devices, passed_along(): return lax.ppermute(block, axis, route)  44.5 us
    convert_element_type x1, local copies, waits for them, and re-layouts, expert_block(): jnp.einsum('erf,efd->erd', hidden, w_down, preferred_element_type=jnp.flo...  38.5 us
    reshape x1, local copies, waits for them, and re-layouts, per_device(): fill_slots(normed, slot_index, total_slots, topk)  37.7 us
    ppermute x14, starting transfers between devices, passed_along(): return lax.ppermute(block, axis, route)  36.7 us
    another operation x3, other arithmetic  35.9 us
    gather x1, local copies, waits for them, and re-layouts, per_device(): returned[slot_index].astype(jnp.float32).reshape(tok_count, topk, width)  19.5 us
  transfers between devices with their start and end apart: 16, of which 10 were waited for; matrix products, arithmetic and copies ran while one was open for 4% of the time, Pallas kernels for 0%

commit v1 on v0

v1 whole, which is shorter than its diff:
```python
import jax
import jax.numpy as jnp
from jax import lax
from jax.sharding import PartitionSpec as P


def rms_normed(tokens, norm_gain):
    values = tokens.astype(jnp.float32)
    scale = lax.rsqrt(jnp.mean(values * values, axis=-1, keepdims=True) + 1e-06)
    return (values * scale * norm_gain).astype(jnp.bfloat16)


def route_positions(routes, experts):
    tok_count = routes.shape[0]
    expert_ids = jnp.arange(experts, dtype=jnp.int32)
    onehot = routes[:, :, None] == expert_ids[None, None, :]
    member = jnp.any(onehot, axis=1).astype(jnp.bfloat16)
    rows = jnp.arange(tok_count, dtype=jnp.int32)
    earlier = (rows[None, :] < rows[:, None]).astype(jnp.bfloat16)
    counts = jnp.dot(earlier, member, preferred_element_type=jnp.float32)
    picked = jnp.sum(jnp.where(onehot, counts[:, None, :], 0.0), axis=2)
    return picked.astype(jnp.int32)


def expert_block(rows, w_gate, w_up, w_down):
    gate = jnp.einsum("erd,edf->erf", rows, w_gate, preferred_element_type=jnp.float32)
    upward = jnp.einsum("erd,edf->erf", rows, w_up, preferred_element_type=jnp.float32)
    hidden = (jax.nn.silu(gate) * upward).astype(jnp.bfloat16)
    return jnp.einsum("erf,efd->erd", hidden, w_down, preferred_element_type=jnp.float32).astype(
        jnp.bfloat16
    )


def relayout(kv_prefill, block_map, block_empty):
    layers, blocks, block_rows, kv_width = kv_prefill.shape
    exp_count = lax.axis_size("exp")
    keep = (1 - block_empty).astype(kv_prefill.dtype)
    peer = block_map // blocks // exp_count
    target = block_map % blocks
    order = jnp.argsort(peer)
    outgoing = kv_prefill[:, order] * keep[order][None, :, None, None]
    labels = target[order]
    arrived = lax.all_to_all(outgoing, "seq", split_axis=1, concat_axis=1, tiled=True)
    slots = lax.all_to_all(labels, "seq", split_axis=0, concat_axis=0, tiled=True)
    return arrived[:, jnp.argsort(slots)]


def per_device(
    tokens,
    norm_gain,
    routes,
    route_weights,
    w_gate,
    w_up,
    w_down,
    kv_prefill,
    block_map,
    block_empty,
):
    local_experts = w_gate.shape[0]
    exp_count = lax.axis_size("exp")
    seq_count = lax.axis_size("seq")
    experts = local_experts * exp_count
    tok_count, topk = routes.shape
    capacity = tok_count * topk // experts + 1
    seq_per_expert = seq_count // local_experts
    per_dev = -(-capacity // seq_per_expert)
    my_seq = lax.axis_index("seq")

    normed = rms_normed(tokens, norm_gain)
    width = normed.shape[1]

    position = route_positions(routes, experts)
    owner = routes // local_experts
    local_index = routes % local_experts
    sender = local_index * seq_per_expert + position // per_dev
    within = position % per_dev

    send_slots = exp_count * per_dev
    slot_of = jnp.where(sender == my_seq, owner * per_dev + within, -1)
    slot_ids = jnp.arange(send_slots, dtype=jnp.int32)
    pick = jnp.any(slot_of[None, :, :] == slot_ids[:, None, None], axis=2).astype(jnp.bfloat16)
    outgoing = jnp.dot(pick, normed, preferred_element_type=jnp.float32).astype(jnp.bfloat16)
    outgoing = outgoing.reshape(exp_count, per_dev, width)
    arrived = lax.all_to_all(outgoing, "exp", split_axis=0, concat_axis=0, tiled=True)
    gathered = lax.all_gather(arrived, "seq", axis=0, tiled=False)
    rows = gathered.reshape(local_experts, seq_per_expert * exp_count * per_dev, width)

    partial_value = expert_block(rows, w_gate, w_up, w_down)
    summed = lax.psum_scatter(partial_value, "seq", scatter_dimension=2, tiled=True)
    part_width = summed.shape[2]
    summed = summed.reshape(local_experts, seq_per_expert, exp_count, per_dev, part_width)
    summed = jnp.transpose(summed, (2, 0, 1, 3, 4))
    returned = lax.all_to_all(summed, "exp", split_axis=0, concat_axis=0, tiled=True)
    recv_slots = exp_count * seq_count * per_dev
    returned = returned.reshape(recv_slots, part_width)

    recv_slot = (owner * seq_count + sender) * per_dev + within
    recv_ids = jnp.arange(recv_slots, dtype=jnp.int32)
    weights = route_weights.astype(jnp.float32)
    mix = jnp.sum(
        jnp.where(recv_slot[:, :, None] == recv_ids[None, None, :], weights[:, :, None], 0.0), axis=1
    ).astype(jnp.bfloat16)
    mixed = jnp.dot(mix, returned, preferred_element_type=jnp.float32).astype(jnp.bfloat16)

    kv_decode = relayout(kv_prefill, block_map, block_empty)
    return (mixed, kv_decode)


def solution(mesh):
    in_specs = (
        P("exp", None),
        P(),
        P("exp", None),
        P("exp", None),
        P("exp", None, "seq"),
        P("exp", None, "seq"),
        P("exp", "seq", None),
        P(None, ("seq", "exp"), None, None),
        P(("seq", "exp")),
        P(("seq", "exp")),
    )
    out_specs = (P("exp", "seq"), P(None, ("seq", "exp"), None, None))
    return jax.shard_map(
        per_device, mesh=mesh, in_specs=in_specs, out_specs=out_specs, check_vma=False
    )
```

time: 727 us -> 437 us (0.60)
  blocking collectives: 189 us -> 41.1 us
  local copies, waits for them, and re-layouts: 169 us -> 54.3 us
  other arithmetic: 55.6 us -> 13.2 us
  waiting for transfers between devices: 227 us -> 258 us
  starting transfers between devices: 44.2 us -> 20.7 us
  matrix products: 18.9 us -> 28.2 us
    all_to_all x1 -> x3, waiting for transfers between devices: 182 us -> 19.1 us  [the longest x1 19.1 us: per_device(): lax.all_to_all(summed, 'exp', split_axis=0, concat_axis=0, tiled=True)]
    all_to_all x1, blocking collectives: 189 us -> 41.1 us  [per_device(): lax.all_to_all(outgoing, 'exp', split_axis=0, concat_axis=0, tiled=True)]
    reduce_scatter x0 -> x1, waiting for transfers between devices: none -> 123 us  [per_device(): lax.psum_scatter(partial_value, 'seq', scatter_dimension=2, tiled=True)]
    all_gather x0 -> x1, waiting for transfers between devices: none -> 116 us  [per_device(): gathered = lax.all_gather(arrived, 'seq', axis=0, tiled=False)]
    convert_element_type x3 -> x0, local copies, waits for them, and re-layouts: 52.9 us -> none  [the longest x1 38.5 us: expert_block(): jnp.einsum('erf,efd->erd', hidden, w_down, preferred_element_type=jnp.flo...]
    ppermute x14 -> x0, waiting for transfers between devices: 44.5 us -> none  [passed_along(): return lax.ppermute(block, axis, route)]
    ppermute x14 -> x0, starting transfers between devices: 36.7 us -> none  [passed_along(): return lax.ppermute(block, axis, route)]
    another operation x3 -> x0, other arithmetic: 35.9 us -> none
  transfers between devices with their start and end apart: 16 -> 5, of which waited for: 10 -> 3; matrix products, arithmetic and copies ran while one was open for 4% -> 7% of each run, Pallas kernels for 0% -> 0%
where the time goes in v1:
time: 437 us; the launch traced here: 430 us
  waiting for transfers between devices  258 us (59%)
  local copies, waits for them, and re-layouts  54.3 us (12%)
  blocking collectives  41.1 us (9%)
  matrix products  28.2 us (6%)
  starting transfers between devices  20.7 us (5%)
  between operations  14.2 us (3%)
  other arithmetic  13.2 us (3%)
    reduce_scatter x1, waiting for transfers between devices, per_device(): lax.psum_scatter(partial_value, 'seq', scatter_dimension=2, tiled=True)  123 us
    all_gather x1, waiting for transfers between devices, per_device(): gathered = lax.all_gather(arrived, 'seq', axis=0, tiled=False)  116 us
    all_to_all x1, blocking collectives, per_device(): lax.all_to_all(outgoing, 'exp', split_axis=0, concat_axis=0, tiled=True)  41.1 us
    all_to_all x1, waiting for transfers between devices, per_device(): lax.all_to_all(summed, 'exp', split_axis=0, concat_axis=0, tiled=True)  19.1 us
    dot_general x1, matrix products, expert_block(): jnp.einsum('erf,efd->erd', hidden, w_down, preferred_element_type=jnp.flo...  15.4 us
    reshape x1, local copies, waits for them, and re-layouts, per_device(): gathered.reshape(local_experts, seq_per_expert * exp_count * per_dev, width)  13.7 us
    all_gather x1, local copies, waits for them, and re-layouts, per_device(): gathered = lax.all_gather(arrived, 'seq', axis=0, tiled=False)  12.7 us
  transfers between devices with their start and end apart: 5, of which 3 were waited for; matrix products, arithmetic and copies ran while one was open for 7% of the time, Pallas kernels for 0%

profile of v1, /device:TPU:120, one launch (start us, length us, event | category | flops | bytes accessed | tf_op | source)
XLA Modules:
  0.0 429.9 jit_solution(16730967040517648215)
XLA Ops:
  7.2 0.0 copy-start
  7.2 0.0 all-gather.3.cloned.1.call-start
  7.2 0.9 fusion.10
  8.1 0.2 fusion.11
  8.3 0.8 select_reduce_fusion.1
  9.1 0.7 multiply_add_fusion
  9.8 0.2 fusion.3
  10.0 1.7 fusion
  11.6 2.9 convolution_convert_fusion.1
  14.6 1.5 reshape.33
  16.0 41.1 %all_to_all.27 = bf16[32,7,2560]{2,1,0:T(8,128)(2,1)S(1)} all-to-all(bf16[32,7,2560]{2,1,0:T(8,128)(2,1)S(1)} %reshape.33), channel_id=1, replica_groups=mesh['seq'=8,'exp'=32] {'exp'}, dimensions={0} | all-to-all | bytes 2293760 | tf_op jit(solution)/shard_map/all_to_all | solution.py:85
  57.2 1.4 copy.60
  58.6 0.0 all-gather.3.cloned.1.call-update
  58.6 0.2 reduce-scatter.2.cloned.1.call-start
  58.8 115.7 %all-gather.3.cloned.1.call-done = bf16[256,7,2560]{2,0,1:T(8,128)(2,1)} async-done(((bf16[32,7,2560]{2,0,1:T(8,128)(2,1)}), bf16[256,7,2560]{2,0,1:T(8,128)(2,1)}) %all-gather.3.cloned.1.call-update) | async-done | bytes 9175056 | tf_op jit(solution)/shard_map/all_gather | solution.py:86
  174.5 12.7 %copy.61 = bf16[256,7,2560]{2,1,0:T(8,128)(2,1)} copy(bf16[256,7,2560]{2,0,1:T(8,128)(2,1)} %all-gather.3.cloned.1.call-done) | data formatting | bytes 18350080 | tf_op jit(solution)/shard_map/all_gather | solution.py:86
  187.2 13.7 %reshape.34 = bf16[2,896,2560]{2,1,0:T(8,128)(2,1)} reshape(bf16[256,7,2560]{2,1,0:T(8,128)(2,1)} %copy.61) | data formatting | bytes 18350080 | tf_op jit(solution)/shard_map/reshape | solution.py:87
  200.9 7.2 %fusion.19 = f32[2,896,192]{1,2,0:T(8,128)S(1)} fusion(bf16[2,896,2560]{2,1,0:T(8,128)(2,1)} %reshape.34, bf16[2,2560,192]{1,2,0:T(8,128)(2,1)} %param.14), kind=kOutput, calls=%fused_computation.62 | convolution fusion | flops 1761607680 | bytes 12517376 | tf_op jit(solution)/shard_map/erd,edf->erf/dot_general | solution.py:26
  208.0 15.4 %convolution_convert_fusion = bf16[2,896,2560]{1,2,0:T(8,128)(2,1)} fusion(bf16[2,192,2560]{2,1,0:T(8,128)(2,1)} %param.16, bf16[2,896,2560]{2,1,0:T(8,128)(2,1)} %reshape.34, bf16[2,2560,192]{1,2,0:T(8,128)(2,1)} %param.15, f32[2,896,192]{1,2,0:T(8,128)S(1)} %fusion.19), kind=kOutput, calls=%fused_computation.6 | convolution fusion | flops 3529867264 | bytes 23658496 | tf_op jit(solution)/shard_map/erf,efd->erd/dot_general | solution.py:29
  223.5 0.0 copy-start.2
  223.5 0.0 reduce-scatter.2.cloned.1.call-update
  223.5 0.6 copy-done.2
  224.2 1.0 sort.31
  225.1 0.6 gather_fusion.2
  225.8 0.7 copy.65
  226.5 5.6 %all-to-all-start.3 = ((s32[8,1,1]{2,1,0:T(1,128)}), s32[8,1,1]{2,1,0:T(1,128)S(1)}, u32[]{:S(2)}, u32[]{:S(2)}) async-start(s32[8,1,1]{2,1,0:T(1,128)} %copy.65), calls=%async_computation.4 | async-start | bytes 8192 | tf_op jit(solution)/shard_map/all_to_all | solution.py:44
  232.1 0.0 copy-done
  232.1 0.0 copy-start.3
  232.1 2.0 gather_fusion
  234.1 0.0 copy-done.3
  234.1 0.6 gather_fusion.1
  234.7 3.8 multiply_bitcast_fusion
  238.5 0.0 all-to-all-done.3
  238.5 7.2 %all-to-all-start.2 = ((bf16[4,8,32,1024]{3,2,0,1:T(8,128)(2,1)}), bf16[4,8,32,1024]{3,2,0,1:T(8,128)(2,1)}, u32[]{:S(2)}, u32[]{:S(2)}) async-start(bf16[4,8,32,1024]{3,2,0,1:T(8,128)(2,1)} %multiply_bitcast_fusion), calls=%async_computation.3 | async-start | bytes 4194304 | tf_op jit(solution)/shard_map/all_to_all | solution.py:43
  245.7 123.4 %reduce-scatter.2.cloned.1.call-done = bf16[2,896,320]{1,2,0:T(8,128)(2,1)} async-done(((bf16[2,896,2560]{1,2,0:T(8,128)(2,1)}), bf16[2,896,320]{1,2,0:T(8,128)(2,1)}) %reduce-scatter.2.cloned.1.call-update) | async-done | bytes 1146896 | tf_op jit(solution)/shard_map/reduce_scatter | solution.py:90
  369.2 4.4 %copy.62 = bf16[2,896,320]{2,0,1:T(2,128)(2,1)S(1)} copy(bf16[2,896,320]{1,2,0:T(8,128)(2,1)} %reduce-scatter.2.cloned.1.call-done) | data formatting | bytes 2293760 | tf_op jit(solution)/shard_map/reduce_scatter | solution.py:90
  373.5 2.0 copy.63
  375.5 0.0 copy-start.1
  375.5 0.0 all-to-all-done.2
  375.5 7.6 %all-to-all-start.1 = ((bf16[32,2,4,7,320]{4,1,3,2,0:T(2,128)(2,1)}), bf16[32,2,4,7,320]{4,1,3,2,0:T(2,128)(2,1)S(1)}, u32[]{:S(2)}, u32[]{:S(2)}) async-start(bf16[32,2,4,7,320]{4,1,3,2,0:T(2,128)(2,1)} %copy.63), calls=%async_computation.2 | async-start | bytes 2752512 | tf_op jit(solution)/shard_map/all_to_all | solution.py:94
  383.2 0.0 copy-done.1
  383.2 3.0 select_reduce_fusion
  386.2 0.2 reduce
  386.4 1.0 sort.32
  387.4 3.2 copy.66
  390.6 3.6 gather_fusion.3
  394.2 3.2 copy.67
  397.4 19.1 %all-to-all-done.1 = bf16[32,2,4,7,320]{4,1,3,2,0:T(2,128)(2,1)S(1)} async-done(((bf16[32,2,4,7,320]{4,1,3,2,0:T(2,128)(2,1)}), bf16[32,2,4,7,320]{4,1,3,2,0:T(2,128)(2,1)S(1)}, u32[]{:S(2)}, u32[]{:S(2)}) %all-to-all-start.1) | async-done | bytes 1146912 | tf_op jit(solution)/shard_map/all_to_all | solution.py:94
  416.5 1.5 copy.64
  418.0 2.6 reshape.36
  420.6 2.5 convolution_convert_fusion.2
  (10 shorter events, 0.1 us)
Async XLA Ops:
  7.2 224.9 %copy-start = (bf16[4,8,32,1024]{3,2,1,0:T(8,128)(2,1)S(1)}, bf16[4,8,32,1024]{3,2,1,0:T(8,128)(2,1)}, u32[]{:S(2)}) copy-start(bf16[4,8,32,1024]{3,2,1,0:T(8,128)(2,1)} %param.17) | copy-start | bytes 6291460
  7.2 167.3 %all-gather.3.cloned.1.call-start = ((), (), s32[]{:S(2)}) async-start(), calls=%async_computation.6 | async-start | bytes 10321920 | tf_op jit(solution)/shard_map/all_gather | solution.py:86
  58.6 310.6 %reduce-scatter.2.cloned.1.call-start = ((), (), s32[]{:S(2)}) async-start(), calls=%async_computation.5 | async-start | bytes 10321920 | tf_op jit(solution)/shard_map/reduce_scatter | solution.py:90
  223.5 0.7 copy-start.2
  226.5 12.0 %all-to-all-start.3 = ((s32[8,1,1]{2,1,0:T(1,128)}), s32[8,1,1]{2,1,0:T(1,128)S(1)}, u32[]{:S(2)}, u32[]{:S(2)}) async-start(s32[8,1,1]{2,1,0:T(1,128)} %copy.65), calls=%async_computation.4 | async-start | bytes 8192 | tf_op jit(solution)/shard_map/all_to_all | solution.py:44
  232.1 2.0 copy-start.3
  238.5 137.1 %all-to-all-start.2 = ((bf16[4,8,32,1024]{3,2,0,1:T(8,128)(2,1)}), bf16[4,8,32,1024]{3,2,0,1:T(8,128)(2,1)}, u32[]{:S(2)}, u32[]{:S(2)}) async-start(bf16[4,8,32,1024]{3,2,0,1:T(8,128)(2,1)} %multiply_bitcast_fusion), calls=%async_computation.3 | async-start | bytes 4194304 | tf_op jit(solution)/shard_map/all_to_all | solution.py:43
  375.5 7.6 %copy-start.1 = (bf16[256,6]{0,1:T(8,128)(2,1)S(1)}, bf16[256,6]{0,1:T(8,128)(2,1)}, u32[]{:S(2)}) copy-start(bf16[256,6]{0,1:T(8,128)(2,1)} %param.13) | copy-start | bytes 9220
  375.5 40.9 %all-to-all-start.1 = ((bf16[32,2,4,7,320]{4,1,3,2,0:T(2,128)(2,1)}), bf16[32,2,4,7,320]{4,1,3,2,0:T(2,128)(2,1)S(1)}, u32[]{:S(2)}, u32[]{:S(2)}) async-start(bf16[32,2,4,7,320]{4,1,3,2,0:T(2,128)(2,1)} %copy.63), calls=%async_computation.2 | async-start | bytes 2752512 | tf_op jit(solution)/shard_map/all_to_all | solution.py:94
Sparse Core Ops, SparseCore 0:
  58.7 115.7 all-gather.2
  223.6 145.4 reduce-scatter.1

commit v2 on v1

--- a/solution.py
+++ b/solution.py
@@ -20,15 +20,6 @@
     counts = jnp.dot(earlier, member, preferred_element_type=jnp.float32)
     picked = jnp.sum(jnp.where(onehot, counts[:, None, :], 0.0), axis=2)
     return picked.astype(jnp.int32)
-
-
-def expert_block(rows, w_gate, w_up, w_down):
-    gate = jnp.einsum("erd,edf->erf", rows, w_gate, preferred_element_type=jnp.float32)
-    upward = jnp.einsum("erd,edf->erf", rows, w_up, preferred_element_type=jnp.float32)
-    hidden = (jax.nn.silu(gate) * upward).astype(jnp.bfloat16)
-    return jnp.einsum("erf,efd->erd", hidden, w_down, preferred_element_type=jnp.float32).astype(
-        jnp.bfloat16
-    )
 
 
 def relayout(kv_prefill, block_map, block_empty):
@@ -76,26 +67,33 @@
     sender = local_index * seq_per_expert + position // per_dev
     within = position % per_dev
 
-    send_slots = exp_count * per_dev
-    slot_of = jnp.where(sender == my_seq, owner * per_dev + within, -1)
+    send_slots = per_dev * exp_count
+    slot_of = jnp.where(sender == my_seq, within * exp_count + owner, -1)
     slot_ids = jnp.arange(send_slots, dtype=jnp.int32)
     pick = jnp.any(slot_of[None, :, :] == slot_ids[:, None, None], axis=2).astype(jnp.bfloat16)
     outgoing = jnp.dot(pick, normed, preferred_element_type=jnp.float32).astype(jnp.bfloat16)
-    outgoing = outgoing.reshape(exp_count, per_dev, width)
-    arrived = lax.all_to_all(outgoing, "exp", split_axis=0, concat_axis=0, tiled=True)
-    gathered = lax.all_gather(arrived, "seq", axis=0, tiled=False)
-    rows = gathered.reshape(local_experts, seq_per_expert * exp_count * per_dev, width)
+    outgoing = outgoing.reshape(per_dev, exp_count, width)
+    arrived = lax.all_to_all(outgoing, "exp", split_axis=1, concat_axis=1, tiled=True)
+    copies = jnp.broadcast_to(arrived[None], (seq_count,) + arrived.shape)
+    gathered = lax.all_to_all(copies, "seq", split_axis=0, concat_axis=0, tiled=True)
+    rows = gathered.reshape(local_experts, seq_per_expert * per_dev * exp_count, width)
 
-    partial_value = expert_block(rows, w_gate, w_up, w_down)
-    summed = lax.psum_scatter(partial_value, "seq", scatter_dimension=2, tiled=True)
-    part_width = summed.shape[2]
-    summed = summed.reshape(local_experts, seq_per_expert, exp_count, per_dev, part_width)
-    summed = jnp.transpose(summed, (2, 0, 1, 3, 4))
-    returned = lax.all_to_all(summed, "exp", split_axis=0, concat_axis=0, tiled=True)
-    recv_slots = exp_count * seq_count * per_dev
+    gate = jnp.einsum("erd,edf->erf", rows, w_gate, preferred_element_type=jnp.float32)
+    upward = jnp.einsum("erd,edf->erf", rows, w_up, preferred_element_type=jnp.float32)
+    hidden = (jax.nn.silu(gate) * upward).astype(jnp.bfloat16)
+    part_width = width // seq_count
+    down = w_down.reshape(local_experts, w_down.shape[1], seq_count, part_width)
+    partial_value = jnp.einsum(
+        "erf,efcd->cerd", hidden, down, preferred_element_type=jnp.float32
+    ).astype(jnp.bfloat16)
+    pieces = lax.all_to_all(partial_value, "seq", split_axis=0, concat_axis=0, tiled=True)
+    summed = jnp.sum(pieces.astype(jnp.float32), axis=0).astype(jnp.bfloat16)
+    summed = summed.reshape(seq_count * per_dev, exp_count, part_width)
+    returned = lax.all_to_all(summed, "exp", split_axis=1, concat_axis=1, tiled=True)
+    recv_slots = seq_count * per_dev * exp_count
     returned = returned.reshape(recv_slots, part_width)
 
-    recv_slot = (owner * seq_count + sender) * per_dev + within
+    recv_slot = (sender * per_dev + within) * exp_count + owner
     recv_ids = jnp.arange(recv_slots, dtype=jnp.int32)
     weights = route_weights.astype(jnp.float32)
     mix = jnp.sum(

time: 437 us -> 382 us (0.87)
  waiting for transfers between devices: 258 us -> 227 us
  local copies, waits for them, and re-layouts: 54.3 us -> 36.9 us
  between operations: 14.2 us -> 0.8 us
  starting transfers between devices: 20.7 us -> 29.6 us
  other arithmetic: 13.2 us -> 18.7 us
  matrix products: 28.2 us -> 22.8 us
    all_to_all x1 -> x3, waiting for transfers between devices: 19.1 us -> 210 us  [the longest x1 95.9 us: per_device(): lax.all_to_all(partial_value, 'seq', split_axis=0, concat_axis=0, tiled=T...]
    reduce_scatter x1 -> x0, waiting for transfers between devices: 123 us -> none  [per_device(): lax.psum_scatter(partial_value, 'seq', scatter_dimension=2, tiled=True)]
    all_gather x1 -> x0, waiting for transfers between devices: 116 us -> none  [per_device(): gathered = lax.all_gather(arrived, 'seq', axis=0, tiled=False)]
    all_to_all x1, waiting for transfers between devices: 0.01 us -> 16.9 us  [relayout(): lax.all_to_all(outgoing, 'seq', split_axis=1, concat_axis=1, tiled=True)]
    all_gather x1 -> x0, local copies, waits for them, and re-layouts: 12.7 us -> none  [per_device(): gathered = lax.all_gather(arrived, 'seq', axis=0, tiled=False)]
    all_to_all x1 -> x3, starting transfers between devices: 7.6 us -> 19.5 us  [the longest x1 7.22 us: per_device(): lax.all_to_all(partial_value, 'seq', split_axis=0, concat_axis=0, tiled=T...]
    reshape x3, local copies, waits for them, and re-layouts: 17.7 us -> 6.87 us  [the longest x1 4.68 us: per_device(): down = w_down.reshape(local_experts, w_down.shape[1], seq_count, part_width)]
    convert_element_type x0 -> x1, local copies, waits for them, and re-layouts: none -> 8.04 us  [per_device(): partial_value = jnp.einsum('erf,efcd->cerd', hidden, down, preferred_elem...]
  transfers between devices with their start and end apart: 5 -> 5, of which waited for: 3 -> 4; matrix products, arithmetic and copies ran while one was open for 7% -> 17% of each run, Pallas kernels for 0% -> 0%
where the time goes in v2:
time: 382 us; the launch traced here: 377 us
  waiting for transfers between devices  227 us (59%)
  blocking collectives  41.1 us (11%)
  local copies, waits for them, and re-layouts  36.9 us (10%)
  starting transfers between devices  29.6 us (8%)
  matrix products  22.8 us (6%)
  other arithmetic  18.7 us (5%)
    all_to_all x1, waiting for transfers between devices, per_device(): lax.all_to_all(partial_value, 'seq', split_axis=0, concat_axis=0, tiled=T...  95.9 us
    all_to_all x1, waiting for transfers between devices, per_device(): lax.all_to_all(copies, 'seq', split_axis=0, concat_axis=0, tiled=True)  95.1 us
    all_to_all x1, blocking collectives, per_device(): lax.all_to_all(outgoing, 'exp', split_axis=1, concat_axis=1, tiled=True)  41.1 us
    all_to_all x1, waiting for transfers between devices, per_device(): lax.all_to_all(summed, 'exp', split_axis=1, concat_axis=1, tiled=True)  19.2 us
    all_to_all x1, waiting for transfers between devices, relayout(): lax.all_to_all(outgoing, 'seq', split_axis=1, concat_axis=1, tiled=True)  16.9 us
    convert_element_type x1, local copies, waits for them, and re-layouts, per_device(): partial_value = jnp.einsum('erf,efcd->cerd', hidden, down, preferred_elem...  8.04 us
  transfers between devices with their start and end apart: 5, of which 4 were waited for; matrix products, arithmetic and copies ran while one was open for 17% of the time, Pallas kernels for 0%

profile of v2, /device:TPU:120, one launch (start us, length us, event | category | flops | bytes accessed | tf_op | source)
XLA Modules:
  0.0 377.1 jit_solution(5521941620104679368)
XLA Ops:
  0.6 0.0 copy-start
  0.6 0.9 fusion.11
  1.5 0.2 fusion.12
  1.7 0.8 select_reduce_fusion.1
  2.5 0.7 multiply_add_fusion
  3.2 0.2 fusion.4
  3.4 1.7 fusion
  5.1 1.9 convolution_convert_fusion
  7.0 0.6 copy.62
  7.6 41.1 %all_to_all.37 = bf16[7,32,2560]{2,0,1:T(8,128)(2,1)S(1)} all-to-all(bf16[7,32,2560]{2,0,1:T(8,128)(2,1)S(1)} %copy.62), channel_id=1, replica_groups=mesh['seq'=8,'exp'=32] {'exp'}, dimensions={1} | all-to-all | bytes 2293760 | tf_op jit(solution)/shard_map/all_to_all | solution.py:76
  48.8 0.4 copy.63
  49.2 4.7 %broadcast_in_dim.36 = bf16[8,7,32,2560]{3,2,1,0:T(8,128)(2,1)} broadcast(bf16[7,32,2560]{2,1,0:T(8,128)(2,1)S(1)} %copy.63), dimensions={1,2,3} | broadcast | bytes 10321920 | tf_op jit(solution)/shard_map/broadcast_in_dim | solution.py:77
  53.9 6.9 %all-to-all-start.1 = ((bf16[8,7,32,2560]{3,2,1,0:T(8,128)(2,1)}), bf16[8,7,32,2560]{3,2,1,0:T(8,128)(2,1)}, u32[]{:S(2)}, u32[]{:S(2)}) async-start(bf16[8,7,32,2560]{3,2,1,0:T(8,128)(2,1)} %broadcast_in_dim.36), calls=%async_computation.1 | async-start | bytes 18350080 | tf_op jit(solution)/shard_map/all_to_all | solution.py:78
  60.7 0.0 copy-start.5
  60.7 4.7 %reshape.39 = bf16[2,192,8,320]{3,2,1,0:T(8,128)(2,1)} reshape(bf16[2,192,2560]{2,1,0:T(8,128)(2,1)} %param.16) | data formatting | bytes 3932160 | tf_op jit(solution)/shard_map/reshape | solution.py:85
  65.4 0.0 copy-done.5
  65.5 1.0 sort.31
  66.4 0.6 gather_fusion.2
  67.1 0.7 copy.70
  67.8 95.1 %all-to-all-done.1 = bf16[8,7,32,2560]{3,2,1,0:T(8,128)(2,1)} async-done(((bf16[8,7,32,2560]{3,2,1,0:T(8,128)(2,1)}), bf16[8,7,32,2560]{3,2,1,0:T(8,128)(2,1)}, u32[]{:S(2)}, u32[]{:S(2)}) %all-to-all-start.1) | async-done | bytes 9175072 | tf_op jit(solution)/shard_map/all_to_all | solution.py:78
  162.8 5.0 %all-to-all-start.5 = ((s32[8,1,1]{2,1,0:T(1,128)}), s32[8,1,1]{2,1,0:T(1,128)S(1)}, u32[]{:S(2)}, u32[]{:S(2)}) async-start(s32[8,1,1]{2,1,0:T(1,128)} %copy.70), calls=%async_computation.5 | async-start | bytes 8192 | tf_op jit(solution)/shard_map/all_to_all | solution.py:35
  167.9 0.0 copy-start.4
  167.9 7.3 %fusion.19 = f32[2,896,192]{1,2,0:T(8,128)S(1)} fusion(bf16[2,896,2560]{2,1,0:T(8,128)(2,1)} %bitcast.1, bf16[2,2560,192]{1,2,0:T(8,128)(2,1)} %param.14), kind=kOutput, calls=%fused_computation.62 | convolution fusion | flops 1761607680 | bytes 12517376 | tf_op jit(solution)/shard_map/erd,edf->erf/dot_general | solution.py:81
  175.1 0.0 copy-done.4
  175.2 0.0 copy-start.1
  175.2 6.8 %fusion.9 = bf16[2,896,192,1]{1,2,3,0:T(8,128)(2,1)S(1)} fusion(bf16[2,896,2560]{2,1,0:T(8,128)(2,1)} %bitcast.1, bf16[2,2560,192]{1,2,0:T(8,128)(2,1)S(1)} %copy-done.4, f32[2,896,192]{1,2,0:T(8,128)S(1)} %fusion.19), kind=kOutput, calls=%fused_computation.21 | convolution fusion | flops 1763672064 | bytes 13205504 | tf_op jit(solution)/shard_map/erd,edf->erf/dot_general | solution.py:82
  182.0 0.0 copy-done.1
  182.0 5.3 %convert_bitcast_fusion = bf16[8,2,896,320]{2,3,0,1:T(8,128)(2,1)} fusion(bf16[2,896,192,1]{1,2,3,0:T(8,128)(2,1)S(1)} %fusion.9, bf16[2,192,8,320]{3,2,1,0:T(8,128)(2,1)S(1)} %copy-done.1), kind=kOutput, calls=%fused_computation.6 | convolution fusion | flops 1766195200 | bytes 11829248 | tf_op jit(solution)/shard_map/erf,efcd->cerd/dot_general | solution.py:86
  187.3 8.0 %copy.65 = bf16[8,2,896,320]{2,3,1,0:T(8,128)(2,1)} copy(bf16[8,2,896,320]{2,3,0,1:T(8,128)(2,1)} %convert_bitcast_fusion) | data formatting | bytes 18350080 | tf_op jit(solution)/shard_map/convert_element_type | solution.py:88
  195.3 0.0 all-to-all-done.5
  195.3 7.2 %all-to-all-start.2 = ((bf16[8,2,896,320]{2,3,1,0:T(8,128)(2,1)}), bf16[8,2,896,320]{2,3,1,0:T(8,128)(2,1)}, u32[]{:S(2)}, u32[]{:S(2)}) async-start(bf16[8,2,896,320]{2,3,1,0:T(8,128)(2,1)} %copy.65), calls=%async_computation.2 | async-start | bytes 18350080 | tf_op jit(solution)/shard_map/all_to_all | solution.py:89
  202.6 0.0 copy-done
  202.6 0.0 copy-start.6
  202.6 2.0 gather_fusion
  204.6 0.0 copy-done.6
  204.6 0.6 gather_fusion.1
  205.2 3.1 multiply_bitcast_fusion
  208.3 95.9 %all-to-all-done.2 = bf16[8,2,896,320]{2,3,1,0:T(8,128)(2,1)} async-done(((bf16[8,2,896,320]{2,3,1,0:T(8,128)(2,1)}), bf16[8,2,896,320]{2,3,1,0:T(8,128)(2,1)}, u32[]{:S(2)}, u32[]{:S(2)}) %all-to-all-start.2) | async-done | bytes 9175072 | tf_op jit(solution)/shard_map/all_to_all | solution.py:89
  304.3 5.0 %all-to-all-start.4 = ((bf16[4,8,32,1024]{3,2,0,1:T(8,128)(2,1)}), bf16[4,8,32,1024]{3,2,0,1:T(8,128)(2,1)}, u32[]{:S(2)}, u32[]{:S(2)}) async-start(bf16[4,8,32,1024]{3,2,0,1:T(8,128)(2,1)} %multiply_bitcast_fusion), calls=%async_computation.4 | async-start | bytes 4194304 | tf_op jit(solution)/shard_map/all_to_all | solution.py:34
  309.3 6.2 %reduce_sum.42 = bf16[2,896,320]{1,2,0:T(8,128)(2,1)} reduce(bf16[8,2,896,320]{2,3,1,0:T(8,128)(2,1)} %all-to-all-done.2, bf16[]{:T(256)} %constant.97.clone.1), dimensions={0}, to_apply=%region_5.6 | reduce | flops 4014080 | bytes 10321922 | tf_op jit(solution)/shard_map/reduce_sum | solution.py:90
  315.5 1.8 copy.67
  317.3 0.0 copy-start.3
  317.3 1.5 copy.68
  318.8 16.9 %all-to-all-done.4 = bf16[4,8,32,1024]{3,2,0,1:T(8,128)(2,1)} async-done(((bf16[4,8,32,1024]{3,2,0,1:T(8,128)(2,1)}), bf16[4,8,32,1024]{3,2,0,1:T(8,128)(2,1)}, u32[]{:S(2)}, u32[]{:S(2)}) %all-to-all-start.4) | async-done | bytes 2097184 | tf_op jit(solution)/shard_map/all_to_all | solution.py:34
  335.7 5.5 %all-to-all-start.3 = ((bf16[56,32,320]{2,0,1:T(8,128)(2,1)}), bf16[56,32,320]{2,0,1:T(8,128)(2,1)S(1)}, u32[]{:S(2)}, u32[]{:S(2)}) async-start(bf16[56,32,320]{2,0,1:T(8,128)(2,1)} %copy.68), calls=%async_computation.3 | async-start | bytes 2752512 | tf_op jit(solution)/shard_map/all_to_all | solution.py:92
  341.2 0.0 copy-done.3
  341.2 3.0 select_reduce_fusion
  344.2 0.2 reduce.1
  344.4 1.0 sort.32
  345.4 3.2 copy.71
  348.6 3.6 gather_fusion.3
  352.2 3.2 copy.72
  355.4 19.2 %all-to-all-done.3 = bf16[56,32,320]{2,0,1:T(8,128)(2,1)S(1)} async-done(((bf16[56,32,320]{2,0,1:T(8,128)(2,1)}), bf16[56,32,320]{2,0,1:T(8,128)(2,1)S(1)}, u32[]{:S(2)}, u32[]{:S(2)}) %all-to-all-start.3) | async-done | bytes 1146912 | tf_op jit(solution)/shard_map/all_to_all | solution.py:92
  374.6 0.0 copy-start.2
  374.6 0.2 copy.69
  374.8 1.0 copy-done.2
  375.8 1.3 convolution_convert_fusion.1
  (10 shorter events, 0.1 us)
Async XLA Ops:
  0.6 201.9 %copy-start = (bf16[4,8,32,1024]{3,2,1,0:T(8,128)(2,1)S(1)}, bf16[4,8,32,1024]{3,2,1,0:T(8,128)(2,1)}, u32[]{:S(2)}) copy-start(bf16[4,8,32,1024]{3,2,1,0:T(8,128)(2,1)} %param.17) | copy-start | bytes 6291460
  53.9 108.9 %all-to-all-start.1 = ((bf16[8,7,32,2560]{3,2,1,0:T(8,128)(2,1)}), bf16[8,7,32,2560]{3,2,1,0:T(8,128)(2,1)}, u32[]{:S(2)}, u32[]{:S(2)}) async-start(bf16[8,7,32,2560]{3,2,1,0:T(8,128)(2,1)} %broadcast_in_dim.36), calls=%async_computation.1 | async-start | bytes 18350080 | tf_op jit(solution)/shard_map/all_to_all | solution.py:78
  60.7 4.7 %copy-start.5 = (s32[8]{0:T(128)S(1)}, s32[8]{0:T(128)}, u32[]{:S(2)}) copy-start(s32[8]{0:T(128)} %param.18) | copy-start | bytes 100
  162.8 32.5 %all-to-all-start.5 = ((s32[8,1,1]{2,1,0:T(1,128)}), s32[8,1,1]{2,1,0:T(1,128)S(1)}, u32[]{:S(2)}, u32[]{:S(2)}) async-start(s32[8,1,1]{2,1,0:T(1,128)} %copy.70), calls=%async_computation.5 | async-start | bytes 8192 | tf_op jit(solution)/shard_map/all_to_all | solution.py:35
  167.9 7.3 %copy-start.4 = (bf16[2,2560,192]{1,2,0:T(8,128)(2,1)S(1)}, bf16[2,2560,192]{1,2,0:T(8,128)(2,1)}, u32[]{:S(2)}) copy-start(bf16[2,2560,192]{1,2,0:T(8,128)(2,1)} %param.15) | copy-start | bytes 5898244
  175.2 6.8 %copy-start.1 = (bf16[2,192,8,320]{3,2,1,0:T(8,128)(2,1)S(1)}, bf16[2,192,8,320]{3,2,1,0:T(8,128)(2,1)}, u32[]{:S(2)}) copy-start(bf16[2,192,8,320]{3,2,1,0:T(8,128)(2,1)} %reshape.39) | copy-start | bytes 5898244
  195.3 108.9 %all-to-all-start.2 = ((bf16[8,2,896,320]{2,3,1,0:T(8,128)(2,1)}), bf16[8,2,896,320]{2,3,1,0:T(8,128)(2,1)}, u32[]{:S(2)}, u32[]{:S(2)}) async-start(bf16[8,2,896,320]{2,3,1,0:T(8,128)(2,1)} %copy.65), calls=%async_computation.2 | async-start | bytes 18350080 | tf_op jit(solution)/shard_map/all_to_all | solution.py:89
  202.6 2.0 copy-start.6
  304.3 31.5 %all-to-all-start.4 = ((bf16[4,8,32,1024]{3,2,0,1:T(8,128)(2,1)}), bf16[4,8,32,1024]{3,2,0,1:T(8,128)(2,1)}, u32[]{:S(2)}, u32[]{:S(2)}) async-start(bf16[4,8,32,1024]{3,2,0,1:T(8,128)(2,1)} %multiply_bitcast_fusion), calls=%async_computation.4 | async-start | bytes 4194304 | tf_op jit(solution)/shard_map/all_to_all | solution.py:34
  317.3 23.9 %copy-start.3 = (bf16[256,6]{0,1:T(8,128)(2,1)S(1)}, bf16[256,6]{0,1:T(8,128)(2,1)}, u32[]{:S(2)}) copy-start(bf16[256,6]{0,1:T(8,128)(2,1)} %param.13) | copy-start | bytes 9220
  335.7 38.9 %all-to-all-start.3 = ((bf16[56,32,320]{2,0,1:T(8,128)(2,1)}), bf16[56,32,320]{2,0,1:T(8,128)(2,1)S(1)}, u32[]{:S(2)}, u32[]{:S(2)}) async-start(bf16[56,32,320]{2,0,1:T(8,128)(2,1)} %copy.68), calls=%async_computation.3 | async-start | bytes 2752512 | tf_op jit(solution)/shard_map/all_to_all | solution.py:92
  374.6 1.2 copy-start.2

commit v3 on v2

--- a/solution.py
+++ b/solution.py
@@ -22,15 +22,17 @@
     return picked.astype(jnp.int32)
 
 
-def relayout(kv_prefill, block_map, block_empty):
+def relayout_outgoing(kv_prefill, block_map, block_empty):
     layers, blocks, block_rows, kv_width = kv_prefill.shape
     exp_count = lax.axis_size("exp")
     keep = (1 - block_empty).astype(kv_prefill.dtype)
     peer = block_map // blocks // exp_count
     target = block_map % blocks
     order = jnp.argsort(peer)
-    outgoing = kv_prefill[:, order] * keep[order][None, :, None, None]
-    labels = target[order]
+    return kv_prefill[:, order] * keep[order][None, :, None, None], target[order]
+
+
+def relayout_exchange(outgoing, labels):
     arrived = lax.all_to_all(outgoing, "seq", split_axis=1, concat_axis=1, tiled=True)
     slots = lax.all_to_all(labels, "seq", split_axis=0, concat_axis=0, tiled=True)
     return arrived[:, jnp.argsort(slots)]
@@ -76,6 +78,8 @@
     arrived = lax.all_to_all(outgoing, "exp", split_axis=1, concat_axis=1, tiled=True)
     copies = jnp.broadcast_to(arrived[None], (seq_count,) + arrived.shape)
     gathered = lax.all_to_all(copies, "seq", split_axis=0, concat_axis=0, tiled=True)
+    kv_out, kv_labels = relayout_outgoing(kv_prefill, block_map, block_empty)
+    gathered, kv_out, kv_labels = lax.optimization_barrier((gathered, kv_out, kv_labels))
     rows = gathered.reshape(local_experts, seq_per_expert * per_dev * exp_count, width)
 
     gate = jnp.einsum("erd,edf->erf", rows, w_gate, preferred_element_type=jnp.float32)
@@ -86,6 +90,8 @@
     partial_value = jnp.einsum(
         "erf,efcd->cerd", hidden, down, preferred_element_type=jnp.float32
     ).astype(jnp.bfloat16)
+    kv_decode = relayout_exchange(kv_out, kv_labels)
+    kv_decode, partial_value = lax.optimization_barrier((kv_decode, partial_value))
     pieces = lax.all_to_all(partial_value, "seq", split_axis=0, concat_axis=0, tiled=True)
     summed = jnp.sum(pieces.astype(jnp.float32), axis=0).astype(jnp.bfloat16)
     summed = summed.reshape(seq_count * per_dev, exp_count, part_width)
@@ -101,7 +107,6 @@
     ).astype(jnp.bfloat16)
     mixed = jnp.dot(mix, returned, preferred_element_type=jnp.float32).astype(jnp.bfloat16)
 
-    kv_decode = relayout(kv_prefill, block_map, block_empty)
     return (mixed, kv_decode)
 
 

time: 382 us -> 386 us (1.010)
  blocking collectives: 41.1 us -> 149 us
  waiting for transfers between devices: 227 us -> 130 us
  starting transfers between devices: 29.6 us -> 25.2 us
    all_to_all x0 -> x1, blocking collectives: none -> 108 us  [per_device(): lax.all_to_all(partial_value, 'seq', split_axis=0, concat_axis=0, tiled=T...]
    all_to_all x3 -> x2, waiting for transfers between devices: 113 us -> 11.5 us  [the longest x1 11.5 us: relayout_exchange(): lax.all_to_all(outgoing, 'seq', split_axis=1, concat_axis=1, tiled=True)]
    convert_element_type x1 -> x0, local copies, waits for them, and re-layouts: 8.04 us -> none  [per_device(): partial_value = jnp.einsum('erf,efcd->cerd', hidden, down, preferred_elem...]
    optimization_barrier x0 -> x1, local copies, waits for them, and re-layouts: none -> 8.04 us  [per_device(): lax.optimization_barrier((kv_decode, partial_value))]
    all_to_all x1, waiting for transfers between devices: 19.2 us -> 27 us  [per_device(): lax.all_to_all(summed, 'exp', split_axis=1, concat_axis=1, tiled=True)]
    all_to_all x3 -> x2, starting transfers between devices: 17.3 us -> 12.2 us  [the longest x1 7.22 us: relayout_exchange(): lax.all_to_all(outgoing, 'seq', split_axis=1, concat_axis=1, tiled=True)]
  transfers between devices with their start and end apart: 5 -> 4, of which waited for: 4 -> 3; matrix products, arithmetic and copies ran while one was open for 17% -> 10% of each run, Pallas kernels for 0% -> 0%
where the time goes in v3:
time: 386 us; the launch traced here: 379 us
  blocking collectives  149 us (39%)
  waiting for transfers between devices  130 us (34%)
  local copies, waits for them, and re-layouts  34.7 us (9%)
  starting transfers between devices  25.2 us (7%)
  matrix products  23.2 us (6%)
  other arithmetic  16.2 us (4%)
    all_to_all x1, blocking collectives, per_device(): lax.all_to_all(partial_value, 'seq', split_axis=0, concat_axis=0, tiled=T...  108 us
    all_to_all x1, waiting for transfers between devices, per_device(): lax.all_to_all(copies, 'seq', split_axis=0, concat_axis=0, tiled=True)  91.4 us
    all_to_all x1, blocking collectives, per_device(): lax.all_to_all(outgoing, 'exp', split_axis=1, concat_axis=1, tiled=True)  41.1 us
    all_to_all x1, waiting for transfers between devices, per_device(): lax.all_to_all(summed, 'exp', split_axis=1, concat_axis=1, tiled=True)  27 us
    all_to_all x1, waiting for transfers between devices, relayout_exchange(): lax.all_to_all(outgoing, 'seq', split_axis=1, concat_axis=1, tiled=True)  11.5 us
    optimization_barrier x1, local copies, waits for them, and re-layouts, per_device(): lax.optimization_barrier((kv_decode, partial_value))  8.04 us
  transfers between devices with their start and end apart: 4, of which 3 were waited for; matrix products, arithmetic and copies ran while one was open for 10% of the time, Pallas kernels for 0%

profile of v3, /device:TPU:120, one launch (start us, length us, event | category | flops | bytes accessed | tf_op | source)
XLA Modules:
  0.0 379.4 jit_solution(11186940651239439623)
XLA Ops:
  0.6 0.0 copy-start
  0.6 0.9 fusion.11
  1.6 0.2 fusion.12
  1.7 0.8 select_reduce_fusion.1
  2.5 0.7 multiply_add_fusion
  3.2 0.2 fusion.4
  3.4 1.7 fusion
  5.1 1.9 convolution_convert_fusion
  7.0 0.6 copy.62
  7.6 41.1 %all_to_all.37 = bf16[7,32,2560]{2,0,1:T(8,128)(2,1)S(1)} all-to-all(bf16[7,32,2560]{2,0,1:T(8,128)(2,1)S(1)} %copy.62), channel_id=1, replica_groups=mesh['seq'=8,'exp'=32] {'exp'}, dimensions={1} | all-to-all | bytes 2293760 | tf_op jit(solution)/shard_map/all_to_all | solution.py:78
  48.8 0.4 copy.63
  49.2 4.7 %broadcast_in_dim.32 = bf16[8,7,32,2560]{3,2,1,0:T(8,128)(2,1)} broadcast(bf16[7,32,2560]{2,1,0:T(8,128)(2,1)S(1)} %copy.63), dimensions={1,2,3} | broadcast | bytes 10321920 | tf_op jit(solution)/shard_map/broadcast_in_dim | solution.py:79
  53.9 0.0 copy-start.6
  53.9 7.0 %all-to-all-start.1 = ((bf16[8,7,32,2560]{3,2,1,0:T(8,128)(2,1)}), bf16[8,7,32,2560]{3,2,1,0:T(8,128)(2,1)}, u32[]{:S(2)}, u32[]{:S(2)}) async-start(bf16[8,7,32,2560]{3,2,1,0:T(8,128)(2,1)} %broadcast_in_dim.32), calls=%async_computation.1 | async-start | bytes 18350080 | tf_op jit(solution)/shard_map/all_to_all | solution.py:80
  60.9 0.0 copy-done.6
  60.9 1.0 sort.31
  61.9 0.0 copy-done
  61.9 0.0 copy-start.7
  61.9 2.0 gather_fusion
  63.9 0.0 copy-done.7
  63.9 0.6 gather_fusion.1
  64.6 0.6 gather_fusion.2
  65.2 0.0 copy-start.3
  65.2 4.8 %reshape.39 = bf16[2,192,8,320]{3,2,1,0:T(8,128)(2,1)} reshape(bf16[2,192,2560]{2,1,0:T(8,128)(2,1)} %param.16) | data formatting | bytes 3932160 | tf_op jit(solution)/shard_map/reshape | solution.py:89
  70.0 0.0 copy-done.3
  70.0 1.5 multiply_bitcast_fusion
  71.6 91.4 %all-to-all-done.1 = bf16[8,7,32,2560]{3,2,1,0:T(8,128)(2,1)} async-done(((bf16[8,7,32,2560]{3,2,1,0:T(8,128)(2,1)}), bf16[8,7,32,2560]{3,2,1,0:T(8,128)(2,1)}, u32[]{:S(2)}, u32[]{:S(2)}) %all-to-all-start.1) | async-done | bytes 9175072 | tf_op jit(solution)/shard_map/all_to_all | solution.py:80
  163.0 0.7 copy.64
  163.6 5.0 %all-to-all-start.3 = ((s32[8,1,1]{2,1,0:T(1,128)}), s32[8,1,1]{2,1,0:T(1,128)S(1)}, u32[]{:S(2)}, u32[]{:S(2)}) async-start(s32[8,1,1]{2,1,0:T(1,128)} %copy.64), calls=%async_computation.3 | async-start | bytes 8192 | tf_op jit(solution)/shard_map/all_to_all | solution.py:37
  168.7 7.1 %fusion.19 = f32[2,896,192]{1,2,0:T(8,128)S(1)} fusion(bf16[2,896,2560]{2,1,0:T(8,128)(2,1)} %bitcast.4, bf16[2,2560,192]{1,2,0:T(8,128)(2,1)} %param.14), kind=kOutput, calls=%fused_computation.62 | convolution fusion | flops 1761607680 | bytes 12517376 | tf_op jit(solution)/shard_map/erd,edf->erf/dot_general | solution.py:85
  175.8 0.0 all-to-all-done.3
  175.8 7.2 %all-to-all-start.2 = ((bf16[4,8,32,1024]{3,2,0,1:T(8,128)(2,1)}), bf16[4,8,32,1024]{3,2,0,1:T(8,128)(2,1)S(1)}, u32[]{:S(2)}, u32[]{:S(2)}) async-start(bf16[4,8,32,1024]{3,2,0,1:T(8,128)(2,1)} %multiply_bitcast_fusion), calls=%async_computation.2 | async-start | bytes 4194304 | tf_op jit(solution)/shard_map/all_to_all | solution.py:36
  183.0 0.0 copy-start.2
  183.1 7.3 %fusion.9 = bf16[2,896,192,1]{1,2,3,0:T(8,128)(2,1)S(1)} fusion(bf16[2,896,2560]{2,1,0:T(8,128)(2,1)} %bitcast.4, bf16[2,2560,192]{1,2,0:T(8,128)(2,1)} %param.15, f32[2,896,192]{1,2,0:T(8,128)S(1)} %fusion.19), kind=kOutput, calls=%fused_computation.21 | convolution fusion | flops 1763672064 | bytes 13205504 | tf_op jit(solution)/shard_map/erd,edf->erf/dot_general | solution.py:86
  190.4 0.0 copy-done.2
  190.4 5.3 %convert_bitcast_fusion = bf16[8,2,896,320]{2,3,0,1:T(8,128)(2,1)} fusion(bf16[2,896,192,1]{1,2,3,0:T(8,128)(2,1)S(1)} %fusion.9, bf16[2,192,8,320]{3,2,1,0:T(8,128)(2,1)S(1)} %copy-done.2), kind=kOutput, calls=%fused_computation.6 | convolution fusion | flops 1766195200 | bytes 11829248 | tf_op jit(solution)/shard_map/erf,efcd->cerd/dot_general | solution.py:90
  195.7 0.2 reduce.1
  196.0 1.0 sort.32
  196.9 11.5 %all-to-all-done.2 = bf16[4,8,32,1024]{3,2,0,1:T(8,128)(2,1)S(1)} async-done(((bf16[4,8,32,1024]{3,2,0,1:T(8,128)(2,1)}), bf16[4,8,32,1024]{3,2,0,1:T(8,128)(2,1)S(1)}, u32[]{:S(2)}, u32[]{:S(2)}) %all-to-all-start.2) | async-done | bytes 2097184 | tf_op jit(solution)/shard_map/all_to_all | solution.py:36
  208.5 1.6 copy.65
  210.1 3.6 gather_fusion.3
  213.7 8.0 %copy.67 = bf16[8,2,896,320]{2,3,1,0:T(8,128)(2,1)} copy(bf16[8,2,896,320]{2,3,0,1:T(8,128)(2,1)} %convert_bitcast_fusion) | data formatting | bytes 18350080 | tf_op jit(solution)/shard_map/optimization_barrier | solution.py:94
  221.7 108.2 %all_to_all.38 = bf16[8,2,896,320]{2,3,1,0:T(8,128)(2,1)} all-to-all(bf16[8,2,896,320]{2,3,1,0:T(8,128)(2,1)} %copy.67), channel_id=1, replica_groups=mesh['seq'=8,'exp'=32] {'seq'}, dimensions={0} | all-to-all | bytes 18350080 | tf_op jit(solution)/shard_map/all_to_all | solution.py:95
  329.9 5.2 %reduce_sum.42 = bf16[2,896,320]{1,2,0:T(8,128)(2,1)S(1)} reduce(bf16[8,2,896,320]{2,3,1,0:T(8,128)(2,1)} %all_to_all.38, bf16[]{:T(256)} %constant.101.clone.1), dimensions={0}, to_apply=%region_7.8 | reduce | flops 4014080 | bytes 10321922 | tf_op jit(solution)/shard_map/reduce_sum | solution.py:96
  335.1 0.8 copy.69
  336.0 0.0 copy-start.5
  336.0 1.6 copy.70
  337.5 6.0 %all-to-all-start.5 = ((bf16[56,32,320]{2,0,1:T(8,128)(2,1)}), bf16[56,32,320]{2,0,1:T(8,128)(2,1)S(1)}, u32[]{:S(2)}, u32[]{:S(2)}) async-start(bf16[56,32,320]{2,0,1:T(8,128)(2,1)} %copy.70), calls=%async_computation.5 | async-start | bytes 2752512 | tf_op jit(solution)/shard_map/all_to_all | solution.py:98
  343.5 0.0 copy-done.5
  343.6 3.0 select_reduce_fusion
  346.5 0.0 copy-start.1
  346.5 3.3 copy.72
  349.9 27.0 %all-to-all-done.5 = bf16[56,32,320]{2,0,1:T(8,128)(2,1)S(1)} async-done(((bf16[56,32,320]{2,0,1:T(8,128)(2,1)}), bf16[56,32,320]{2,0,1:T(8,128)(2,1)S(1)}, u32[]{:S(2)}, u32[]{:S(2)}) %all-to-all-start.5) | async-done | bytes 1146912 | tf_op jit(solution)/shard_map/all_to_all | solution.py:98
  376.9 0.0 copy-start.4
  376.9 0.2 copy.71
  377.1 1.0 copy-done.4
  378.1 1.3 convolution_convert_fusion.1
  379.4 0.0 copy-done.1
  (10 shorter events, 0.1 us)
Async XLA Ops:
  0.6 61.3 %copy-start = (bf16[4,8,32,1024]{3,2,1,0:T(8,128)(2,1)S(1)}, bf16[4,8,32,1024]{3,2,1,0:T(8,128)(2,1)}, u32[]{:S(2)}) copy-start(bf16[4,8,32,1024]{3,2,1,0:T(8,128)(2,1)} %param.17) | copy-start | bytes 6291460
  53.9 7.0 %copy-start.6 = (s32[8]{0:T(128)S(1)}, s32[8]{0:T(128)}, u32[]{:S(2)}) copy-start(s32[8]{0:T(128)} %param.18) | copy-start | bytes 100
  53.9 109.1 %all-to-all-start.1 = ((bf16[8,7,32,2560]{3,2,1,0:T(8,128)(2,1)}), bf16[8,7,32,2560]{3,2,1,0:T(8,128)(2,1)}, u32[]{:S(2)}, u32[]{:S(2)}) async-start(bf16[8,7,32,2560]{3,2,1,0:T(8,128)(2,1)} %broadcast_in_dim.32), calls=%async_computation.1 | async-start | bytes 18350080 | tf_op jit(solution)/shard_map/all_to_all | solution.py:80
  61.9 2.0 copy-start.7
  65.2 4.8 %copy-start.3 = (bf16[8,4,32,1024]{3,2,1,0:T(8,128)(2,1)S(1)}, bf16[8,4,32,1024]{3,2,1,0:T(8,128)(2,1)}, u32[]{:S(2)}) copy-start(bf16[8,4,32,1024]{3,2,1,0:T(8,128)(2,1)} %gather_fusion) | copy-start | bytes 6291460
  163.6 12.2 %all-to-all-start.3 = ((s32[8,1,1]{2,1,0:T(1,128)}), s32[8,1,1]{2,1,0:T(1,128)S(1)}, u32[]{:S(2)}, u32[]{:S(2)}) async-start(s32[8,1,1]{2,1,0:T(1,128)} %copy.64), calls=%async_computation.3 | async-start | bytes 8192 | tf_op jit(solution)/shard_map/all_to_all | solution.py:37
  175.8 32.7 %all-to-all-start.2 = ((bf16[4,8,32,1024]{3,2,0,1:T(8,128)(2,1)}), bf16[4,8,32,1024]{3,2,0,1:T(8,128)(2,1)S(1)}, u32[]{:S(2)}, u32[]{:S(2)}) async-start(bf16[4,8,32,1024]{3,2,0,1:T(8,128)(2,1)} %multiply_bitcast_fusion), calls=%async_computation.2 | async-start | bytes 4194304 | tf_op jit(solution)/shard_map/all_to_all | solution.py:36
  183.0 7.3 %copy-start.2 = (bf16[2,192,8,320]{3,2,1,0:T(8,128)(2,1)S(1)}, bf16[2,192,8,320]{3,2,1,0:T(8,128)(2,1)}, u32[]{:S(2)}) copy-start(bf16[2,192,8,320]{3,2,1,0:T(8,128)(2,1)} %reshape.39) | copy-start | bytes 5898244
  336.0 7.6 %copy-start.5 = (bf16[256,6]{0,1:T(8,128)(2,1)S(1)}, bf16[256,6]{0,1:T(8,128)(2,1)}, u32[]{:S(2)}) copy-start(bf16[256,6]{0,1:T(8,128)(2,1)} %param.13) | copy-start | bytes 9220
  337.5 39.4 %all-to-all-start.5 = ((bf16[56,32,320]{2,0,1:T(8,128)(2,1)}), bf16[56,32,320]{2,0,1:T(8,128)(2,1)S(1)}, u32[]{:S(2)}, u32[]{:S(2)}) async-start(bf16[56,32,320]{2,0,1:T(8,128)(2,1)} %copy.70), calls=%async_computation.5 | async-start | bytes 2752512 | tf_op jit(solution)/shard_map/all_to_all | solution.py:98
  346.5 32.8 %copy-start.1 = (bf16[4,8,32,1024]{3,2,1,0:T(8,128)(2,1)S(1)}, bf16[4,8,32,1024]{3,2,1,0:T(8,128)(2,1)}, u32[]{:S(2)}) copy-start(bf16[4,8,32,1024]{3,2,1,0:T(8,128)(2,1)} %param.17) | copy-start | bytes 6291460
  376.9 1.2 copy-start.4

commit v4 on v3

--- a/solution.py
+++ b/solution.py
@@ -57,7 +57,8 @@
     tok_count, topk = routes.shape
     capacity = tok_count * topk // experts + 1
     seq_per_expert = seq_count // local_experts
-    per_dev = -(-capacity // seq_per_expert)
+    share = (capacity * 2) // (3 * seq_per_expert)
+    direct = capacity - share * seq_per_expert
     my_seq = lax.axis_index("seq")
 
     normed = rms_normed(tokens, norm_gain)
@@ -66,21 +67,38 @@
     position = route_positions(routes, experts)
     owner = routes // local_experts
     local_index = routes % local_experts
-    sender = local_index * seq_per_expert + position // per_dev
-    within = position % per_dev
+    shared = position >= direct
+    sender = local_index * seq_per_expert + (position - direct) // share
+    within = (position - direct) % share
 
-    send_slots = per_dev * exp_count
-    slot_of = jnp.where(sender == my_seq, within * exp_count + owner, -1)
-    slot_ids = jnp.arange(send_slots, dtype=jnp.int32)
-    pick = jnp.any(slot_of[None, :, :] == slot_ids[:, None, None], axis=2).astype(jnp.bfloat16)
-    outgoing = jnp.dot(pick, normed, preferred_element_type=jnp.float32).astype(jnp.bfloat16)
-    outgoing = outgoing.reshape(per_dev, exp_count, width)
-    arrived = lax.all_to_all(outgoing, "exp", split_axis=1, concat_axis=1, tiled=True)
-    copies = jnp.broadcast_to(arrived[None], (seq_count,) + arrived.shape)
-    gathered = lax.all_to_all(copies, "seq", split_axis=0, concat_axis=0, tiled=True)
+    direct_slots = local_experts * direct
+    direct_of = jnp.where(shared, -1, (local_index * direct + position) * exp_count + owner)
+    direct_ids = jnp.arange(direct_slots * exp_count, dtype=jnp.int32)
+    pick = jnp.any(direct_of[None, :, :] == direct_ids[:, None, None], axis=2).astype(jnp.bfloat16)
+    direct_rows = jnp.dot(pick, normed, preferred_element_type=jnp.float32).astype(jnp.bfloat16)
+    direct_rows = direct_rows.reshape(direct_slots, exp_count, width)
+
+    share_of = jnp.where(shared & (sender == my_seq), within * exp_count + owner, -1)
+    share_ids = jnp.arange(share * exp_count, dtype=jnp.int32)
+    pick = jnp.any(share_of[None, :, :] == share_ids[:, None, None], axis=2).astype(jnp.bfloat16)
+    share_rows = jnp.dot(pick, normed, preferred_element_type=jnp.float32).astype(jnp.bfloat16)
+    share_rows = share_rows.reshape(share, exp_count, width)
+
+    share_arrived = lax.all_to_all(share_rows, "exp", split_axis=1, concat_axis=1, tiled=True)
+    share_gathered = lax.all_gather(share_arrived, "seq", axis=0, tiled=False)
+    direct_arrived = lax.all_to_all(direct_rows, "exp", split_axis=1, concat_axis=1, tiled=True)
+
     kv_out, kv_labels = relayout_outgoing(kv_prefill, block_map, block_empty)
-    gathered, kv_out, kv_labels = lax.optimization_barrier((gathered, kv_out, kv_labels))
-    rows = gathered.reshape(local_experts, seq_per_expert * per_dev * exp_count, width)
+    share_gathered, direct_arrived, kv_out, kv_labels = lax.optimization_barrier(
+        (share_gathered, direct_arrived, kv_out, kv_labels)
+    )
+    share_gathered = share_gathered.reshape(
+        local_experts, seq_per_expert * share, exp_count, width
+    )
+    direct_arrived = direct_arrived.reshape(local_experts, direct, exp_count, width)
+    rows = jnp.concatenate([direct_arrived, share_gathered], axis=1).reshape(
+        local_experts, capacity * exp_count, width
+    )
 
     gate = jnp.einsum("erd,edf->erf", rows, w_gate, preferred_element_type=jnp.float32)
     upward = jnp.einsum("erd,edf->erf", rows, w_up, preferred_element_type=jnp.float32)
@@ -94,12 +112,12 @@
     kv_decode, partial_value = lax.optimization_barrier((kv_decode, partial_value))
     pieces = lax.all_to_all(partial_value, "seq", split_axis=0, concat_axis=0, tiled=True)
     summed = jnp.sum(pieces.astype(jnp.float32), axis=0).astype(jnp.bfloat16)
-    summed = summed.reshape(seq_count * per_dev, exp_count, part_width)
+    summed = summed.reshape(local_experts * capacity, exp_count, part_width)
     returned = lax.all_to_all(summed, "exp", split_axis=1, concat_axis=1, tiled=True)
-    recv_slots = seq_count * per_dev * exp_count
+    recv_slots = local_experts * capacity * exp_count
     returned = returned.reshape(recv_slots, part_width)
 
-    recv_slot = (sender * per_dev + within) * exp_count + owner
+    recv_slot = (local_index * capacity + position) * exp_count + owner
     recv_ids = jnp.arange(recv_slots, dtype=jnp.int32)
     weights = route_weights.astype(jnp.float32)
     mix = jnp.sum(

time: 386 us -> 403 us (1.044)
  blocking collectives: 149 us -> 135 us
  between operations: 0.81 us -> 14.2 us
  other arithmetic: 16.2 us -> 23.7 us
    all_gather x0 -> x1, waiting for transfers between devices: none -> 14.3 us  [per_device(): share_gathered = lax.all_gather(share_arrived, 'seq', axis=0, tiled=False)]
    all_to_all x1, blocking collectives: 41.1 us -> 26.9 us  [per_device(): lax.all_to_all(share_rows, 'exp', split_axis=1, concat_axis=1, tiled=True)]
    all_to_all x1, waiting for transfers between devices: 91.4 us -> 80 us  [per_device(): lax.all_to_all(direct_rows, 'exp', split_axis=1, concat_axis=1, tiled=True)]
    concatenate x0 -> x1, other arithmetic: none -> 7.38 us  [per_device(): jnp.concatenate([direct_arrived, share_gathered], axis=1)]
    broadcast_in_dim x1 -> x0, local copies, waits for them, and re-layouts: 4.71 us -> none  [per_device(): copies = jnp.broadcast_to(arrived[None], (seq_count,) + arrived.shape)]
    optimization_barrier x0 -> x1, local copies, waits for them, and re-layouts: none -> 4.55 us  [per_device(): lax.optimization_barrier((share_gathered, direct_arrived, kv_out, kv_labe...]
  transfers between devices with their start and end apart: 4 -> 5, of which waited for: 3 -> 4; matrix products, arithmetic and copies ran while one was open for 10% -> 13% of each run, Pallas kernels for 0% -> 0%
where the time goes in v4:
time: 403 us; the launch traced here: 397 us
  blocking collectives  135 us (33%)
  waiting for transfers between devices  133 us (33%)
  local copies, waits for them, and re-layouts  38.4 us (10%)
  starting transfers between devices  27.9 us (7%)
  matrix products  24.6 us (6%)
  other arithmetic  23.7 us (6%)
  between operations  14.2 us (4%)
    all_to_all x1, blocking collectives, per_device(): lax.all_to_all(partial_value, 'seq', split_axis=0, concat_axis=0, tiled=T...  108 us
    all_to_all x1, waiting for transfers between devices, per_device(): lax.all_to_all(direct_rows, 'exp', split_axis=1, concat_axis=1, tiled=True)  80 us
    all_to_all x1, waiting for transfers between devices, per_device(): lax.all_to_all(summed, 'exp', split_axis=1, concat_axis=1, tiled=True)  27.6 us
    all_to_all x1, blocking collectives, per_device(): lax.all_to_all(share_rows, 'exp', split_axis=1, concat_axis=1, tiled=True)  26.9 us
    all_gather x1, waiting for transfers between devices, per_device(): share_gathered = lax.all_gather(share_arrived, 'seq', axis=0, tiled=False)  14.3 us
    all_to_all x1, waiting for transfers between devices, relayout_exchange(): lax.all_to_all(outgoing, 'seq', split_axis=1, concat_axis=1, tiled=True)  11 us
  transfers between devices with their start and end apart: 5, of which 4 were waited for; matrix products, arithmetic and copies ran while one was open for 13% of the time, Pallas kernels for 0%

profile of v4, /device:TPU:120, one launch (start us, length us, event | category | flops | bytes accessed | tf_op | source)
XLA Modules:
  0.0 396.7 jit_solution(13146786569854127102)
XLA Ops:
  7.2 0.0 copy-start
  7.2 0.0 all-gather.3.cloned.1.call-start
  7.2 0.9 fusion.9
  8.1 0.2 fusion.12
  8.3 0.8 select_reduce_fusion.1
  9.1 1.7 fusion.1
  10.7 0.7 multiply_add_fusion
  11.5 0.1 fusion.8
  11.6 1.9 convolution_convert_fusion.1
  13.5 0.0 copy-start.4
  13.5 0.0 copy-start.6
  13.5 0.5 copy.71
  14.0 26.9 %all_to_all.37 = bf16[4,32,2560]{2,0,1:T(4,128)(2,1)S(1)} all-to-all(bf16[4,32,2560]{2,0,1:T(4,128)(2,1)S(1)} %copy.71), channel_id=1, replica_groups=mesh['seq'=8,'exp'=32] {'exp'}, dimensions={1} | all-to-all | bytes 1310720 | tf_op jit(solution)/shard_map/all_to_all | solution.py:87
  40.9 1.0 copy.72
  41.9 0.0 all-gather.3.cloned.1.call-update
  41.9 0.6 fusion
  42.5 0.0 copy-done.4
  42.5 0.0 copy-done.6
  42.5 1.1 convolution_convert_fusion
  43.6 3.5 copy.73
  47.1 7.3 %all-to-all-start.1 = ((bf16[18,32,2560]{2,0,1:T(8,128)(2,1)}), bf16[18,32,2560]{2,0,1:T(8,128)(2,1)}, u32[]{:S(2)}, u32[]{:S(2)}) async-start(bf16[18,32,2560]{2,0,1:T(8,128)(2,1)} %copy.73), calls=%async_computation.1 | async-start | bytes 7864320 | tf_op jit(solution)/shard_map/all_to_all | solution.py:89
  54.4 0.0 copy-done.9
  54.4 1.0 sort.31
  55.4 0.0 copy-done
  55.4 0.0 copy-start.10
  55.4 2.0 gather_fusion
  57.4 0.0 copy-done.10
  57.4 0.6 gather_fusion.1
  58.1 0.6 gather_fusion.2
  58.7 4.8 %reshape.51 = bf16[2,192,8,320]{3,2,1,0:T(8,128)(2,1)} reshape(bf16[2,192,2560]{2,1,0:T(8,128)(2,1)} %param.16) | data formatting | bytes 3932160 | tf_op jit(solution)/shard_map/reshape | solution.py:107
  63.6 0.0 copy-done.3
  63.6 1.5 multiply_bitcast_fusion
  65.1 80.0 %all-to-all-done.1 = bf16[18,32,2560]{2,0,1:T(8,128)(2,1)} async-done(((bf16[18,32,2560]{2,0,1:T(8,128)(2,1)}), bf16[18,32,2560]{2,0,1:T(8,128)(2,1)}, u32[]{:S(2)}, u32[]{:S(2)}) %all-to-all-start.1) | async-done | bytes 2949152 | tf_op jit(solution)/shard_map/all_to_all | solution.py:89
  145.1 14.3 %all-gather.3.cloned.1.call-done = bf16[32,32,2560]{2,1,0:T(8,128)(2,1)} async-done(((bf16[4,32,2560]{2,1,0:T(8,128)(2,1)}), bf16[32,32,2560]{2,1,0:T(8,128)(2,1)}) %all-gather.3.cloned.1.call-update) | async-done | bytes 5242896 | tf_op jit(solution)/shard_map/all_gather | solution.py:88
  159.4 4.6 %copy.76 = bf16[18,32,2560]{2,1,0:T(8,128)(2,1)} copy(bf16[18,32,2560]{2,0,1:T(8,128)(2,1)} %all-to-all-done.1) | data formatting | bytes 5898240 | tf_op jit(solution)/shard_map/optimization_barrier | solution.py:92
  164.0 0.7 copy.74
  164.6 5.6 %all-to-all-start.3 = ((s32[8,1,1]{2,1,0:T(1,128)}), s32[8,1,1]{2,1,0:T(1,128)S(1)}, u32[]{:S(2)}, u32[]{:S(2)}) async-start(s32[8,1,1]{2,1,0:T(1,128)} %copy.74), calls=%async_computation.3 | async-start | bytes 8192 | tf_op jit(solution)/shard_map/all_to_all | solution.py:37
  170.3 7.4 %pad_maximum_fusion = bf16[2,25,32,2560]{3,2,1,0:T(8,128)(2,1)} fusion(bf16[2,16,32,2560]{3,2,1,0:T(8,128)(2,1)} %bitcast.33, bf16[2,9,32,2560]{3,2,1,0:T(8,128)(2,1)} %bitcast.29), kind=kLoop, calls=%fused_computation.7 | loop fusion | flops 4096000 | bytes 16384000 | tf_op jit(solution)/shard_map/concatenate | solution.py:99
  177.7 0.0 copy-done.8
  177.7 7.5 %fusion.23 = f32[2,800,192]{1,2,0:T(8,128)} fusion(bf16[2,800,2560]{2,1,0:T(8,128)(2,1)} %bitcast.31, bf16[2,2560,192]{1,2,0:T(8,128)(2,1)S(1)} %copy-done.8), kind=kOutput, calls=%fused_computation.72 | convolution fusion | flops 1572864000 | bytes 11386880 | tf_op jit(solution)/shard_map/erd,edf->erf/dot_general | solution.py:103
  185.1 0.0 all-to-all-done.3
  185.2 7.2 %all-to-all-start.2 = ((bf16[4,8,32,1024]{3,2,0,1:T(8,128)(2,1)}), bf16[4,8,32,1024]{3,2,0,1:T(8,128)(2,1)S(1)}, u32[]{:S(2)}, u32[]{:S(2)}) async-start(bf16[4,8,32,1024]{3,2,0,1:T(8,128)(2,1)} %multiply_bitcast_fusion), calls=%async_computation.2 | async-start | bytes 4194304 | tf_op jit(solution)/shard_map/all_to_all | solution.py:36
  192.4 7.4 %fusion.6 = bf16[2,800,192,1]{1,2,3,0:T(8,128)(2,1)S(1)} fusion(bf16[2,800,2560]{2,1,0:T(8,128)(2,1)} %bitcast.32, bf16[2,2560,192]{1,2,0:T(8,128)(2,1)} %param.15, f32[2,800,192]{1,2,0:T(8,128)} %fusion.23), kind=kOutput, calls=%fused_computation.21 | convolution fusion | flops 1574707200 | bytes 12001280 | tf_op jit(solution)/shard_map/erd,edf->erf/dot_general | solution.py:104
  199.8 0.0 copy-done.2
  199.8 5.3 %convert_bitcast_fusion = bf16[8,2,800,320]{2,3,0,1:T(8,128)(2,1)} fusion(bf16[2,800,192,1]{1,2,3,0:T(8,128)(2,1)S(1)} %fusion.6, bf16[2,192,8,320]{3,2,1,0:T(8,128)(2,1)S(1)} %copy-done.2), kind=kOutput, calls=%fused_computation.6 | convolution fusion | flops 1576960000 | bytes 10772480 | tf_op jit(solution)/shard_map/erf,efcd->cerd/dot_general | solution.py:108
  205.1 0.2 reduce.1
  205.4 1.0 sort.32
  206.4 11.0 %all-to-all-done.2 = bf16[4,8,32,1024]{3,2,0,1:T(8,128)(2,1)S(1)} async-done(((bf16[4,8,32,1024]{3,2,0,1:T(8,128)(2,1)}), bf16[4,8,32,1024]{3,2,0,1:T(8,128)(2,1)S(1)}, u32[]{:S(2)}, u32[]{:S(2)}) %all-to-all-start.2) | async-done | bytes 2097184 | tf_op jit(solution)/shard_map/all_to_all | solution.py:36
  217.3 1.6 copy.75
  218.9 3.6 gather_fusion.3
  222.5 8.0 %copy.78 = bf16[8,2,800,320]{2,3,1,0:T(8,128)(2,1)} copy(bf16[8,2,800,320]{2,3,0,1:T(8,128)(2,1)} %convert_bitcast_fusion) | data formatting | bytes 16384000 | tf_op jit(solution)/shard_map/optimization_barrier | solution.py:112
  230.6 108.2 %all_to_all.38 = bf16[8,2,800,320]{2,3,1,0:T(8,128)(2,1)} all-to-all(bf16[8,2,800,320]{2,3,1,0:T(8,128)(2,1)} %copy.78), channel_id=1, replica_groups=mesh['seq'=8,'exp'=32] {'seq'}, dimensions={0} | all-to-all | bytes 16384000 | tf_op jit(solution)/shard_map/all_to_all | solution.py:113
  338.7 5.3 %reduce_sum.42 = bf16[2,800,320]{1,2,0:T(8,128)(2,1)S(1)} reduce(bf16[8,2,800,320]{2,3,1,0:T(8,128)(2,1)} %all_to_all.38, bf16[]{:T(256)} %constant.112.clone.1), dimensions={0}, to_apply=%region_8.9 | reduce | flops 3584000 | bytes 9216002 | tf_op jit(solution)/shard_map/reduce_sum | solution.py:114
  344.1 0.8 copy.80
  344.9 0.0 copy-start.7
  344.9 1.5 copy.81
  346.4 7.7 %all-to-all-start.5 = ((bf16[50,32,320]{2,0,1:T(8,128)(2,1)}), bf16[50,32,320]{2,0,1:T(8,128)(2,1)S(1)}, u32[]{:S(2)}, u32[]{:S(2)}) async-start(bf16[50,32,320]{2,0,1:T(8,128)(2,1)} %copy.81), calls=%async_computation.5 | async-start | bytes 2752512 | tf_op jit(solution)/shard_map/all_to_all | solution.py:116
  354.1 2.4 select_reduce_fusion
  356.6 3.3 copy.83
  359.9 27.6 %all-to-all-done.5 = bf16[50,32,320]{2,0,1:T(8,128)(2,1)S(1)} async-done(((bf16[50,32,320]{2,0,1:T(8,128)(2,1)}), bf16[50,32,320]{2,0,1:T(8,128)(2,1)S(1)}, u32[]{:S(2)}, u32[]{:S(2)}) %all-to-all-start.5) | async-done | bytes 1024032 | tf_op jit(solution)/shard_map/all_to_all | solution.py:116
  387.4 0.2 copy.82
  387.6 1.0 copy-done.5
  388.6 1.3 convolution_convert_fusion.2
  389.9 0.0 copy-done.1
  (17 shorter events, 0.1 us)
Async XLA Ops:
  7.2 48.3 %copy-start = (bf16[4,8,32,1024]{3,2,1,0:T(8,128)(2,1)S(1)}, bf16[4,8,32,1024]{3,2,1,0:T(8,128)(2,1)}, u32[]{:S(2)}) copy-start(bf16[4,8,32,1024]{3,2,1,0:T(8,128)(2,1)} %param.17) | copy-start | bytes 6291460
  7.2 152.2 %all-gather.3.cloned.1.call-start = ((), (), s32[]{:S(2)}) async-start(), calls=%async_computation.6 | async-start | bytes 5898240 | tf_op jit(solution)/shard_map/all_gather | solution.py:88
  13.5 29.0 %copy-start.4 = (bf16[256,2560]{1,0:T(8,128)(2,1)S(1)}, bf16[256,2560]{1,0:T(8,128)(2,1)}, u32[]{:S(2)}) copy-start(bf16[256,2560]{1,0:T(8,128)(2,1)} %param.10) | copy-start | bytes 3932164
  13.5 29.0 %copy-start.6 = (f32[2560]{0:T(1024)S(1)}, f32[2560]{0:T(1024)}, u32[]{:S(2)}) copy-start(f32[2560]{0:T(1024)} %param.11) | copy-start | bytes 30724
  47.1 7.3 %copy-start.9 = (s32[8]{0:T(128)S(1)}, s32[8]{0:T(128)}, u32[]{:S(2)}) copy-start(s32[8]{0:T(128)} %param.18) | copy-start | bytes 100
  47.1 98.0 %all-to-all-start.1 = ((bf16[18,32,2560]{2,0,1:T(8,128)(2,1)}), bf16[18,32,2560]{2,0,1:T(8,128)(2,1)}, u32[]{:S(2)}, u32[]{:S(2)}) async-start(bf16[18,32,2560]{2,0,1:T(8,128)(2,1)} %copy.73), calls=%async_computation.1 | async-start | bytes 7864320 | tf_op jit(solution)/shard_map/all_to_all | solution.py:89
  55.4 2.0 copy-start.10
  58.7 4.8 %copy-start.3 = (bf16[8,4,32,1024]{3,2,1,0:T(8,128)(2,1)S(1)}, bf16[8,4,32,1024]{3,2,1,0:T(8,128)(2,1)}, u32[]{:S(2)}) copy-start(bf16[8,4,32,1024]{3,2,1,0:T(8,128)(2,1)} %gather_fusion) | copy-start | bytes 6291460
  164.6 20.5 %all-to-all-start.3 = ((s32[8,1,1]{2,1,0:T(1,128)}), s32[8,1,1]{2,1,0:T(1,128)S(1)}, u32[]{:S(2)}, u32[]{:S(2)}) async-start(s32[8,1,1]{2,1,0:T(1,128)} %copy.74), calls=%async_computation.3 | async-start | bytes 8192 | tf_op jit(solution)/shard_map/all_to_all | solution.py:37
  170.3 7.4 %copy-start.8 = (bf16[2,2560,192]{1,2,0:T(8,128)(2,1)S(1)}, bf16[2,2560,192]{1,2,0:T(8,128)(2,1)}, u32[]{:S(2)}) copy-start(bf16[2,2560,192]{1,2,0:T(8,128)(2,1)} %param.14) | copy-start | bytes 5898244
  185.2 32.2 %all-to-all-start.2 = ((bf16[4,8,32,1024]{3,2,0,1:T(8,128)(2,1)}), bf16[4,8,32,1024]{3,2,0,1:T(8,128)(2,1)S(1)}, u32[]{:S(2)}, u32[]{:S(2)}) async-start(bf16[4,8,32,1024]{3,2,0,1:T(8,128)(2,1)} %multiply_bitcast_fusion), calls=%async_computation.2 | async-start | bytes 4194304 | tf_op jit(solution)/shard_map/all_to_all | solution.py:36
  192.4 7.4 %copy-start.2 = (bf16[2,192,8,320]{3,2,1,0:T(8,128)(2,1)S(1)}, bf16[2,192,8,320]{3,2,1,0:T(8,128)(2,1)}, u32[]{:S(2)}) copy-start(bf16[2,192,8,320]{3,2,1,0:T(8,128)(2,1)} %reshape.51) | copy-start | bytes 5898244
  344.9 9.3 %copy-start.7 = (bf16[256,6]{0,1:T(8,128)(2,1)S(1)}, bf16[256,6]{0,1:T(8,128)(2,1)}, u32[]{:S(2)}) copy-start(bf16[256,6]{0,1:T(8,128)(2,1)} %param.13) | copy-start | bytes 9220
  346.4 41.1 %all-to-all-start.5 = ((bf16[50,32,320]{2,0,1:T(8,128)(2,1)}), bf16[50,32,320]{2,0,1:T(8,128)(2,1)S(1)}, u32[]{:S(2)}, u32[]{:S(2)}) async-start(bf16[50,32,320]{2,0,1:T(8,128)(2,1)} %copy.81), calls=%async_computation.5 | async-start | bytes 2752512 | tf_op jit(solution)/shard_map/all_to_all | solution.py:116
  356.6 33.3 %copy-start.1 = (bf16[4,8,32,1024]{3,2,1,0:T(8,128)(2,1)S(1)}, bf16[4,8,32,1024]{3,2,1,0:T(8,128)(2,1)}, u32[]{:S(2)}) copy-start(bf16[4,8,32,1024]{3,2,1,0:T(8,128)(2,1)} %param.17) | copy-start | bytes 6291460
  387.4 1.1 copy-start.5
Sparse Core Ops, SparseCore 0:
  42.0 117.3 all-gather.2

commit v5 on v2

--- a/solution.py
+++ b/solution.py
@@ -55,7 +55,8 @@
     tok_count, topk = routes.shape
     capacity = tok_count * topk // experts + 1
     seq_per_expert = seq_count // local_experts
-    per_dev = -(-capacity // seq_per_expert)
+    share = capacity // seq_per_expert
+    direct = capacity - share * seq_per_expert
     my_seq = lax.axis_index("seq")
 
     normed = rms_normed(tokens, norm_gain)
@@ -64,36 +65,50 @@
     position = route_positions(routes, experts)
     owner = routes // local_experts
     local_index = routes % local_experts
-    sender = local_index * seq_per_expert + position // per_dev
-    within = position % per_dev
+    shared = position < share * seq_per_expert
+    sender = local_index * seq_per_expert + position // share
+    within = position % share
 
-    send_slots = per_dev * exp_count
-    slot_of = jnp.where(sender == my_seq, within * exp_count + owner, -1)
-    slot_ids = jnp.arange(send_slots, dtype=jnp.int32)
+    send_groups = share + local_experts * direct
+    direct_group = share + local_index * direct + position - share * seq_per_expert
+    slot_of = jnp.where(
+        shared,
+        jnp.where(sender == my_seq, within * exp_count + owner, -1),
+        direct_group * exp_count + owner,
+    )
+    slot_ids = jnp.arange(send_groups * exp_count, dtype=jnp.int32)
     pick = jnp.any(slot_of[None, :, :] == slot_ids[:, None, None], axis=2).astype(jnp.bfloat16)
     outgoing = jnp.dot(pick, normed, preferred_element_type=jnp.float32).astype(jnp.bfloat16)
-    outgoing = outgoing.reshape(per_dev, exp_count, width)
+    outgoing = outgoing.reshape(send_groups, exp_count, width)
     arrived = lax.all_to_all(outgoing, "exp", split_axis=1, concat_axis=1, tiled=True)
-    copies = jnp.broadcast_to(arrived[None], (seq_count,) + arrived.shape)
+    share_part = arrived[:share]
+    copies = jnp.broadcast_to(share_part[None], (seq_count,) + share_part.shape)
     gathered = lax.all_to_all(copies, "seq", split_axis=0, concat_axis=0, tiled=True)
-    rows = gathered.reshape(local_experts, seq_per_expert * per_dev * exp_count, width)
+    share_rows = gathered.reshape(local_experts, seq_per_expert * share * exp_count, width)
+    direct_rows = arrived[share:].reshape(local_experts, direct * exp_count, width)
 
-    gate = jnp.einsum("erd,edf->erf", rows, w_gate, preferred_element_type=jnp.float32)
-    upward = jnp.einsum("erd,edf->erf", rows, w_up, preferred_element_type=jnp.float32)
-    hidden = (jax.nn.silu(gate) * upward).astype(jnp.bfloat16)
     part_width = width // seq_count
     down = w_down.reshape(local_experts, w_down.shape[1], seq_count, part_width)
-    partial_value = jnp.einsum(
-        "erf,efcd->cerd", hidden, down, preferred_element_type=jnp.float32
-    ).astype(jnp.bfloat16)
+
+    def expert_pieces(rows):
+        gate = jnp.einsum("erd,edf->erf", rows, w_gate, preferred_element_type=jnp.float32)
+        upward = jnp.einsum("erd,edf->erf", rows, w_up, preferred_element_type=jnp.float32)
+        hidden = (jax.nn.silu(gate) * upward).astype(jnp.bfloat16)
+        return jnp.einsum(
+            "erf,efcd->cerd", hidden, down, preferred_element_type=jnp.float32
+        ).astype(jnp.bfloat16)
+
+    partial_value = jnp.concatenate(
+        [expert_pieces(share_rows), expert_pieces(direct_rows)], axis=2
+    )
     pieces = lax.all_to_all(partial_value, "seq", split_axis=0, concat_axis=0, tiled=True)
     summed = jnp.sum(pieces.astype(jnp.float32), axis=0).astype(jnp.bfloat16)
-    summed = summed.reshape(seq_count * per_dev, exp_count, part_width)
+    summed = summed.reshape(local_experts * capacity, exp_count, part_width)
     returned = lax.all_to_all(summed, "exp", split_axis=1, concat_axis=1, tiled=True)
-    recv_slots = seq_count * per_dev * exp_count
+    recv_slots = local_experts * capacity * exp_count
     returned = returned.reshape(recv_slots, part_width)
 
-    recv_slot = (sender * per_dev + within) * exp_count + owner
+    recv_slot = (local_index * capacity + position) * exp_count + owner
     recv_ids = jnp.arange(recv_slots, dtype=jnp.int32)
     weights = route_weights.astype(jnp.float32)
     mix = jnp.sum(

time: 382 us -> 376 us (0.984)
  waiting for transfers between devices: 227 us -> 204 us
  other arithmetic: 18.7 us -> 26.4 us
  matrix products: 22.8 us -> 29.3 us
    all_to_all x1, waiting for transfers between devices: 95.1 us -> 71.6 us  [per_device(): lax.all_to_all(copies, 'seq', split_axis=0, concat_axis=0, tiled=True)]
    concatenate x0 -> x1, other arithmetic: none -> 8.09 us  [per_device(): jnp.concatenate([expert_pieces(share_rows), expert_pieces(direct_rows)],...]
    concatenate x0 -> x1, local copies, waits for them, and re-layouts: none -> 8.04 us  [per_device(): jnp.concatenate([expert_pieces(share_rows), expert_pieces(direct_rows)],...]
    dot_general x3 -> x4, matrix products: 19.4 us -> 26 us  [the longest x2 16.2 us: expert_pieces(): jnp.einsum('erf,efcd->cerd', hidden, down, preferred_element_type=jnp.flo...]
    convert_element_type x1, local copies, waits for them, and re-layouts: 8.04 us -> 1.63 us  [expert_pieces(): return jnp.einsum('erf,efcd->cerd', hidden, down, preferred_element_type=...]
  transfers between devices with their start and end apart: 5 -> 5, of which waited for: 4 -> 4; matrix products, arithmetic and copies ran while one was open for 17% -> 22% of each run, Pallas kernels for 0% -> 0%
where the time goes in v5:
time: 376 us; the launch traced here: 371 us
  waiting for transfers between devices  204 us (54%)
  blocking collectives  41.1 us (11%)
  local copies, waits for them, and re-layouts  39.7 us (11%)
  starting transfers between devices  29.6 us (8%)
  matrix products  29.3 us (8%)
  other arithmetic  26.4 us (7%)
    all_to_all x1, waiting for transfers between devices, per_device(): lax.all_to_all(partial_value, 'seq', split_axis=0, concat_axis=0, tiled=T...  95.9 us
    all_to_all x1, waiting for transfers between devices, per_device(): lax.all_to_all(copies, 'seq', split_axis=0, concat_axis=0, tiled=True)  71.6 us
    all_to_all x1, blocking collectives, per_device(): lax.all_to_all(outgoing, 'exp', split_axis=1, concat_axis=1, tiled=True)  41.1 us
    all_to_all x1, waiting for transfers between devices, per_device(): lax.all_to_all(summed, 'exp', split_axis=1, concat_axis=1, tiled=True)  19.8 us
    all_to_all x1, waiting for transfers between devices, relayout(): lax.all_to_all(outgoing, 'seq', split_axis=1, concat_axis=1, tiled=True)  16.9 us
    dot_general x2, matrix products, expert_pieces(): jnp.einsum('erf,efcd->cerd', hidden, down, preferred_element_type=jnp.flo...  16.2 us
    dot_general x2, matrix products, expert_pieces(): jnp.einsum('erd,edf->erf', rows, w_gate, preferred_element_type=jnp.float32)  9.7 us
    concatenate x1, other arithmetic, per_device(): jnp.concatenate([expert_pieces(share_rows), expert_pieces(direct_rows)],...  8.09 us
  transfers between devices with their start and end apart: 5, of which 4 were waited for; matrix products, arithmetic and copies ran while one was open for 22% of the time, Pallas kernels for 0%

profile of v5, /device:TPU:120, one launch (start us, length us, event | category | flops | bytes accessed | tf_op | source)
XLA Modules:
  0.0 371.2 jit_solution(17073021926417790172)
XLA Ops:
  0.6 0.0 copy-start
  0.6 0.9 fusion.16
  1.5 0.2 fusion.21
  1.7 0.8 select_reduce_fusion.1
  2.5 0.7 multiply_add_fusion
  3.2 0.2 fusion.6
  3.5 1.7 fusion
  5.1 2.0 convolution_convert_fusion
  7.1 0.7 copy.88
  7.8 41.1 %all_to_all.37 = bf16[8,32,2560]{2,0,1:T(8,128)(2,1)S(1)} all-to-all(bf16[8,32,2560]{2,0,1:T(8,128)(2,1)S(1)} %copy.88), channel_id=1, replica_groups=mesh['seq'=8,'exp'=32] {'exp'}, dimensions={1} | all-to-all | bytes 2621440 | tf_op jit(solution)/shard_map/all_to_all | solution.py:83
  49.0 0.3 copy.89
  49.3 4.1 %broadcast_in_dim.36 = bf16[8,6,32,2560]{3,2,1,0:T(8,128)(2,1)} broadcast(bf16[6,32,2560]{2,1,0:T(8,128)(2,1)S(1)} %copy.89), dimensions={1,2,3} | broadcast | bytes 8847360 | tf_op jit(solution)/shard_map/broadcast_in_dim | solution.py:85
  53.3 6.9 %all-to-all-start.1 = ((bf16[8,6,32,2560]{3,2,1,0:T(8,128)(2,1)}), bf16[8,6,32,2560]{3,2,1,0:T(8,128)(2,1)}, u32[]{:S(2)}, u32[]{:S(2)}) async-start(bf16[8,6,32,2560]{3,2,1,0:T(8,128)(2,1)} %broadcast_in_dim.36), calls=%async_computation.1 | async-start | bytes 15728640 | tf_op jit(solution)/shard_map/all_to_all | solution.py:86
  60.2 0.0 copy-start.4
  60.2 4.7 %reshape.39 = bf16[2,192,8,320]{3,2,1,0:T(8,128)(2,1)} reshape(bf16[2,192,2560]{2,1,0:T(8,128)(2,1)} %param.16) | data formatting | bytes 3932160 | tf_op jit(solution)/shard_map/reshape | solution.py:91
  64.9 0.0 copy-done.4
  64.9 1.0 sort.31
  65.9 0.6 gather_fusion.2
  66.5 0.7 copy.100
  67.2 0.3 slice.17
  67.6 0.0 copy-start.1
  67.6 0.7 copy-done.1
  68.3 2.2 fusion.19
  70.5 3.6 fusion.3
  74.1 0.9 copy.119
  75.0 1.6 copy.94
  76.6 71.6 %all-to-all-done.1 = bf16[8,6,32,2560]{3,2,1,0:T(8,128)(2,1)} async-done(((bf16[8,6,32,2560]{3,2,1,0:T(8,128)(2,1)}), bf16[8,6,32,2560]{3,2,1,0:T(8,128)(2,1)}, u32[]{:S(2)}, u32[]{:S(2)}) %all-to-all-start.1) | async-done | bytes 7864352 | tf_op jit(solution)/shard_map/all_to_all | solution.py:86
  148.3 5.0 %all-to-all-start.5 = ((s32[8,1,1]{2,1,0:T(1,128)}), s32[8,1,1]{2,1,0:T(1,128)S(1)}, u32[]{:S(2)}, u32[]{:S(2)}) async-start(s32[8,1,1]{2,1,0:T(1,128)} %copy.100), calls=%async_computation.5 | async-start | bytes 8192 | tf_op jit(solution)/shard_map/all_to_all | solution.py:35
  153.3 7.5 %fusion.42 = f32[2,768,192]{1,2,0:T(8,128)} fusion(bf16[2,768,2560]{2,1,0:T(8,128)(2,1)} %bitcast.1, bf16[2,2560,192]{1,2,0:T(8,128)(2,1)} %param.14), kind=kOutput, calls=%fused_computation.87 | convolution fusion | flops 1509949440 | bytes 11010048 | tf_op jit(solution)/shard_map/erd,edf->erf/dot_general | solution.py:94
  160.8 12.6 %convert_bitcast_fusion = bf16[8,2,768,320]{2,3,0,1:T(8,128)(2,1)} fusion(bf16[2,192,8,320]{3,2,1,0:T(8,128)(2,1)} %reshape.39, bf16[2,768,2560]{2,1,0:T(8,128)(2,1)} %bitcast.1, bf16[2,2560,192]{1,2,0:T(8,128)(2,1)} %param.15, f32[2,768,192]{1,2,0:T(8,128)} %fusion.42), kind=kOutput, calls=%fused_computation.7 | convolution fusion | flops 3025600512 | bytes 20840448 | tf_op jit(solution)/shard_map/erf,efcd->cerd/dot_general | solution.py:97
  173.4 8.1 %pad_maximum_fusion = bf16[8,2,800,320]{2,3,0,1:T(8,128)(2,1)} fusion(bf16[8,2,32,320]{2,3,0,1:T(8,128)(2,1)S(1)} %copy.94, bf16[8,2,768,320]{2,3,0,1:T(8,128)(2,1)} %convert_bitcast_fusion), kind=kLoop, calls=%fused_computation.6 | loop fusion | flops 16384000 | bytes 16384000 | tf_op jit(solution)/shard_map/concatenate | solution.py:101
  181.5 8.0 %copy.95 = bf16[8,2,800,320]{2,3,1,0:T(8,128)(2,1)} copy(bf16[8,2,800,320]{2,3,0,1:T(8,128)(2,1)} %pad_maximum_fusion) | data formatting | bytes 16384000 | tf_op jit(solution)/shard_map/concatenate | solution.py:101
  189.5 0.0 all-to-all-done.5
  189.5 7.2 %all-to-all-start.2 = ((bf16[8,2,800,320]{2,3,1,0:T(8,128)(2,1)}), bf16[8,2,800,320]{2,3,1,0:T(8,128)(2,1)}, u32[]{:S(2)}, u32[]{:S(2)}) async-start(bf16[8,2,800,320]{2,3,1,0:T(8,128)(2,1)} %copy.95), calls=%async_computation.2 | async-start | bytes 18350080 | tf_op jit(solution)/shard_map/all_to_all | solution.py:104
  196.7 0.0 copy-done
  196.7 0.0 copy-start.5
  196.7 2.0 gather_fusion
  198.7 0.0 copy-done.5
  198.8 0.6 gather_fusion.1
  199.4 3.1 multiply_bitcast_fusion
  202.5 95.9 %all-to-all-done.2 = bf16[8,2,800,320]{2,3,1,0:T(8,128)(2,1)} async-done(((bf16[8,2,800,320]{2,3,1,0:T(8,128)(2,1)}), bf16[8,2,800,320]{2,3,1,0:T(8,128)(2,1)}, u32[]{:S(2)}, u32[]{:S(2)}) %all-to-all-start.2) | async-done | bytes 8192032 | tf_op jit(solution)/shard_map/all_to_all | solution.py:104
  298.5 5.0 %all-to-all-start.4 = ((bf16[4,8,32,1024]{3,2,0,1:T(8,128)(2,1)}), bf16[4,8,32,1024]{3,2,0,1:T(8,128)(2,1)}, u32[]{:S(2)}, u32[]{:S(2)}) async-start(bf16[4,8,32,1024]{3,2,0,1:T(8,128)(2,1)} %multiply_bitcast_fusion), calls=%async_computation.4 | async-start | bytes 4194304 | tf_op jit(solution)/shard_map/all_to_all | solution.py:34
  303.5 6.3 %reduce_sum.42 = bf16[2,800,320]{1,2,0:T(8,128)(2,1)} reduce(bf16[8,2,800,320]{2,3,1,0:T(8,128)(2,1)} %all-to-all-done.2, bf16[]{:T(256)} %constant.105.clone.1), dimensions={0}, to_apply=%region_5.6 | reduce | flops 3584000 | bytes 9216002 | tf_op jit(solution)/shard_map/reduce_sum | solution.py:105
  309.7 1.7 copy.97
  311.5 0.0 copy-start.3
  311.5 1.5 copy.98
  313.0 16.9 %all-to-all-done.4 = bf16[4,8,32,1024]{3,2,0,1:T(8,128)(2,1)} async-done(((bf16[4,8,32,1024]{3,2,0,1:T(8,128)(2,1)}), bf16[4,8,32,1024]{3,2,0,1:T(8,128)(2,1)}, u32[]{:S(2)}, u32[]{:S(2)}) %all-to-all-start.4) | async-done | bytes 2097184 | tf_op jit(solution)/shard_map/all_to_all | solution.py:34
  329.9 5.5 %all-to-all-start.3 = ((bf16[50,32,320]{2,0,1:T(8,128)(2,1)}), bf16[50,32,320]{2,0,1:T(8,128)(2,1)S(1)}, u32[]{:S(2)}, u32[]{:S(2)}) async-start(bf16[50,32,320]{2,0,1:T(8,128)(2,1)} %copy.98), calls=%async_computation.3 | async-start | bytes 2752512 | tf_op jit(solution)/shard_map/all_to_all | solution.py:107
  335.4 0.0 copy-done.3
  335.4 2.4 select_reduce_fusion
  337.8 0.2 reduce.1
  338.1 1.0 sort.32
  339.1 3.2 copy.101
  342.2 3.6 gather_fusion.3
  345.9 3.2 copy.102
  349.0 19.8 %all-to-all-done.3 = bf16[50,32,320]{2,0,1:T(8,128)(2,1)S(1)} async-done(((bf16[50,32,320]{2,0,1:T(8,128)(2,1)}), bf16[50,32,320]{2,0,1:T(8,128)(2,1)S(1)}, u32[]{:S(2)}, u32[]{:S(2)}) %all-to-all-start.3) | async-done | bytes 1024032 | tf_op jit(solution)/shard_map/all_to_all | solution.py:107
  368.8 0.0 copy-start.2
  368.8 0.2 copy.99
  369.0 1.0 copy-done.2
  370.0 1.3 convolution_convert_fusion.1
  (10 shorter events, 0.1 us)
Async XLA Ops:
  0.6 196.1 %copy-start = (bf16[4,8,32,1024]{3,2,1,0:T(8,128)(2,1)S(1)}, bf16[4,8,32,1024]{3,2,1,0:T(8,128)(2,1)}, u32[]{:S(2)}) copy-start(bf16[4,8,32,1024]{3,2,1,0:T(8,128)(2,1)} %param.17) | copy-start | bytes 6291460
  53.3 94.9 %all-to-all-start.1 = ((bf16[8,6,32,2560]{3,2,1,0:T(8,128)(2,1)}), bf16[8,6,32,2560]{3,2,1,0:T(8,128)(2,1)}, u32[]{:S(2)}, u32[]{:S(2)}) async-start(bf16[8,6,32,2560]{3,2,1,0:T(8,128)(2,1)} %broadcast_in_dim.36), calls=%async_computation.1 | async-start | bytes 15728640 | tf_op jit(solution)/shard_map/all_to_all | solution.py:86
  60.2 4.7 %copy-start.4 = (s32[8]{0:T(128)S(1)}, s32[8]{0:T(128)}, u32[]{:S(2)}) copy-start(s32[8]{0:T(128)} %param.18) | copy-start | bytes 100
  67.6 0.7 copy-start.1
  148.3 41.3 %all-to-all-start.5 = ((s32[8,1,1]{2,1,0:T(1,128)}), s32[8,1,1]{2,1,0:T(1,128)S(1)}, u32[]{:S(2)}, u32[]{:S(2)}) async-start(s32[8,1,1]{2,1,0:T(1,128)} %copy.100), calls=%async_computation.5 | async-start | bytes 8192 | tf_op jit(solution)/shard_map/all_to_all | solution.py:35
  189.5 108.9 %all-to-all-start.2 = ((bf16[8,2,800,320]{2,3,1,0:T(8,128)(2,1)}), bf16[8,2,800,320]{2,3,1,0:T(8,128)(2,1)}, u32[]{:S(2)}, u32[]{:S(2)}) async-start(bf16[8,2,800,320]{2,3,1,0:T(8,128)(2,1)} %copy.95), calls=%async_computation.2 | async-start | bytes 18350080 | tf_op jit(solution)/shard_map/all_to_all | solution.py:104
  196.7 2.0 copy-start.5
  298.5 31.5 %all-to-all-start.4 = ((bf16[4,8,32,1024]{3,2,0,1:T(8,128)(2,1)}), bf16[4,8,32,1024]{3,2,0,1:T(8,128)(2,1)}, u32[]{:S(2)}, u32[]{:S(2)}) async-start(bf16[4,8,32,1024]{3,2,0,1:T(8,128)(2,1)} %multiply_bitcast_fusion), calls=%async_computation.4 | async-start | bytes 4194304 | tf_op jit(solution)/shard_map/all_to_all | solution.py:34
  311.5 23.9 %copy-start.3 = (bf16[256,6]{0,1:T(8,128)(2,1)S(1)}, bf16[256,6]{0,1:T(8,128)(2,1)}, u32[]{:S(2)}) copy-start(bf16[256,6]{0,1:T(8,128)(2,1)} %param.13) | copy-start | bytes 9220
  329.9 38.9 %all-to-all-start.3 = ((bf16[50,32,320]{2,0,1:T(8,128)(2,1)}), bf16[50,32,320]{2,0,1:T(8,128)(2,1)S(1)}, u32[]{:S(2)}, u32[]{:S(2)}) async-start(bf16[50,32,320]{2,0,1:T(8,128)(2,1)} %copy.98), calls=%async_computation.3 | async-start | bytes 2752512 | tf_op jit(solution)/shard_map/all_to_all | solution.py:107
  368.8 1.1 copy-start.2

commit v6 on v5

--- a/solution.py
+++ b/solution.py
@@ -22,18 +22,29 @@
     return picked.astype(jnp.int32)
 
 
-def relayout(kv_prefill, block_map, block_empty):
+def relayout_outgoing(kv_prefill, block_map, block_empty):
     layers, blocks, block_rows, kv_width = kv_prefill.shape
     exp_count = lax.axis_size("exp")
     keep = (1 - block_empty).astype(kv_prefill.dtype)
     peer = block_map // blocks // exp_count
     target = block_map % blocks
     order = jnp.argsort(peer)
-    outgoing = kv_prefill[:, order] * keep[order][None, :, None, None]
-    labels = target[order]
-    arrived = lax.all_to_all(outgoing, "seq", split_axis=1, concat_axis=1, tiled=True)
-    slots = lax.all_to_all(labels, "seq", split_axis=0, concat_axis=0, tiled=True)
-    return arrived[:, jnp.argsort(slots)]
+    kept = kv_prefill[:, order] * keep[order][None, :, None, None]
+    kept = jnp.transpose(kept, (1, 0, 2, 3)).reshape(blocks, -1)
+    tags = jnp.broadcast_to(target[order].astype(kv_prefill.dtype)[:, None], (blocks, 128))
+    return jnp.concatenate([kept, tags], axis=1)
+
+
+def relayout_finish(outgoing, kv_prefill):
+    layers, blocks, block_rows, kv_width = kv_prefill.shape
+    block_size = layers * block_rows * kv_width
+    arrived = lax.all_to_all(outgoing, "seq", split_axis=0, concat_axis=0, tiled=True)
+    slots = arrived[:, block_size].astype(jnp.int32)
+    place = (slots[None, :] == jnp.arange(blocks, dtype=jnp.int32)[:, None]).astype(arrived.dtype)
+    data = arrived[:, :block_size].reshape(blocks, layers, block_rows, kv_width)
+    return jnp.einsum(
+        "ms,slrk->lmrk", place, data, preferred_element_type=jnp.float32
+    ).astype(arrived.dtype)
 
 
 def per_device(
@@ -84,6 +95,8 @@
     share_part = arrived[:share]
     copies = jnp.broadcast_to(share_part[None], (seq_count,) + share_part.shape)
     gathered = lax.all_to_all(copies, "seq", split_axis=0, concat_axis=0, tiled=True)
+    kv_out = relayout_outgoing(kv_prefill, block_map, block_empty)
+    gathered, kv_out = lax.optimization_barrier((gathered, kv_out))
     share_rows = gathered.reshape(local_experts, seq_per_expert * share * exp_count, width)
     direct_rows = arrived[share:].reshape(local_experts, direct * exp_count, width)
 
@@ -101,6 +114,8 @@
     partial_value = jnp.concatenate(
         [expert_pieces(share_rows), expert_pieces(direct_rows)], axis=2
     )
+    kv_decode = relayout_finish(kv_out, kv_prefill)
+    kv_decode, partial_value = lax.optimization_barrier((kv_decode, partial_value))
     pieces = lax.all_to_all(partial_value, "seq", split_axis=0, concat_axis=0, tiled=True)
     summed = jnp.sum(pieces.astype(jnp.float32), axis=0).astype(jnp.bfloat16)
     summed = summed.reshape(local_experts * capacity, exp_count, part_width)
@@ -116,7 +131,6 @@
     ).astype(jnp.bfloat16)
     mixed = jnp.dot(mix, returned, preferred_element_type=jnp.float32).astype(jnp.bfloat16)
 
-    kv_decode = relayout(kv_prefill, block_map, block_empty)
     return (mixed, kv_decode)
 
 

time: 376 us -> 381 us (1.013)
  waiting for transfers between devices: 204 us -> 124 us
  blocking collectives: 41.1 us -> 109 us
  local copies, waits for them, and re-layouts: 39.7 us -> 52 us
  other arithmetic: 26.4 us -> 32.6 us
    all_to_all x3 -> x2, waiting for transfers between devices: 113 us -> 24.7 us  [the longest x1 24.7 us: per_device(): lax.all_to_all(outgoing, 'exp', split_axis=1, concat_axis=1, tiled=True)]
    all_to_all x1, blocking collectives: 41.1 us -> 109 us  [per_device(): lax.all_to_all(partial_value, 'seq', split_axis=0, concat_axis=0, tiled=T...]
    unnamed x13 -> x21, local copies, waits for them, and re-layouts: 4.9 us -> 23.7 us
    concatenate x1 -> x0, local copies, waits for them, and re-layouts: 8.04 us -> none  [per_device(): jnp.concatenate([expert_pieces(share_rows), expert_pieces(direct_rows)],...]
    optimization_barrier x0 -> x1, local copies, waits for them, and re-layouts: none -> 7.98 us  [per_device(): lax.optimization_barrier((kv_decode, partial_value))]
    all_to_all x1, other arithmetic: 0.23 us -> 7.42 us  [relayout_finish(): lax.all_to_all(outgoing, 'seq', split_axis=0, concat_axis=0, tiled=True)]
    all_to_all x1, waiting for transfers between devices: 19.8 us -> 26.7 us  [per_device(): lax.all_to_all(summed, 'exp', split_axis=1, concat_axis=1, tiled=True)]
    all_to_all x3 -> x2, starting transfers between devices: 17.3 us -> 13.8 us  [the longest x1 8.75 us: per_device(): lax.all_to_all(outgoing, 'exp', split_axis=1, concat_axis=1, tiled=True)]
  transfers between devices with their start and end apart: 5 -> 4, of which waited for: 4 -> 3; matrix products, arithmetic and copies ran while one was open for 22% -> 15% of each run, Pallas kernels for 0% -> 0%
where the time goes in v6:
time: 381 us; the launch traced here: 374 us
  waiting for transfers between devices  124 us (33%)
  blocking collectives  109 us (29%)
  local copies, waits for them, and re-layouts  52 us (14%)
  other arithmetic  32.6 us (9%)
  matrix products  29.3 us (8%)
  starting transfers between devices  26.8 us (7%)
    all_to_all x1, blocking collectives, per_device(): lax.all_to_all(partial_value, 'seq', split_axis=0, concat_axis=0, tiled=T...  109 us
    all_to_all x1, waiting for transfers between devices, per_device(): lax.all_to_all(copies, 'seq', split_axis=0, concat_axis=0, tiled=True)  72.7 us
    all_to_all x1, waiting for transfers between devices, per_device(): lax.all_to_all(summed, 'exp', split_axis=1, concat_axis=1, tiled=True)  26.7 us
    all_to_all x1, waiting for transfers between devices, per_device(): lax.all_to_all(outgoing, 'exp', split_axis=1, concat_axis=1, tiled=True)  24.7 us
    unnamed x21, local copies, waits for them, and re-layouts  23.7 us
    dot_general x2, matrix products, expert_pieces(): jnp.einsum('erf,efcd->cerd', hidden, down, preferred_element_type=jnp.flo...  16.2 us
    all_to_all x1, starting transfers between devices, per_device(): lax.all_to_all(outgoing, 'exp', split_axis=1, concat_axis=1, tiled=True)  8.75 us
    concatenate x1, other arithmetic, per_device(): jnp.concatenate([expert_pieces(share_rows), expert_pieces(direct_rows)],...  8.09 us
  transfers between devices with their start and end apart: 4, of which 3 were waited for; matrix products, arithmetic and copies ran while one was open for 15% of the time, Pallas kernels for 0%

profile of v6, /device:TPU:120, one launch (start us, length us, event | category | flops | bytes accessed | tf_op | source)
XLA Modules:
  0.0 374.3 jit_solution(2147383014694369788)
XLA Ops:
  0.6 0.0 copy-start
  0.6 0.9 fusion.16
  1.6 0.2 fusion.21
  1.7 0.8 select_reduce_fusion.1
  2.5 0.7 multiply_add_fusion
  3.2 0.2 fusion.6
  3.5 1.7 fusion
  5.1 2.0 convolution_convert_fusion
  7.1 0.0 copy-start.6
  7.1 1.8 copy.82
  8.9 8.7 %all-to-all-start = ((bf16[8,32,2560]{2,0,1:T(8,128)(2,1)}), bf16[8,32,2560]{2,0,1:T(8,128)(2,1)S(1)}, u32[]{:S(2)}, u32[]{:S(2)}) async-start(bf16[8,32,2560]{2,0,1:T(8,128)(2,1)} %copy.82), calls=%async_computation | async-start | bytes 2621440 | tf_op jit(solution)/shard_map/all_to_all | solution.py:94
  17.6 0.0 copy-done.6
  17.7 1.0 sort.17
  18.7 0.6 gather_fusion.2
  19.3 0.0 copy-done
  19.3 0.0 copy-start.7
  19.3 2.0 gather_fusion
  21.3 0.0 copy-done.7
  21.3 0.6 gather_fusion.1
  22.0 1.8 broadcast_multiply_fusion
  23.8 1.2 copy.103
  25.0 24.7 %all-to-all-done = bf16[8,32,2560]{2,0,1:T(8,128)(2,1)S(1)} async-done(((bf16[8,32,2560]{2,0,1:T(8,128)(2,1)}), bf16[8,32,2560]{2,0,1:T(8,128)(2,1)S(1)}, u32[]{:S(2)}, u32[]{:S(2)}) %all-to-all-start) | async-done | bytes 1310752 | tf_op jit(solution)/shard_map/all_to_all | solution.py:94
  49.7 0.3 copy.83
  50.0 4.1 %broadcast_in_dim.32 = bf16[8,6,32,2560]{3,2,1,0:T(8,128)(2,1)} broadcast(bf16[6,32,2560]{2,1,0:T(8,128)(2,1)S(1)} %copy.83), dimensions={1,2,3} | broadcast | bytes 8847360 | tf_op jit(solution)/shard_map/broadcast_in_dim | solution.py:96
  54.0 6.9 %all-to-all-start.1 = ((bf16[8,6,32,2560]{3,2,1,0:T(8,128)(2,1)}), bf16[8,6,32,2560]{3,2,1,0:T(8,128)(2,1)}, u32[]{:S(2)}, u32[]{:S(2)}) async-start(bf16[8,6,32,2560]{3,2,1,0:T(8,128)(2,1)} %broadcast_in_dim.32), calls=%async_computation.1 | async-start | bytes 15728640 | tf_op jit(solution)/shard_map/all_to_all | solution.py:97
  60.9 0.1 broadcast_in_dim.34
  61.0 2.1 pad_maximum_fusion.1
  63.1 4.9 %reshape.57 = bf16[2,192,8,320]{3,2,1,0:T(8,128)(2,1)} reshape(bf16[2,192,2560]{2,1,0:T(8,128)(2,1)} %param.16) | data formatting | bytes 3932160 | tf_op jit(solution)/shard_map/reshape | solution.py:104
  67.9 0.3 slice.25
  68.3 0.0 copy-start.3
  68.3 0.7 copy-done.3
  69.0 0.0 copy-done.2
  69.0 0.7 fusion.19
  69.7 3.6 fusion.3
  73.3 0.9 copy.118
  74.2 1.6 copy.90
  75.8 72.7 %all-to-all-done.1 = bf16[8,6,32,2560]{3,2,1,0:T(8,128)(2,1)} async-done(((bf16[8,6,32,2560]{3,2,1,0:T(8,128)(2,1)}), bf16[8,6,32,2560]{3,2,1,0:T(8,128)(2,1)}, u32[]{:S(2)}, u32[]{:S(2)}) %all-to-all-start.1) | async-done | bytes 7864352 | tf_op jit(solution)/shard_map/all_to_all | solution.py:97
  148.5 0.5 broadcast.129
  149.0 7.4 %reduce.3 = bf16[8,131200]{1,0:T(8,128)(2,1)} reduce(bf16[8,1,131200]{2,0,1:T(8,128)(2,1)} %bitcast.48, bf16[]{:T(256)} %broadcast.129), dimensions={1}, to_apply=%copy.84.reduce_sub_computation | reduce | bytes 4198402 | tf_op jit(solution)/shard_map/all_to_all | solution.py:41
  156.4 4.3 %reshape.92 = bf16[8,2,65600]{2,1,0:T(2,128)(2,1)} reshape(bf16[8,131200]{1,0:T(8,128)(2,1)} %reduce.3) | data formatting | bytes 4198400
  160.7 5.0 %all-to-all-start.2 = ((bf16[8,2,65600]{2,1,0:T(2,128)(2,1)}), bf16[8,2,65600]{2,1,0:T(2,128)(2,1)}, u32[]{:S(2)}, u32[]{:S(2)}) async-start(bf16[8,2,65600]{2,1,0:T(2,128)(2,1)} %reshape.92), calls=%async_computation.2 | async-start | bytes 4202496 | tf_op jit(solution)/shard_map/all_to_all | solution.py:41
  165.7 6.9 %fusion.45 = f32[2,768,192]{1,2,0:T(8,128)} fusion(bf16[2,768,2560]{2,1,0:T(8,128)(2,1)} %bitcast.6, bf16[2,2560,192]{1,2,0:T(8,128)(2,1)S(1)} %copy-done.2), kind=kOutput, calls=%fused_computation.91 | convolution fusion | flops 1509949440 | bytes 11010048 | tf_op jit(solution)/shard_map/erd,edf->erf/dot_general | solution.py:107
  172.7 12.6 %convert_bitcast_fusion = bf16[8,2,768,320]{2,3,0,1:T(8,128)(2,1)} fusion(bf16[2,192,8,320]{3,2,1,0:T(8,128)(2,1)} %reshape.57, bf16[2,768,2560]{2,1,0:T(8,128)(2,1)} %bitcast.6, bf16[2,2560,192]{1,2,0:T(8,128)(2,1)} %param.15, f32[2,768,192]{1,2,0:T(8,128)} %fusion.45), kind=kOutput, calls=%fused_computation.6 | convolution fusion | flops 3025600512 | bytes 20840448 | tf_op jit(solution)/shard_map/erf,efcd->cerd/dot_general | solution.py:110
  185.3 8.1 %pad_maximum_fusion = bf16[8,2,800,320]{2,3,0,1:T(8,128)(2,1)} fusion(bf16[8,2,32,320]{2,3,0,1:T(8,128)(2,1)S(1)} %copy.90, bf16[8,2,768,320]{2,3,0,1:T(8,128)(2,1)} %convert_bitcast_fusion), kind=kLoop, calls=%fused_computation.5 | loop fusion | flops 16384000 | bytes 16384000 | tf_op jit(solution)/shard_map/concatenate | solution.py:114
  193.4 0.0 all-to-all-done.2
  193.4 9.5 %reshape.93 = bf16[8,1,131200]{2,1,0:T(2,128)(2,1)} reshape(bf16[8,2,65600]{2,1,0:T(2,128)(2,1)} %all-to-all-done.2) | data formatting | bytes 4198400
  202.9 2.8 copy.117
  205.7 0.1 slice.23
  205.9 0.1 convert_reduce_fusion
  206.0 2.1 convert_bitcast_fusion.1
  208.0 8.0 %copy.91 = bf16[8,2,800,320]{2,3,1,0:T(8,128)(2,1)} copy(bf16[8,2,800,320]{2,3,0,1:T(8,128)(2,1)} %pad_maximum_fusion) | data formatting | bytes 16384000 | tf_op jit(solution)/shard_map/optimization_barrier | solution.py:118
  216.0 108.7 %all_to_all.32 = bf16[8,2,800,320]{2,3,1,0:T(8,128)(2,1)} all-to-all(bf16[8,2,800,320]{2,3,1,0:T(8,128)(2,1)} %copy.91), channel_id=1, replica_groups=mesh['seq'=8,'exp'=32] {'seq'}, dimensions={0} | all-to-all | bytes 16384000 | tf_op jit(solution)/shard_map/all_to_all | solution.py:119
  324.7 5.3 %reduce_sum.42 = bf16[2,800,320]{1,2,0:T(8,128)(2,1)S(1)} reduce(bf16[8,2,800,320]{2,3,1,0:T(8,128)(2,1)} %all_to_all.32, bf16[]{:T(256)} %constant.110.clone.1), dimensions={0}, to_apply=%region_6.7 | reduce | flops 3584000 | bytes 9216002 | tf_op jit(solution)/shard_map/reduce_sum | solution.py:120
  330.1 0.8 copy.93
  330.9 0.0 copy-start.5
  330.9 1.5 copy.94
  332.4 6.1 %all-to-all-start.4 = ((bf16[50,32,320]{2,0,1:T(8,128)(2,1)}), bf16[50,32,320]{2,0,1:T(8,128)(2,1)S(1)}, u32[]{:S(2)}, u32[]{:S(2)}) async-start(bf16[50,32,320]{2,0,1:T(8,128)(2,1)} %copy.94), calls=%async_computation.4 | async-start | bytes 2752512 | tf_op jit(solution)/shard_map/all_to_all | solution.py:122
  338.5 0.0 copy-done.5
  338.6 2.4 select_reduce_fusion
  341.0 4.2 %copy.96 = bf16[4,8,32,1024]{3,2,1,0:T(8,128)(2,1)} copy(bf16[4,8,32,1024]{3,1,2,0:T(8,128)(2,1)} %convert_bitcast_fusion.1) | data formatting | bytes 4194304
  345.2 26.7 %all-to-all-done.4 = bf16[50,32,320]{2,0,1:T(8,128)(2,1)S(1)} async-done(((bf16[50,32,320]{2,0,1:T(8,128)(2,1)}), bf16[50,32,320]{2,0,1:T(8,128)(2,1)S(1)}, u32[]{:S(2)}, u32[]{:S(2)}) %all-to-all-start.4) | async-done | bytes 1024032 | tf_op jit(solution)/shard_map/all_to_all | solution.py:122
  371.9 0.2 copy.95
  372.1 1.0 copy-done.4
  373.0 1.3 convolution_convert_fusion.1
  (12 shorter events, 0.1 us)
Async XLA Ops:
  0.6 18.7 %copy-start = (bf16[4,8,32,1024]{3,2,1,0:T(8,128)(2,1)S(1)}, bf16[4,8,32,1024]{3,2,1,0:T(8,128)(2,1)}, u32[]{:S(2)}) copy-start(bf16[4,8,32,1024]{3,2,1,0:T(8,128)(2,1)} %param.17) | copy-start | bytes 6291460
  7.1 10.6 %copy-start.6 = (s32[8]{0:T(128)S(1)}, s32[8]{0:T(128)}, u32[]{:S(2)}) copy-start(s32[8]{0:T(128)} %param.18) | copy-start | bytes 100
  8.9 40.8 %all-to-all-start = ((bf16[8,32,2560]{2,0,1:T(8,128)(2,1)}), bf16[8,32,2560]{2,0,1:T(8,128)(2,1)S(1)}, u32[]{:S(2)}, u32[]{:S(2)}) async-start(bf16[8,32,2560]{2,0,1:T(8,128)(2,1)} %copy.82), calls=%async_computation | async-start | bytes 2621440 | tf_op jit(solution)/shard_map/all_to_all | solution.py:94
  19.3 2.0 copy-start.7
  54.0 94.4 %all-to-all-start.1 = ((bf16[8,6,32,2560]{3,2,1,0:T(8,128)(2,1)}), bf16[8,6,32,2560]{3,2,1,0:T(8,128)(2,1)}, u32[]{:S(2)}, u32[]{:S(2)}) async-start(bf16[8,6,32,2560]{3,2,1,0:T(8,128)(2,1)} %broadcast_in_dim.32), calls=%async_computation.1 | async-start | bytes 15728640 | tf_op jit(solution)/shard_map/all_to_all | solution.py:97
  63.1 5.9 %copy-start.2 = (bf16[2,2560,192]{1,2,0:T(8,128)(2,1)S(1)}, bf16[2,2560,192]{1,2,0:T(8,128)(2,1)}, u32[]{:S(2)}) copy-start(bf16[2,2560,192]{1,2,0:T(8,128)(2,1)} %param.14) | copy-start | bytes 5898244
  68.3 0.7 copy-start.3
  160.7 32.7 %all-to-all-start.2 = ((bf16[8,2,65600]{2,1,0:T(2,128)(2,1)}), bf16[8,2,65600]{2,1,0:T(2,128)(2,1)}, u32[]{:S(2)}, u32[]{:S(2)}) async-start(bf16[8,2,65600]{2,1,0:T(2,128)(2,1)} %reshape.92), calls=%async_computation.2 | async-start | bytes 4202496 | tf_op jit(solution)/shard_map/all_to_all | solution.py:41
  330.9 7.7 %copy-start.5 = (bf16[256,6]{0,1:T(8,128)(2,1)S(1)}, bf16[256,6]{0,1:T(8,128)(2,1)}, u32[]{:S(2)}) copy-start(bf16[256,6]{0,1:T(8,128)(2,1)} %param.13) | copy-start | bytes 9220
  332.4 39.5 %all-to-all-start.4 = ((bf16[50,32,320]{2,0,1:T(8,128)(2,1)}), bf16[50,32,320]{2,0,1:T(8,128)(2,1)S(1)}, u32[]{:S(2)}, u32[]{:S(2)}) async-start(bf16[50,32,320]{2,0,1:T(8,128)(2,1)} %copy.94), calls=%async_computation.4 | async-start | bytes 2752512 | tf_op jit(solution)/shard_map/all_to_all | solution.py:122
  341.0 33.3 %copy-start.1 = (bf16[4,8,32,1024]{3,2,1,0:T(8,128)(2,1)S(1)}, bf16[4,8,32,1024]{3,2,1,0:T(8,128)(2,1)}, u32[]{:S(2)}) copy-start(bf16[4,8,32,1024]{3,2,1,0:T(8,128)(2,1)} %param.17) | copy-start | bytes 6291460
  371.9 1.1 copy-start.4

commit v7 on v5

--- a/solution.py
+++ b/solution.py
@@ -54,9 +54,8 @@
     experts = local_experts * exp_count
     tok_count, topk = routes.shape
     capacity = tok_count * topk // experts + 1
-    seq_per_expert = seq_count // local_experts
-    share = capacity // seq_per_expert
-    direct = capacity - share * seq_per_expert
+    share = capacity // seq_count
+    direct = capacity - share * seq_count
     my_seq = lax.axis_index("seq")
 
     normed = rms_normed(tokens, norm_gain)
@@ -65,15 +64,16 @@
     position = route_positions(routes, experts)
     owner = routes // local_experts
     local_index = routes % local_experts
-    shared = position < share * seq_per_expert
-    sender = local_index * seq_per_expert + position // share
+    shared = position < share * seq_count
+    sender = position // share
     within = position % share
 
-    send_groups = share + local_experts * direct
-    direct_group = share + local_index * direct + position - share * seq_per_expert
+    share_groups = local_experts * share
+    send_groups = share_groups + local_experts * direct
+    direct_group = share_groups + local_index * direct + position - share * seq_count
     slot_of = jnp.where(
         shared,
-        jnp.where(sender == my_seq, within * exp_count + owner, -1),
+        jnp.where(sender == my_seq, (local_index * share + within) * exp_count + owner, -1),
         direct_group * exp_count + owner,
     )
     slot_ids = jnp.arange(send_groups * exp_count, dtype=jnp.int32)
@@ -81,29 +81,32 @@
     outgoing = jnp.dot(pick, normed, preferred_element_type=jnp.float32).astype(jnp.bfloat16)
     outgoing = outgoing.reshape(send_groups, exp_count, width)
     arrived = lax.all_to_all(outgoing, "exp", split_axis=1, concat_axis=1, tiled=True)
-    share_part = arrived[:share]
-    copies = jnp.broadcast_to(share_part[None], (seq_count,) + share_part.shape)
-    gathered = lax.all_to_all(copies, "seq", split_axis=0, concat_axis=0, tiled=True)
-    share_rows = gathered.reshape(local_experts, seq_per_expert * share * exp_count, width)
-    direct_rows = arrived[share:].reshape(local_experts, direct * exp_count, width)
 
     part_width = width // seq_count
-    down = w_down.reshape(local_experts, w_down.shape[1], seq_count, part_width)
 
-    def expert_pieces(rows):
-        gate = jnp.einsum("erd,edf->erf", rows, w_gate, preferred_element_type=jnp.float32)
-        upward = jnp.einsum("erd,edf->erf", rows, w_up, preferred_element_type=jnp.float32)
+    def expert_pieces(rows, e):
+        gate = jnp.dot(rows, w_gate[e], preferred_element_type=jnp.float32)
+        upward = jnp.dot(rows, w_up[e], preferred_element_type=jnp.float32)
         hidden = (jax.nn.silu(gate) * upward).astype(jnp.bfloat16)
+        down = w_down[e].reshape(w_down.shape[1], seq_count, part_width)
         return jnp.einsum(
-            "erf,efcd->cerd", hidden, down, preferred_element_type=jnp.float32
+            "rf,fcd->crd", hidden, down, preferred_element_type=jnp.float32
         ).astype(jnp.bfloat16)
 
-    partial_value = jnp.concatenate(
-        [expert_pieces(share_rows), expert_pieces(direct_rows)], axis=2
-    )
-    pieces = lax.all_to_all(partial_value, "seq", split_axis=0, concat_axis=0, tiled=True)
-    summed = jnp.sum(pieces.astype(jnp.float32), axis=0).astype(jnp.bfloat16)
-    summed = summed.reshape(local_experts * capacity, exp_count, part_width)
+    totals = []
+    for e in range(local_experts):
+        share_part = arrived[e * share:(e + 1) * share]
+        copies = jnp.broadcast_to(share_part[None], (seq_count,) + share_part.shape)
+        gathered = lax.all_to_all(copies, "seq", split_axis=0, concat_axis=0, tiled=True)
+        share_rows = gathered.reshape(seq_count * share * exp_count, width)
+        direct_rows = arrived[share_groups + e * direct:share_groups + (e + 1) * direct]
+        direct_rows = direct_rows.reshape(direct * exp_count, width)
+        partial_value = jnp.concatenate(
+            [expert_pieces(share_rows, e), expert_pieces(direct_rows, e)], axis=1
+        )
+        pieces = lax.all_to_all(partial_value, "seq", split_axis=0, concat_axis=0, tiled=True)
+        totals.append(jnp.sum(pieces.astype(jnp.float32), axis=0).astype(jnp.bfloat16))
+    summed = jnp.stack(totals).reshape(local_experts * capacity, exp_count, part_width)
     returned = lax.all_to_all(summed, "exp", split_axis=1, concat_axis=1, tiled=True)
     recv_slots = local_experts * capacity * exp_count
     returned = returned.reshape(recv_slots, part_width)

time: 376 us -> 366 us (0.973)
  blocking collectives: 41.1 us -> 0 us
  starting transfers between devices: 29.6 us -> 48.3 us
  matrix products: 29.3 us -> 33.5 us
    all_to_all x1 -> x0, blocking collectives: 41.1 us -> none  [per_device(): lax.all_to_all(outgoing, 'exp', split_axis=1, concat_axis=1, tiled=True)]
    all_to_all x0 -> x1, waiting for transfers between devices: none -> 29.7 us  [per_device(): lax.all_to_all(outgoing, 'exp', split_axis=1, concat_axis=1, tiled=True)]
    all_to_all x1 -> x2, waiting for transfers between devices: 95.9 us -> 78.5 us  [per_device(): lax.all_to_all(partial_value, 'seq', split_axis=0, concat_axis=0, tiled=T...]
    all_to_all x1 -> x2, waiting for transfers between devices: 71.6 us -> 60.3 us  [per_device(): lax.all_to_all(copies, 'seq', split_axis=0, concat_axis=0, tiled=True)]
    all_to_all x0 -> x1, starting transfers between devices: none -> 8.74 us  [per_device(): lax.all_to_all(outgoing, 'exp', split_axis=1, concat_axis=1, tiled=True)]
    concatenate x1 -> x0, local copies, waits for them, and re-layouts: 8.04 us -> none  [per_device(): jnp.concatenate([expert_pieces(share_rows), expert_pieces(direct_rows)],...]
    slice x2 -> x5, local copies, waits for them, and re-layouts: 0.63 us -> 8.45 us  [the longest x3 4.13 us: per_device(): share_part = arrived[e * share:(e + 1) * share]]
    another operation x0 -> x3, local copies, waits for them, and re-layouts: none -> 6.24 us  [the longest x2 4.52 us: expert_pieces(): down = w_down[e].reshape(w_down.shape[1], seq_count, part_width)]
  transfers between devices with their start and end apart: 5 -> 8, of which waited for: 4 -> 8; matrix products, arithmetic and copies ran while one was open for 22% -> 24% of each run, Pallas kernels for 0% -> 0%
where the time goes in v7:
time: 366 us; the launch traced here: 360 us
  waiting for transfers between devices  207 us (57%)
  starting transfers between devices  48.3 us (13%)
  local copies, waits for them, and re-layouts  41.5 us (11%)
  matrix products  33.5 us (9%)
  other arithmetic  29.2 us (8%)
    all_to_all x2, waiting for transfers between devices, per_device(): lax.all_to_all(partial_value, 'seq', split_axis=0, concat_axis=0, tiled=T...  78.5 us
    all_to_all x2, waiting for transfers between devices, per_device(): lax.all_to_all(copies, 'seq', split_axis=0, concat_axis=0, tiled=True)  60.3 us
    all_to_all x1, waiting for transfers between devices, per_device(): lax.all_to_all(outgoing, 'exp', split_axis=1, concat_axis=1, tiled=True)  29.7 us
    all_to_all x1, waiting for transfers between devices, per_device(): lax.all_to_all(summed, 'exp', split_axis=1, concat_axis=1, tiled=True)  19.7 us
    dot_general x4, matrix products, expert_pieces(): jnp.einsum('rf,fcd->crd', hidden, down, preferred_element_type=jnp.float32)  19.4 us
    all_to_all x1, waiting for transfers between devices, relayout(): lax.all_to_all(outgoing, 'seq', split_axis=1, concat_axis=1, tiled=True)  15.5 us
    all_to_all x2, starting transfers between devices, per_device(): lax.all_to_all(copies, 'seq', split_axis=0, concat_axis=0, tiled=True)  11.5 us
    dot_general x4, matrix products, expert_pieces(): gate = jnp.dot(rows, w_gate[e], preferred_element_type=jnp.float32)  10.7 us
  transfers between devices with their start and end apart: 8, of which 8 were waited for; matrix products, arithmetic and copies ran while one was open for 24% of the time, Pallas kernels for 0%

profile of v7, /device:TPU:120, one launch (start us, length us, event | category | flops | bytes accessed | tf_op | source)
XLA Modules:
  0.0 360.3 jit_solution(7217255248771762336)
XLA Ops:
  0.6 0.9 fusion.60
  1.7 0.8 select_reduce_fusion.1
  2.5 0.7 multiply_add_fusion
  3.2 0.2 fusion.3
  3.5 1.7 fusion
  5.1 2.0 convolution_convert_fusion
  7.1 1.8 copy.100
  8.9 8.7 %all-to-all-start = ((bf16[8,32,2560]{2,0,1:T(8,128)(2,1)}), bf16[8,32,2560]{2,0,1:T(8,128)(2,1)S(1)}, u32[]{:S(2)}, u32[]{:S(2)}) async-start(bf16[8,32,2560]{2,0,1:T(8,128)(2,1)} %copy.100), calls=%async_computation | async-start | bytes 2621440 | tf_op jit(solution)/shard_map/all_to_all | solution.py:83
  17.7 1.0 sort.31
  18.7 0.6 gather_fusion.2
  19.3 0.7 copy.116
  20.0 29.7 %all-to-all-done = bf16[8,32,2560]{2,0,1:T(8,128)(2,1)S(1)} async-done(((bf16[8,32,2560]{2,0,1:T(8,128)(2,1)}), bf16[8,32,2560]{2,0,1:T(8,128)(2,1)S(1)}, u32[]{:S(2)}, u32[]{:S(2)}) %all-to-all-start) | async-done | bytes 1310752 | tf_op jit(solution)/shard_map/all_to_all | solution.py:83
  49.7 6.9 %all-to-all-start.7 = ((s32[8,1,1]{2,1,0:T(1,128)}), s32[8,1,1]{2,1,0:T(1,128)S(1)}, u32[]{:S(2)}, u32[]{:S(2)}) async-start(s32[8,1,1]{2,1,0:T(1,128)} %copy.116), calls=%async_computation.7 | async-start | bytes 8192 | tf_op jit(solution)/shard_map/all_to_all | solution.py:35
  56.5 1.3 fusion.95
  57.8 0.9 copy.107
  58.7 3.4 all-to-all-done.7
  62.1 3.3 broadcast_in_dim.39
  65.4 6.5 %all-to-all-start.3 = ((bf16[8,3,32,2560]{3,2,1,0:T(8,128)(2,1)}), bf16[8,3,32,2560]{3,2,1,0:T(8,128)(2,1)}, u32[]{:S(2)}, u32[]{:S(2)}) async-start(bf16[8,3,32,2560]{3,2,1,0:T(8,128)(2,1)} %broadcast_in_dim.39), calls=%async_computation.3 | async-start | bytes 7864320 | tf_op jit(solution)/shard_map/all_to_all | solution.py:100
  71.9 2.0 copy.101
  73.9 42.3 %all-to-all-done.3 = bf16[8,3,32,2560]{3,2,1,0:T(8,128)(2,1)} async-done(((bf16[8,3,32,2560]{3,2,1,0:T(8,128)(2,1)}), bf16[8,3,32,2560]{3,2,1,0:T(8,128)(2,1)}, u32[]{:S(2)}, u32[]{:S(2)}) %all-to-all-start.3) | async-done | bytes 3932192 | tf_op jit(solution)/shard_map/all_to_all | solution.py:100
  116.2 3.4 broadcast_in_dim.38
  119.6 5.0 %all-to-all-start.1 = ((bf16[8,3,32,2560]{3,2,1,0:T(8,128)(2,1)}), bf16[8,3,32,2560]{3,2,1,0:T(8,128)(2,1)}, u32[]{:S(2)}, u32[]{:S(2)}) async-start(bf16[8,3,32,2560]{3,2,1,0:T(8,128)(2,1)} %broadcast_in_dim.38), calls=%async_computation.1 | async-start | bytes 7864320 | tf_op jit(solution)/shard_map/all_to_all | solution.py:100
  124.6 3.0 fusion.94
  127.6 2.8 reshape_squeeze.9
  130.4 1.3 fusion.96
  131.7 0.7 copy-done.4
  132.5 1.6 fusion.24
  134.0 2.6 fusion.15
  136.7 0.4 copy.112
  137.1 3.8 %fusion.26 = f32[768,192]{0,1:T(8,128)S(1)} fusion(bf16[768,2560]{1,0:T(8,128)(2,1)} %bitcast.10, bf16[2,2560,192]{1,2,0:T(8,128)(2,1)} %param.14), kind=kOutput, calls=%fused_computation.45 | convolution fusion | flops 754974720 | bytes 5505024 | tf_op jit(solution)/shard_map/dot_general | solution.py:88
  140.9 7.1 %convert_bitcast_fusion = bf16[8,768,320]{1,2,0:T(8,128)(2,1)} fusion(bf16[768,2560]{1,0:T(8,128)(2,1)} %bitcast.10, bf16[192,8,320]{2,1,0:T(8,128)(2,1)} %reshape_squeeze.9, bf16[2,2560,192]{1,2,0:T(8,128)(2,1)} %param.15, f32[768,192]{0,1:T(8,128)S(1)} %fusion.26), kind=kOutput, calls=%fused_computation.8 | convolution fusion | flops 1512800256 | bytes 10616832 | tf_op jit(solution)/shard_map/rf,fcd->crd/dot_general | solution.py:92
  148.0 4.7 %pad_maximum_fusion.1 = bf16[8,800,320]{1,2,0:T(8,128)(2,1)} fusion(bf16[8,32,320]{1,2,0:T(8,128)(2,1)S(1)} %copy.112, bf16[8,768,320]{1,2,0:T(8,128)(2,1)} %convert_bitcast_fusion), kind=kLoop, calls=%fused_computation.7 | loop fusion | flops 8192000 | bytes 8192000 | tf_op jit(solution)/shard_map/concatenate | solution.py:104
  152.8 18.0 %all-to-all-done.1 = bf16[8,3,32,2560]{3,2,1,0:T(8,128)(2,1)} async-done(((bf16[8,3,32,2560]{3,2,1,0:T(8,128)(2,1)}), bf16[8,3,32,2560]{3,2,1,0:T(8,128)(2,1)}, u32[]{:S(2)}, u32[]{:S(2)}) %all-to-all-start.1) | async-done | bytes 3932192 | tf_op jit(solution)/shard_map/all_to_all | solution.py:100
  170.7 5.0 %all-to-all-start.4 = ((bf16[8,800,320]{1,2,0:T(8,128)(2,1)}), bf16[8,800,320]{1,2,0:T(8,128)(2,1)}, u32[]{:S(2)}, u32[]{:S(2)}) async-start(bf16[8,800,320]{1,2,0:T(8,128)(2,1)} %pad_maximum_fusion.1), calls=%async_computation.4 | async-start | bytes 9175040 | tf_op jit(solution)/shard_map/all_to_all | solution.py:107
  175.8 1.7 reshape_squeeze.8
  177.5 1.6 fusion.31
  179.1 2.5 fusion.18
  181.7 0.4 copy.106
  182.0 3.8 %fusion.33 = f32[768,192]{0,1:T(8,128)S(1)} fusion(bf16[768,2560]{1,0:T(8,128)(2,1)} %bitcast.1, bf16[2,2560,192]{1,2,0:T(8,128)(2,1)} %param.14), kind=kOutput, calls=%fused_computation.51 | convolution fusion | flops 754974720 | bytes 5505024 | tf_op jit(solution)/shard_map/dot_general | solution.py:88
  185.8 7.1 %convert_bitcast_fusion.1 = bf16[8,768,320]{1,2,0:T(8,128)(2,1)} fusion(bf16[768,2560]{1,0:T(8,128)(2,1)} %bitcast.1, bf16[192,8,320]{2,1,0:T(8,128)(2,1)} %reshape_squeeze.8, bf16[2,2560,192]{1,2,0:T(8,128)(2,1)} %param.15, f32[768,192]{0,1:T(8,128)S(1)} %fusion.33), kind=kOutput, calls=%fused_computation.9 | convolution fusion | flops 1512800256 | bytes 10616832 | tf_op jit(solution)/shard_map/rf,fcd->crd/dot_general | solution.py:92
  193.0 4.8 %pad_maximum_fusion = bf16[8,800,320]{1,2,0:T(8,128)(2,1)} fusion(bf16[8,32,320]{1,2,0:T(8,128)(2,1)S(1)} %copy.106, bf16[8,768,320]{1,2,0:T(8,128)(2,1)} %convert_bitcast_fusion.1), kind=kLoop, calls=%fused_computation.6 | loop fusion | flops 8192000 | bytes 8192000 | tf_op jit(solution)/shard_map/concatenate | solution.py:104
  197.7 31.1 %all-to-all-done.4 = bf16[8,800,320]{1,2,0:T(8,128)(2,1)} async-done(((bf16[8,800,320]{1,2,0:T(8,128)(2,1)}), bf16[8,800,320]{1,2,0:T(8,128)(2,1)}, u32[]{:S(2)}, u32[]{:S(2)}) %all-to-all-start.4) | async-done | bytes 4096032 | tf_op jit(solution)/shard_map/all_to_all | solution.py:107
  228.9 5.0 %all-to-all-start.2 = ((bf16[8,800,320]{1,2,0:T(8,128)(2,1)}), bf16[8,800,320]{1,2,0:T(8,128)(2,1)}, u32[]{:S(2)}, u32[]{:S(2)}) async-start(bf16[8,800,320]{1,2,0:T(8,128)(2,1)} %pad_maximum_fusion), calls=%async_computation.2 | async-start | bytes 9175040 | tf_op jit(solution)/shard_map/all_to_all | solution.py:107
  233.9 2.0 gather_fusion
  235.9 0.6 gather_fusion.1
  236.5 3.1 multiply_bitcast_fusion
  239.7 47.3 %all-to-all-done.2 = bf16[8,800,320]{1,2,0:T(8,128)(2,1)} async-done(((bf16[8,800,320]{1,2,0:T(8,128)(2,1)}), bf16[8,800,320]{1,2,0:T(8,128)(2,1)}, u32[]{:S(2)}, u32[]{:S(2)}) %all-to-all-start.2) | async-done | bytes 4096032 | tf_op jit(solution)/shard_map/all_to_all | solution.py:107
  287.0 5.0 %all-to-all-start.6 = ((bf16[4,8,32,1024]{3,2,0,1:T(8,128)(2,1)}), bf16[4,8,32,1024]{3,2,0,1:T(8,128)(2,1)}, u32[]{:S(2)}, u32[]{:S(2)}) async-start(bf16[4,8,32,1024]{3,2,0,1:T(8,128)(2,1)} %multiply_bitcast_fusion), calls=%async_computation.6 | async-start | bytes 4194304 | tf_op jit(solution)/shard_map/all_to_all | solution.py:34
  292.0 3.3 reduce_sum.55
  295.3 3.3 reduce_sum.54
  298.6 1.2 pad_maximum_fusion.2
  299.7 1.7 copy.113
  301.5 1.5 copy.114
  303.0 15.5 %all-to-all-done.6 = bf16[4,8,32,1024]{3,2,0,1:T(8,128)(2,1)} async-done(((bf16[4,8,32,1024]{3,2,0,1:T(8,128)(2,1)}), bf16[4,8,32,1024]{3,2,0,1:T(8,128)(2,1)}, u32[]{:S(2)}, u32[]{:S(2)}) %all-to-all-start.6) | async-done | bytes 2097184 | tf_op jit(solution)/shard_map/all_to_all | solution.py:34
  318.5 6.1 %all-to-all-start.5 = ((bf16[50,32,320]{2,0,1:T(8,128)(2,1)}), bf16[50,32,320]{2,0,1:T(8,128)(2,1)S(1)}, u32[]{:S(2)}, u32[]{:S(2)}) async-start(bf16[50,32,320]{2,0,1:T(8,128)(2,1)} %copy.114), calls=%async_computation.5 | async-start | bytes 2752512 | tf_op jit(solution)/shard_map/all_to_all | solution.py:110
  324.6 2.4 select_reduce_fusion
  327.0 0.2 reduce.2
  327.3 1.0 sort.32
  328.2 3.2 copy.117
  331.4 3.6 %gather_fusion.3 = bf16[8,4,32,1024]{3,2,1,0:T(8,128)(2,1)} fusion(bf16[4,8,32,1024]{3,2,1,0:T(8,128)(2,1)} %copy.117, s32[1024]{0:T(1024)S(1)} %pad_clamp_fusion), kind=kCustom, calls=%fused_computation.3 | custom fusion | bytes 4194336 | tf_op jit(solution)/shard_map/gather | solution.py:36
  335.0 3.2 copy.118
  338.2 19.7 %all-to-all-done.5 = bf16[50,32,320]{2,0,1:T(8,128)(2,1)S(1)} async-done(((bf16[50,32,320]{2,0,1:T(8,128)(2,1)}), bf16[50,32,320]{2,0,1:T(8,128)(2,1)S(1)}, u32[]{:S(2)}, u32[]{:S(2)}) %all-to-all-start.5) | async-done | bytes 1024032 | tf_op jit(solution)/shard_map/all_to_all | solution.py:110
  358.1 1.0 copy-done.2
  359.1 1.3 convolution_convert_fusion.1
  (28 shorter events, 0.6 us)
Async XLA Ops:
  0.6 233.3 %copy-start = (bf16[4,8,32,1024]{3,2,1,0:T(8,128)(2,1)S(1)}, bf16[4,8,32,1024]{3,2,1,0:T(8,128)(2,1)}, u32[]{:S(2)}) copy-start(bf16[4,8,32,1024]{3,2,1,0:T(8,128)(2,1)} %param.17) | copy-start | bytes 6291460
  7.1 10.5 %copy-start.6 = (s32[8]{0:T(128)S(1)}, s32[8]{0:T(128)}, u32[]{:S(2)}) copy-start(s32[8]{0:T(128)} %param.18) | copy-start | bytes 100
  8.9 40.8 %all-to-all-start = ((bf16[8,32,2560]{2,0,1:T(8,128)(2,1)}), bf16[8,32,2560]{2,0,1:T(8,128)(2,1)S(1)}, u32[]{:S(2)}, u32[]{:S(2)}) async-start(bf16[8,32,2560]{2,0,1:T(8,128)(2,1)} %copy.100), calls=%async_computation | async-start | bytes 2621440 | tf_op jit(solution)/shard_map/all_to_all | solution.py:83
  49.7 12.4 %all-to-all-start.7 = ((s32[8,1,1]{2,1,0:T(1,128)}), s32[8,1,1]{2,1,0:T(1,128)S(1)}, u32[]{:S(2)}, u32[]{:S(2)}) async-start(s32[8,1,1]{2,1,0:T(1,128)} %copy.116), calls=%async_computation.7 | async-start | bytes 8192 | tf_op jit(solution)/shard_map/all_to_all | solution.py:35
  65.4 50.8 %all-to-all-start.3 = ((bf16[8,3,32,2560]{3,2,1,0:T(8,128)(2,1)}), bf16[8,3,32,2560]{3,2,1,0:T(8,128)(2,1)}, u32[]{:S(2)}, u32[]{:S(2)}) async-start(bf16[8,3,32,2560]{3,2,1,0:T(8,128)(2,1)} %broadcast_in_dim.39), calls=%async_computation.3 | async-start | bytes 7864320 | tf_op jit(solution)/shard_map/all_to_all | solution.py:100
  119.6 51.1 %all-to-all-start.1 = ((bf16[8,3,32,2560]{3,2,1,0:T(8,128)(2,1)}), bf16[8,3,32,2560]{3,2,1,0:T(8,128)(2,1)}, u32[]{:S(2)}, u32[]{:S(2)}) async-start(bf16[8,3,32,2560]{3,2,1,0:T(8,128)(2,1)} %broadcast_in_dim.38), calls=%async_computation.1 | async-start | bytes 7864320 | tf_op jit(solution)/shard_map/all_to_all | solution.py:100
  131.7 0.7 copy-start.4
  152.8 23.0 %copy-start.1 = (bf16[1,192,2560]{2,1,0:T(8,128)(2,1)S(1)}, bf16[1,192,2560]{2,1,0:T(8,128)(2,1)}, u32[]{:S(2)}) copy-start(bf16[1,192,2560]{2,1,0:T(8,128)(2,1)} %get-tuple-element.18) | copy-start | bytes 2949124
  170.7 58.1 %all-to-all-start.4 = ((bf16[8,800,320]{1,2,0:T(8,128)(2,1)}), bf16[8,800,320]{1,2,0:T(8,128)(2,1)}, u32[]{:S(2)}, u32[]{:S(2)}) async-start(bf16[8,800,320]{1,2,0:T(8,128)(2,1)} %pad_maximum_fusion.1), calls=%async_computation.4 | async-start | bytes 9175040 | tf_op jit(solution)/shard_map/all_to_all | solution.py:107
  175.7 1.7 copy-start.3
  228.9 58.1 %all-to-all-start.2 = ((bf16[8,800,320]{1,2,0:T(8,128)(2,1)}), bf16[8,800,320]{1,2,0:T(8,128)(2,1)}, u32[]{:S(2)}, u32[]{:S(2)}) async-start(bf16[8,800,320]{1,2,0:T(8,128)(2,1)} %pad_maximum_fusion), calls=%async_computation.2 | async-start | bytes 9175040 | tf_op jit(solution)/shard_map/all_to_all | solution.py:107
  233.9 2.0 copy-start.7
  287.0 31.5 %all-to-all-start.6 = ((bf16[4,8,32,1024]{3,2,0,1:T(8,128)(2,1)}), bf16[4,8,32,1024]{3,2,0,1:T(8,128)(2,1)}, u32[]{:S(2)}, u32[]{:S(2)}) async-start(bf16[4,8,32,1024]{3,2,0,1:T(8,128)(2,1)} %multiply_bitcast_fusion), calls=%async_computation.6 | async-start | bytes 4194304 | tf_op jit(solution)/shard_map/all_to_all | solution.py:34
  301.5 23.1 %copy-start.5 = (bf16[256,6]{0,1:T(8,128)(2,1)S(1)}, bf16[256,6]{0,1:T(8,128)(2,1)}, u32[]{:S(2)}) copy-start(bf16[256,6]{0,1:T(8,128)(2,1)} %param.13) | copy-start | bytes 9220
  318.5 39.5 %all-to-all-start.5 = ((bf16[50,32,320]{2,0,1:T(8,128)(2,1)}), bf16[50,32,320]{2,0,1:T(8,128)(2,1)S(1)}, u32[]{:S(2)}, u32[]{:S(2)}) async-start(bf16[50,32,320]{2,0,1:T(8,128)(2,1)} %copy.114), calls=%async_computation.5 | async-start | bytes 2752512 | tf_op jit(solution)/shard_map/all_to_all | solution.py:110
  357.9 1.1 copy-start.2

commit v8 on v7

--- a/solution.py
+++ b/solution.py
@@ -29,11 +29,15 @@
     peer = block_map // blocks // exp_count
     target = block_map % blocks
     order = jnp.argsort(peer)
-    outgoing = kv_prefill[:, order] * keep[order][None, :, None, None]
-    labels = target[order]
+    kept = kv_prefill[:, order] * keep[order][None, :, None, None]
+    tags = jnp.broadcast_to(
+        target[order].astype(kv_prefill.dtype)[None, :, None, None], (layers, blocks, block_rows, 128)
+    )
+    outgoing = jnp.concatenate([kept, tags], axis=3)
     arrived = lax.all_to_all(outgoing, "seq", split_axis=1, concat_axis=1, tiled=True)
-    slots = lax.all_to_all(labels, "seq", split_axis=0, concat_axis=0, tiled=True)
-    return arrived[:, jnp.argsort(slots)]
+    slots = arrived[0, :, 0, kv_width].astype(jnp.int32)
+    data = lax.slice_in_dim(arrived, 0, kv_width, axis=3)
+    return jnp.take(data, jnp.argsort(slots), axis=1)
 
 
 def per_device(

time: 366 us -> 357 us (0.975)
  blocking collectives: 0 us -> 41.1 us
  waiting for transfers between devices: 207 us -> 175 us
  starting transfers between devices: 48.3 us -> 32.4 us
  local copies, waits for them, and re-layouts: 41.5 us -> 36.5 us
    all_to_all x0 -> x1, blocking collectives: none -> 41.1 us  [per_device(): lax.all_to_all(outgoing, 'exp', split_axis=1, concat_axis=1, tiled=True)]
    all_to_all x2 -> x0, waiting for transfers between devices: 33.1 us -> none  [the longest x1 29.7 us: per_device(): lax.all_to_all(outgoing, 'exp', split_axis=1, concat_axis=1, tiled=True)]
    all_to_all x2 -> x0, starting transfers between devices: 15.6 us -> none  [the longest x1 8.74 us: per_device(): lax.all_to_all(outgoing, 'exp', split_axis=1, concat_axis=1, tiled=True)]
    all_to_all x2 -> x0, local copies, waits for them, and re-layouts: 3.87 us -> none  [the longest x1 3.18 us: relayout(): lax.all_to_all(outgoing, 'seq', split_axis=1, concat_axis=1, tiled=True)]
  transfers between devices with their start and end apart: 8 -> 6, of which waited for: 8 -> 6; matrix products, arithmetic and copies ran while one was open for 24% -> 24% of each run, Pallas kernels for 0% -> 0%
where the time goes in v8:
time: 357 us; the launch traced here: 352 us
  waiting for transfers between devices  175 us (49%)
  blocking collectives  41.1 us (12%)
  local copies, waits for them, and re-layouts  36.5 us (10%)
  matrix products  33.5 us (9%)
  starting transfers between devices  32.4 us (9%)
  other arithmetic  32.2 us (9%)
    all_to_all x2, waiting for transfers between devices, per_device(): lax.all_to_all(partial_value, 'seq', split_axis=0, concat_axis=0, tiled=T...  76.2 us
    all_to_all x2, waiting for transfers between devices, per_device(): lax.all_to_all(copies, 'seq', split_axis=0, concat_axis=0, tiled=True)  61.9 us
    all_to_all x1, blocking collectives, per_device(): lax.all_to_all(outgoing, 'exp', split_axis=1, concat_axis=1, tiled=True)  41.1 us
    dot_general x4, matrix products, expert_pieces(): jnp.einsum('rf,fcd->crd', hidden, down, preferred_element_type=jnp.float32)  19.4 us
    all_to_all x1, waiting for transfers between devices, per_device(): lax.all_to_all(summed, 'exp', split_axis=1, concat_axis=1, tiled=True)  18.8 us
    all_to_all x1, waiting for transfers between devices, relayout(): lax.all_to_all(outgoing, 'seq', split_axis=1, concat_axis=1, tiled=True)  18.3 us
    all_to_all x2, starting transfers between devices, per_device(): lax.all_to_all(copies, 'seq', split_axis=0, concat_axis=0, tiled=True)  11.9 us
    dot_general x4, matrix products, expert_pieces(): gate = jnp.dot(rows, w_gate[e], preferred_element_type=jnp.float32)  10.7 us
  transfers between devices with their start and end apart: 6, of which 6 were waited for; matrix products, arithmetic and copies ran while one was open for 24% of the time, Pallas kernels for 0%

profile of v8, /device:TPU:120, one launch (start us, length us, event | category | flops | bytes accessed | tf_op | source)
XLA Modules:
  0.0 351.8 jit_solution(16390480800711758644)
XLA Ops:
  0.6 0.9 fusion.60
  1.5 0.2 fusion.63
  1.7 0.8 select_reduce_fusion.1
  2.5 0.7 multiply_add_fusion
  3.2 0.2 fusion.3
  3.5 1.7 fusion
  5.1 2.0 convolution_convert_fusion
  7.1 0.7 copy.97
  7.8 41.1 %all_to_all.35 = bf16[8,32,2560]{2,0,1:T(8,128)(2,1)S(1)} all-to-all(bf16[8,32,2560]{2,0,1:T(8,128)(2,1)S(1)} %copy.97), channel_id=1, replica_groups=mesh['seq'=8,'exp'=32] {'exp'}, dimensions={1} | all-to-all | bytes 2621440 | tf_op jit(solution)/shard_map/all_to_all | solution.py:87
  49.0 1.3 fusion.96
  50.3 2.3 broadcast_in_dim.48
  52.6 6.9 %all-to-all-start.3 = ((bf16[8,3,32,2560]{3,2,1,0:T(8,128)(2,1)}), bf16[8,3,32,2560]{3,2,1,0:T(8,128)(2,1)}, u32[]{:S(2)}, u32[]{:S(2)}) async-start(bf16[8,3,32,2560]{3,2,1,0:T(8,128)(2,1)} %broadcast_in_dim.48), calls=%async_computation.3 | async-start | bytes 7864320 | tf_op jit(solution)/shard_map/all_to_all | solution.py:104
  59.5 2.0 copy.98
  61.5 43.9 %all-to-all-done.3 = bf16[8,3,32,2560]{3,2,1,0:T(8,128)(2,1)} async-done(((bf16[8,3,32,2560]{3,2,1,0:T(8,128)(2,1)}), bf16[8,3,32,2560]{3,2,1,0:T(8,128)(2,1)}, u32[]{:S(2)}, u32[]{:S(2)}) %all-to-all-start.3) | async-done | bytes 3932192 | tf_op jit(solution)/shard_map/all_to_all | solution.py:104
  105.4 3.4 broadcast_in_dim.47
  108.8 5.0 %all-to-all-start.1 = ((bf16[8,3,32,2560]{3,2,1,0:T(8,128)(2,1)}), bf16[8,3,32,2560]{3,2,1,0:T(8,128)(2,1)}, u32[]{:S(2)}, u32[]{:S(2)}) async-start(bf16[8,3,32,2560]{3,2,1,0:T(8,128)(2,1)} %broadcast_in_dim.47), calls=%async_computation.1 | async-start | bytes 7864320 | tf_op jit(solution)/shard_map/all_to_all | solution.py:104
  113.9 3.0 fusion.95
  116.9 2.8 reshape_squeeze.9
  119.7 1.3 fusion.97
  121.0 0.7 copy-done.4
  121.7 1.6 fusion.24
  123.3 2.6 fusion.15
  126.0 0.4 copy.109
  126.4 3.8 %fusion.26 = f32[768,192]{0,1:T(8,128)S(1)} fusion(bf16[768,2560]{1,0:T(8,128)(2,1)} %bitcast.10, bf16[2,2560,192]{1,2,0:T(8,128)(2,1)} %param.14), kind=kOutput, calls=%fused_computation.47 | convolution fusion | flops 754974720 | bytes 5505024 | tf_op jit(solution)/shard_map/dot_general | solution.py:92
  130.2 7.1 %convert_bitcast_fusion = bf16[8,768,320]{1,2,0:T(8,128)(2,1)} fusion(bf16[768,2560]{1,0:T(8,128)(2,1)} %bitcast.10, bf16[192,8,320]{2,1,0:T(8,128)(2,1)} %reshape_squeeze.9, bf16[2,2560,192]{1,2,0:T(8,128)(2,1)} %param.15, f32[768,192]{0,1:T(8,128)S(1)} %fusion.26), kind=kOutput, calls=%fused_computation.8 | convolution fusion | flops 1512800256 | bytes 10616832 | tf_op jit(solution)/shard_map/rf,fcd->crd/dot_general | solution.py:96
  137.3 4.7 %pad_maximum_fusion.1 = bf16[8,800,320]{1,2,0:T(8,128)(2,1)} fusion(bf16[8,32,320]{1,2,0:T(8,128)(2,1)S(1)} %copy.109, bf16[8,768,320]{1,2,0:T(8,128)(2,1)} %convert_bitcast_fusion), kind=kLoop, calls=%fused_computation.7 | loop fusion | flops 8192000 | bytes 8192000 | tf_op jit(solution)/shard_map/concatenate | solution.py:108
  142.0 18.0 %all-to-all-done.1 = bf16[8,3,32,2560]{3,2,1,0:T(8,128)(2,1)} async-done(((bf16[8,3,32,2560]{3,2,1,0:T(8,128)(2,1)}), bf16[8,3,32,2560]{3,2,1,0:T(8,128)(2,1)}, u32[]{:S(2)}, u32[]{:S(2)}) %all-to-all-start.1) | async-done | bytes 3932192 | tf_op jit(solution)/shard_map/all_to_all | solution.py:104
  160.0 5.0 %all-to-all-start.4 = ((bf16[8,800,320]{1,2,0:T(8,128)(2,1)}), bf16[8,800,320]{1,2,0:T(8,128)(2,1)}, u32[]{:S(2)}, u32[]{:S(2)}) async-start(bf16[8,800,320]{1,2,0:T(8,128)(2,1)} %pad_maximum_fusion.1), calls=%async_computation.4 | async-start | bytes 9175040 | tf_op jit(solution)/shard_map/all_to_all | solution.py:111
  165.0 1.7 reshape_squeeze.8
  166.7 1.6 fusion.31
  168.3 2.5 fusion.18
  170.9 0.4 copy.103
  171.3 3.8 %fusion.33 = f32[768,192]{0,1:T(8,128)S(1)} fusion(bf16[768,2560]{1,0:T(8,128)(2,1)} %bitcast.1, bf16[2,2560,192]{1,2,0:T(8,128)(2,1)} %param.14), kind=kOutput, calls=%fused_computation.53 | convolution fusion | flops 754974720 | bytes 5505024 | tf_op jit(solution)/shard_map/dot_general | solution.py:92
  175.1 7.1 %convert_bitcast_fusion.1 = bf16[8,768,320]{1,2,0:T(8,128)(2,1)} fusion(bf16[768,2560]{1,0:T(8,128)(2,1)} %bitcast.1, bf16[192,8,320]{2,1,0:T(8,128)(2,1)} %reshape_squeeze.8, bf16[2,2560,192]{1,2,0:T(8,128)(2,1)} %param.15, f32[768,192]{0,1:T(8,128)S(1)} %fusion.33), kind=kOutput, calls=%fused_computation.9 | convolution fusion | flops 1512800256 | bytes 10616832 | tf_op jit(solution)/shard_map/rf,fcd->crd/dot_general | solution.py:96
  182.2 4.8 %pad_maximum_fusion = bf16[8,800,320]{1,2,0:T(8,128)(2,1)} fusion(bf16[8,32,320]{1,2,0:T(8,128)(2,1)S(1)} %copy.103, bf16[8,768,320]{1,2,0:T(8,128)(2,1)} %convert_bitcast_fusion.1), kind=kLoop, calls=%fused_computation.6 | loop fusion | flops 8192000 | bytes 8192000 | tf_op jit(solution)/shard_map/concatenate | solution.py:108
  187.0 31.1 %all-to-all-done.4 = bf16[8,800,320]{1,2,0:T(8,128)(2,1)} async-done(((bf16[8,800,320]{1,2,0:T(8,128)(2,1)}), bf16[8,800,320]{1,2,0:T(8,128)(2,1)}, u32[]{:S(2)}, u32[]{:S(2)}) %all-to-all-start.4) | async-done | bytes 4096032 | tf_op jit(solution)/shard_map/all_to_all | solution.py:111
  218.1 5.0 %all-to-all-start.2 = ((bf16[8,800,320]{1,2,0:T(8,128)(2,1)}), bf16[8,800,320]{1,2,0:T(8,128)(2,1)}, u32[]{:S(2)}, u32[]{:S(2)}) async-start(bf16[8,800,320]{1,2,0:T(8,128)(2,1)} %pad_maximum_fusion), calls=%async_computation.2 | async-start | bytes 9175040 | tf_op jit(solution)/shard_map/all_to_all | solution.py:111
  223.2 1.0 sort.31
  224.1 0.6 gather_fusion.2
  224.8 2.0 gather_fusion
  226.8 0.6 gather_fusion.1
  227.5 1.8 multiply_bitcast_fusion
  229.4 1.8 pad_maximum_fusion.2
  231.2 45.1 %all-to-all-done.2 = bf16[8,800,320]{1,2,0:T(8,128)(2,1)} async-done(((bf16[8,800,320]{1,2,0:T(8,128)(2,1)}), bf16[8,800,320]{1,2,0:T(8,128)(2,1)}, u32[]{:S(2)}, u32[]{:S(2)}) %all-to-all-start.2) | async-done | bytes 4096032 | tf_op jit(solution)/shard_map/all_to_all | solution.py:111
  276.3 5.0 %all-to-all-start.6 = ((bf16[4,8,32,1152]{3,2,0,1:T(8,128)(2,1)}), bf16[4,8,32,1152]{3,2,0,1:T(8,128)(2,1)}, u32[]{:S(2)}, u32[]{:S(2)}) async-start(bf16[4,8,32,1152]{3,2,0,1:T(8,128)(2,1)} %pad_maximum_fusion.2), calls=%async_computation.6 | async-start | bytes 4718592 | tf_op jit(solution)/shard_map/all_to_all | solution.py:37
  281.3 3.3 reduce_sum.55
  284.6 3.3 reduce_sum.54
  287.8 1.1 pad_maximum_fusion.3
  289.0 1.7 copy.110
  290.7 1.5 copy.111
  292.2 18.3 %all-to-all-done.6 = bf16[4,8,32,1152]{3,2,0,1:T(8,128)(2,1)} async-done(((bf16[4,8,32,1152]{3,2,0,1:T(8,128)(2,1)}), bf16[4,8,32,1152]{3,2,0,1:T(8,128)(2,1)}, u32[]{:S(2)}, u32[]{:S(2)}) %all-to-all-start.6) | async-done | bytes 2359328 | tf_op jit(solution)/shard_map/all_to_all | solution.py:37
  310.5 5.5 %all-to-all-start.5 = ((bf16[50,32,320]{2,0,1:T(8,128)(2,1)}), bf16[50,32,320]{2,0,1:T(8,128)(2,1)S(1)}, u32[]{:S(2)}, u32[]{:S(2)}) async-start(bf16[50,32,320]{2,0,1:T(8,128)(2,1)} %copy.111), calls=%async_computation.5 | async-start | bytes 2752512 | tf_op jit(solution)/shard_map/all_to_all | solution.py:114
  316.0 2.4 select_reduce_fusion
  318.4 1.8 slice.67
  320.2 1.5 copy.113
  321.7 1.0 fusion.90
  322.6 1.0 sort.32
  323.6 3.6 %gather_fusion.3 = bf16[8,4,32,1024]{3,2,1,0:T(8,128)(2,1)} fusion(bf16[4,8,32,1024]{3,2,1,0:T(8,128)(2,1)} %copy.113, s32[1024]{0:T(1024)S(1)} %pad_clamp_fusion), kind=kCustom, calls=%fused_computation.3 | custom fusion | bytes 4194336 | tf_op jit(solution)/shard_map/jit(_take)/gather | solution.py:40
  327.2 1.9 select_bitcast_fusion
  329.1 1.5 copy.114
  330.6 18.8 %all-to-all-done.5 = bf16[50,32,320]{2,0,1:T(8,128)(2,1)S(1)} async-done(((bf16[50,32,320]{2,0,1:T(8,128)(2,1)}), bf16[50,32,320]{2,0,1:T(8,128)(2,1)S(1)}, u32[]{:S(2)}, u32[]{:S(2)}) %all-to-all-start.5) | async-done | bytes 1024032 | tf_op jit(solution)/shard_map/all_to_all | solution.py:114
  349.4 0.2 copy.112
  349.6 1.0 copy-done.2
  350.6 1.3 convolution_convert_fusion.1
  (30 shorter events, 0.5 us)
Async XLA Ops:
  0.6 224.2 %copy-start = (bf16[4,8,32,1024]{3,2,1,0:T(8,128)(2,1)S(1)}, bf16[4,8,32,1024]{3,2,1,0:T(8,128)(2,1)}, u32[]{:S(2)}) copy-start(bf16[4,8,32,1024]{3,2,1,0:T(8,128)(2,1)} %param.17) | copy-start | bytes 6291460
  52.6 52.8 %all-to-all-start.3 = ((bf16[8,3,32,2560]{3,2,1,0:T(8,128)(2,1)}), bf16[8,3,32,2560]{3,2,1,0:T(8,128)(2,1)}, u32[]{:S(2)}, u32[]{:S(2)}) async-start(bf16[8,3,32,2560]{3,2,1,0:T(8,128)(2,1)} %broadcast_in_dim.48), calls=%async_computation.3 | async-start | bytes 7864320 | tf_op jit(solution)/shard_map/all_to_all | solution.py:104
  108.8 51.1 %all-to-all-start.1 = ((bf16[8,3,32,2560]{3,2,1,0:T(8,128)(2,1)}), bf16[8,3,32,2560]{3,2,1,0:T(8,128)(2,1)}, u32[]{:S(2)}, u32[]{:S(2)}) async-start(bf16[8,3,32,2560]{3,2,1,0:T(8,128)(2,1)} %broadcast_in_dim.47), calls=%async_computation.1 | async-start | bytes 7864320 | tf_op jit(solution)/shard_map/all_to_all | solution.py:104
  121.0 0.7 copy-start.4
  142.0 23.0 %copy-start.1 = (bf16[1,192,2560]{2,1,0:T(8,128)(2,1)S(1)}, bf16[1,192,2560]{2,1,0:T(8,128)(2,1)}, u32[]{:S(2)}) copy-start(bf16[1,192,2560]{2,1,0:T(8,128)(2,1)} %get-tuple-element.18) | copy-start | bytes 2949124
  160.0 58.1 %all-to-all-start.4 = ((bf16[8,800,320]{1,2,0:T(8,128)(2,1)}), bf16[8,800,320]{1,2,0:T(8,128)(2,1)}, u32[]{:S(2)}, u32[]{:S(2)}) async-start(bf16[8,800,320]{1,2,0:T(8,128)(2,1)} %pad_maximum_fusion.1), calls=%async_computation.4 | async-start | bytes 9175040 | tf_op jit(solution)/shard_map/all_to_all | solution.py:111
  165.0 1.7 copy-start.3
  187.0 36.2 %copy-start.6 = (s32[8]{0:T(128)S(1)}, s32[8]{0:T(128)}, u32[]{:S(2)}) copy-start(s32[8]{0:T(128)} %param.18) | copy-start | bytes 100
  218.1 58.1 %all-to-all-start.2 = ((bf16[8,800,320]{1,2,0:T(8,128)(2,1)}), bf16[8,800,320]{1,2,0:T(8,128)(2,1)}, u32[]{:S(2)}, u32[]{:S(2)}) async-start(bf16[8,800,320]{1,2,0:T(8,128)(2,1)} %pad_maximum_fusion), calls=%async_computation.2 | async-start | bytes 9175040 | tf_op jit(solution)/shard_map/all_to_all | solution.py:111
  224.8 2.0 copy-start.7
  276.3 34.3 %all-to-all-start.6 = ((bf16[4,8,32,1152]{3,2,0,1:T(8,128)(2,1)}), bf16[4,8,32,1152]{3,2,0,1:T(8,128)(2,1)}, u32[]{:S(2)}, u32[]{:S(2)}) async-start(bf16[4,8,32,1152]{3,2,0,1:T(8,128)(2,1)} %pad_maximum_fusion.2), calls=%async_computation.6 | async-start | bytes 4718592 | tf_op jit(solution)/shard_map/all_to_all | solution.py:37
  290.7 25.3 %copy-start.5 = (bf16[256,6]{0,1:T(8,128)(2,1)S(1)}, bf16[256,6]{0,1:T(8,128)(2,1)}, u32[]{:S(2)}) copy-start(bf16[256,6]{0,1:T(8,128)(2,1)} %param.13) | copy-start | bytes 9220
  310.5 38.9 %all-to-all-start.5 = ((bf16[50,32,320]{2,0,1:T(8,128)(2,1)}), bf16[50,32,320]{2,0,1:T(8,128)(2,1)S(1)}, u32[]{:S(2)}, u32[]{:S(2)}) async-start(bf16[50,32,320]{2,0,1:T(8,128)(2,1)} %copy.111), calls=%async_computation.5 | async-start | bytes 2752512 | tf_op jit(solution)/shard_map/all_to_all | solution.py:114
  349.4 1.1 copy-start.2
